TPU v7x, 256 devices: a whole 4x4x8 slice. The times are simulated.
256 devices in a mesh: level: 4 (over x), basin: 32 (over y, z), group: 2 (over core).
Axes of the slice: x: 4, y: 4, z: 8, core: 2. Of those that a mesh axis runs over, the one named last changes fastest.
Arguments:
- lateral: float32 [96, 131072], P('group', ('level', 'basin')), may hold values from 0.02 to 2
- cotangent: float32 [96, 131072], P('group', ('level', 'basin')), may hold values from -6 to 6
- attributes: float32 [16, 131072], P(None, ('level', 'basin')), may hold values from -6 to 6
- region: int32 [131072], P(('level', 'basin')), may hold values from 0 to 127
- feeders: int32 [2, 131072], P(None, ('level', 'basin')), may hold values from 0 to 1151
- feeder_count: int32 [131072], P(('level', 'basin')), may hold values from 0 to 2
- live_blocks: int32 [128], P(('level', 'basin')), may hold values from 1 to 8, as said below
- net_weight: float32 [128, 16, 2], replicated, may hold values from -1.5 to 1.5
Outputs:
- outflow: float32 [96, 131072], P('group', ('level', 'basin'))
- grad_net: float32 [128, 16, 2], P('basin')
Inputs may be any that keep to these rules, and one draw needn't show every extreme that they name: `feeders`: entries below 1024 name a reach slot of the same basin shard one level lower in the order; an entry e of 1024 or more names reach slot e - 1024 of the previous basin shard one level lower. Nothing feeds level 0, and the previous shard of basin shard 0 is empty. `live_blocks`: reach slots at or past 128 times this count are padding; some shard is full in every draw.
All inputs are finite; a program needn't handle non-finite values.
Results may differ from a plain program's by a relative error of at most 0.00029.
Values sent between devices are 32-bit elements; how exact they have to be, the bound alone decides.
No kernel may reach another device: no remote copies, remote signals or barrier semaphores. Data moves between devices by JAX's collectives and lax.ppermute only.
A program may use at most 64 MiB of HBM per device.

v0:
```python
import functools

import jax
import jax.numpy as jnp
from jax import lax
from jax.sharding import PartitionSpec as P
from jax.experimental import pallas as pl
from jax.experimental.pallas import tpu as pltpu

BLOCK = 128


def shifted(value, axis, steps):
    count = lax.axis_size(axis)
    leading, last = (max(0, -steps), min(count, count - steps))
    return lax.ppermute(value, axis, [(source, source + steps) for source in range(leading, last)])


def diagonal(value, steps):
    levels, basins = lax.axis_size("level"), lax.axis_size("basin")
    pairs = []
    for level in range(max(0, -steps), min(levels, levels - steps)):
        for basin in range(max(0, -steps), min(basins, basins - steps)):
            pairs.append((level * basins + basin, (level + steps) * basins + basin + steps))
    return lax.ppermute(value, ("level", "basin"), pairs)


def exchanged(value, axis, mask):
    count = lax.axis_size(axis)
    return lax.ppermute(value, axis, [(source, source ^ mask) for source in range(count)])


def scattered_sum(blocks, axis):
    count, mine = (lax.axis_size(axis), lax.axis_index(axis))
    width = count
    while width > 1:
        width //= 2
        lower, upper = blocks[:width], blocks[width:]
        high = (mine & width) > 0
        kept = jnp.where(high, upper, lower)
        sent = jnp.where(high, lower, upper)
        blocks = kept + exchanged(sent, axis, width)
    return blocks[0]


def butterfly_sum(value, axis):
    mask = 1
    while mask < lax.axis_size(axis):
        value = value + exchanged(value, axis, mask)
        mask *= 2
    return value


def whole_window(value):
    return lax.all_gather(value, "group", axis=0, tiled=True)


def carried_in(value, axis, join, neutral, backward):
    count, mine = (lax.axis_size(axis), lax.axis_index(axis))
    pieces = lax.all_gather(value, axis)
    if backward:
        pieces = pieces[::-1]
        mine = count - 1 - mine
    subtotal = jnp.full_like(value, 0) + jnp.asarray(neutral, value.dtype)

    def turn(position, subtotal):
        longer = join(subtotal, pieces[position])
        return jnp.where(position < mine, longer, subtotal)

    return lax.fori_loop(0, count - 1, turn, subtotal)


def recurrence_kernel(retain_ref, drive_ref, out_ref, *, reverse):
    steps = drive_ref.shape[0]
    keep = retain_ref[...]

    def advance(position, state):
        hour = steps - 1 - position if reverse else position
        state = keep * state + drive_ref[pl.ds(hour, 1), :]
        out_ref[pl.ds(hour, 1), :] = state
        return state

    lax.fori_loop(0, steps, advance, jnp.zeros_like(keep), unroll=8)


def recurrence(retain_row, drive, reverse=False):
    steps, width = drive.shape
    return pl.pallas_call(
        functools.partial(recurrence_kernel, reverse=reverse),
        out_shape=jax.ShapeDtypeStruct((steps, width), jnp.float32),
        in_specs=[pl.BlockSpec(memory_space=pltpu.VMEM), pl.BlockSpec(memory_space=pltpu.VMEM)],
        out_specs=pl.BlockSpec(memory_space=pltpu.VMEM),
        cost_estimate=pl.CostEstimate(
            flops=2 * steps * width, transcendentals=0, bytes_accessed=8 * steps * width + 4 * width
        ),
    )(retain_row, drive)


def split_three(value):
    pieces = []
    rest = value
    for _ in range(3):
        piece = lax.reduce_precision(rest, exponent_bits=8, mantissa_bits=7)
        pieces.append(piece)
        rest = rest - piece
    return jnp.concatenate(pieces, axis=0).astype(jnp.bfloat16)


def joined_three(product):
    rows = product.shape[0] // 3
    return (product[:rows] + product[rows : 2 * rows]) + product[2 * rows :]


def coefficients(raw_params):
    travel = 1.0 + 47.0 * jax.nn.sigmoid(raw_params[0])
    weighting = 0.05 + 0.4 * jax.nn.sigmoid(raw_params[1])
    storage = travel * (1.0 - weighting)
    divisor = storage + 0.5
    return (
        (0.5 - travel * weighting) / divisor,
        (0.5 + travel * weighting) / divisor,
        (storage - 0.5) / divisor,
        1.0 / divisor,
    )


def affine_join(earlier, latter):
    return (earlier[0] * latter[0], latter[0] * earlier[1] + latter[1])


def stack_affine(pair):
    return jnp.stack([pair[0], pair[1]], axis=0)


def split_affine(stacked):
    return (stacked[0], stacked[1])


def stacked_affine(earlier, latter):
    return stack_affine(affine_join(split_affine(earlier), split_affine(latter)))


def body(lateral, cotangent, attributes, region, feeders, feeder_count, live_blocks, net_weight):
    steps_dev, reach_dev = lateral.shape
    outlets = reach_dev // 8
    regions, attr_count, param_count = net_weight.shape
    levels = lax.axis_size("level")
    up_count = feeders.shape[0]
    mine = lax.axis_index("group")
    slot_ids = lax.broadcasted_iota(jnp.int32, (reach_dev,), 0)
    live_mask = (slot_ids < live_blocks[0] * BLOCK).astype(jnp.float32)
    member_table = (
        region[None, :] == lax.broadcasted_iota(jnp.int32, (regions, reach_dev), 0)
    ).astype(jnp.float32)
    per_region = jnp.dot(
        jnp.transpose(net_weight, (0, 2, 1)).reshape(regions * param_count, attr_count),
        attributes,
        precision=lax.Precision.HIGHEST,
        preferred_element_type=jnp.float32,
    )
    raw_params = jnp.einsum(
        "rpi,ri->pi",
        per_region.reshape(regions, param_count, reach_dev),
        member_table,
        precision=lax.Precision.HIGHEST,
    )
    coef_set, coef_pull = jax.vjp(coefficients, raw_params)
    gain_now, gain_prev, retain, gain_side = coef_set
    lateral_all = whole_window(lateral)
    cotangent_all = whole_window(cotangent)
    steps_all = lateral_all.shape[0]
    source_ids = lax.broadcasted_iota(jnp.int32, (reach_dev + outlets, reach_dev), 0)
    confluence = jnp.zeros((reach_dev + outlets, reach_dev), jnp.float32)
    for upslot in range(up_count):
        confluence = confluence + (
            (source_ids == feeders[upslot][None, :]) & (upslot < feeder_count)[None, :]
        ).astype(jnp.float32)
    confluence = confluence.astype(jnp.bfloat16)
    retain_row = retain[None, :]
    zero_flow = jnp.zeros((steps_all, reach_dev), jnp.float32)
    zero_row = jnp.zeros((1, reach_dev), jnp.float32)

    def own_half(value):
        return lax.dynamic_slice_in_dim(value, mine * steps_dev, steps_dev, axis=0)

    def route_level(inflow):
        inflow_before = jnp.concatenate([zero_row, inflow[:-1]], axis=0)
        drive = gain_now * inflow + gain_prev * inflow_before + gain_side * lateral_all
        flow = recurrence(retain_row, drive)
        return flow * live_mask

    inflow = zero_flow
    outflow = route_level(inflow)
    for level_step in range(levels - 1):
        upper_flow = whole_window(shifted(own_half(outflow), "level", 1))
        side_flow = diagonal(outflow[:, :outlets], 1)
        source = jnp.concatenate([upper_flow, side_flow], axis=1)
        inflow = joined_three(
            jnp.dot(split_three(source), confluence, preferred_element_type=jnp.float32)
        )
        outflow = route_level(inflow)
    adjoint_down = zero_flow
    adjoint = zero_flow
    for level_step in range(levels):
        adjoint_load = live_mask * (cotangent_all + adjoint_down)
        adjoint = recurrence(retain_row, adjoint_load, reverse=True)
        if level_step + 1 < levels:
            later_adj = jnp.concatenate([adjoint[1:], zero_row], axis=0)
            to_inflow = gain_now * adjoint + gain_prev * later_adj
            spread = joined_three(
                lax.dot_general(
                    split_three(to_inflow),
                    confluence,
                    (((1,), (1,)), ((), ())),
                    preferred_element_type=jnp.float32,
                )
            )
            returned = diagonal(spread[:, reach_dev:], -1)
            own_part = whole_window(shifted(own_half(spread[:, :reach_dev]), "level", -1))
            adjoint_down = own_part.at[:, :outlets].add(returned)
    flow_before = jnp.concatenate([zero_row, outflow[:-1]], axis=0)
    inflow_before = jnp.concatenate([zero_row, inflow[:-1]], axis=0)
    coef_grads = (
        jnp.sum(adjoint * inflow, axis=0),
        jnp.sum(adjoint * inflow_before, axis=0),
        jnp.sum(adjoint * flow_before, axis=0),
        jnp.sum(adjoint * lateral_all, axis=0),
    )
    raw_grad = coef_pull(coef_grads)[0]
    owned_rows = regions // lax.axis_size("basin")
    weighted = (member_table[:, None, :] * raw_grad[None, :, :]).reshape(
        regions * param_count, reach_dev
    )
    summed = jnp.dot(
        weighted, attributes.T, precision=lax.Precision.HIGHEST, preferred_element_type=jnp.float32
    )
    local_grad = jnp.transpose(summed.reshape(regions, param_count, attr_count), (0, 2, 1))
    basins = lax.axis_size("basin")
    owned_share = scattered_sum(
        local_grad.reshape(basins, owned_rows, attr_count, param_count), "basin"
    )
    grad_net = butterfly_sum(owned_share, "level")
    return (own_half(outflow), grad_net)


def solution(mesh):
    in_specs = (
        P("group", ("level", "basin")),
        P("group", ("level", "basin")),
        P(None, ("level", "basin")),
        P(("level", "basin")),
        P(None, ("level", "basin")),
        P(("level", "basin")),
        P(("level", "basin")),
        P(),
    )
    out_specs = (P("group", ("level", "basin")), P("basin", None, None))
    return jax.shard_map(body, mesh=mesh, in_specs=in_specs, out_specs=out_specs, check_vma=False)
```

profile of v0, /device:TPU:26, one launch (start us, length us, event | category | flops | bytes accessed | tf_op | source)
XLA Modules:
  0.0 159.9 jit_solution(12532467614339153846)
XLA Ops:
  4.8 2.1 %all_gather.28 = f32[96,1024]{1,0:T(8,128)S(1)} all-gather(f32[48,1024]{1,0:T(8,128)S(1)} %copy-done.4), channel_id=1, replica_groups=mesh['level'=4,'basin'=32,'group'=2] {'group'}, dimensions={0}, use_global_device_ids=true | all-gather | bytes 589824 | tf_op jit(solution)/shard_map/all_gather | solution.py:55
  12.7 2.1 %fusion.4 = f32[288,1152]{1,0:T(8,128)S(1)} fusion(s32[1024]{0:T(1024)S(1)} %bitcast.69, s32[1024]{0:T(1024)S(1)} %bitcast.63, pred[1024]{0:T(1024)(128)(4,1)S(1)} %get-tuple-element.93, pred[1024]{0:T(1024)(128)(4,1)S(1)} %get-tuple-element.92, bf16[96,1024]{1,0:T(8,128)(2,1)S(1)} %get-tuple-element.74, bf16[96,1024]{1,0:T(8,128)(2,1)S(1)} %get-tuple-element.73, ...), kind=kOutput, calls=%fused_computation.7 | convolution fusion | flops 690683904 | bytes 1927168 | tf_op jit(solution)/shard_map/dot_general | solution.py:211
  14.9 2.4 %collective-permute-start.6 = (f32[48,1024]{1,0:T(8,128)S(1)}, f32[48,1024]{1,0:T(8,128)S(1)}, u32[]{:S(2)}, u32[]{:S(2)}) collective-permute-start(f32[48,1024]{1,0:T(8,128)S(1)} %constant_dynamic-slice_fusion.2), channel_id=1, source_target_pairs={{64,0},{128,64},{192,128},{65,1},{129,65},{193,129},{66,2},{130,66... | collective-permute-start | bytes 589832 | tf_op jit(solution)/shard_map/ppermute | solution.py:16
  17.4 2.1 %all_gather.24 = f32[96,1024]{1,0:T(8,128)S(1)} all-gather(f32[48,1024]{1,0:T(8,128)S(1)} %copy-done.5), channel_id=1, replica_groups=mesh['level'=4,'basin'=32,'group'=2] {'group'}, dimensions={0}, use_global_device_ids=true | all-gather | bytes 589824 | tf_op jit(solution)/shard_map/all_gather | solution.py:55
  20.3 6.8 %collective-permute-start.7 = (f32[96,128]{1,0:T(8,128)S(1)}, f32[96,128]{1,0:T(8,128)S(1)}, u32[]{:S(2)}, u32[]{:S(2)}) collective-permute-start(f32[96,128]{1,0:T(8,128)S(1)} %slice.279), channel_id=1, source_target_pairs={{66,0},{68,2},{70,4},{72,6},{74,8},{76,10},{78,12},{80,14},{82,16}... | collective-permute-start | bytes 147464 | tf_op jit(solution)/shard_map/ppermute | solution.py:25
  34.4 4.6 %collective-permute-start = (f32[48,1024]{1,0:T(8,128)S(1)}, f32[48,1024]{1,0:T(8,128)S(1)}, u32[]{:S(2)}, u32[]{:S(2)}) collective-permute-start(f32[48,1024]{1,0:T(8,128)S(1)} %constant_dynamic-slice_fusion.6), channel_id=1, source_target_pairs={{0,64},{64,128},{128,192},{1,65},{65,129},{129,193},{2,66},{66,130... | collective-permute-start | bytes 589832 | tf_op jit(solution)/shard_map/ppermute | solution.py:16
  44.0 2.1 %all_gather.25 = f32[96,1024]{1,0:T(8,128)S(1)} all-gather(f32[48,1024]{1,0:T(8,128)S(1)} %collective-permute-done), channel_id=1, replica_groups=mesh['level'=4,'basin'=32,'group'=2] {'group'}, dimensions={0}, use_global_device_ids=true | all-gather | bytes 589824 | tf_op jit(solution)/shard_map/all_gather | solution.py:55
  52.2 2.1 %fusion.3 = f32[288,1152]{1,0:T(8,128)S(1)} fusion(s32[1024]{0:T(1024)S(1)} %bitcast.71, s32[1024]{0:T(1024)S(1)} %bitcast.65, pred[1024]{0:T(1024)(128)(4,1)S(1)} %get-tuple-element.93, pred[1024]{0:T(1024)(128)(4,1)S(1)} %get-tuple-element.92, bf16[96,1024]{1,0:T(8,128)(2,1)S(1)} %get-tuple-element.72, bf16[96,1024]{1,0:T(8,128)(2,1)S(1)} %get-tuple-element.71, ...), kind=kOutput, calls=%fused_computation.6 | convolution fusion | flops 690683904 | bytes 1927168 | tf_op jit(solution)/shard_map/dot_general | solution.py:211
  56.4 4.5 %collective-permute-start.9 = (f32[96,128]{1,0:T(8,128)S(1)}, f32[96,128]{1,0:T(8,128)S(1)}, u32[]{:S(2)}, u32[]{:S(2)}) collective-permute-start(f32[96,128]{1,0:T(8,128)S(1)} %slice.286), channel_id=1, source_target_pairs={{66,0},{68,2},{70,4},{72,6},{74,8},{76,10},{78,12},{80,14},{82,16}... | collective-permute-start | bytes 147464 | tf_op jit(solution)/shard_map/ppermute | solution.py:25
  67.5 4.6 %collective-permute-start.2 = (f32[48,1024]{1,0:T(8,128)S(1)}, f32[48,1024]{1,0:T(8,128)S(1)}, u32[]{:S(2)}, u32[]{:S(2)}) collective-permute-start(f32[48,1024]{1,0:T(8,128)S(1)} %constant_dynamic-slice_fusion.5), channel_id=1, source_target_pairs={{0,64},{64,128},{128,192},{1,65},{65,129},{129,193},{2,66},{66,130... | collective-permute-start | bytes 589832 | tf_op jit(solution)/shard_map/ppermute | solution.py:16
  77.1 2.3 %all_gather.26 = f32[96,1024]{1,0:T(8,128)S(1)} all-gather(f32[48,1024]{1,0:T(8,128)S(1)} %collective-permute-done.2), channel_id=1, replica_groups=mesh['level'=4,'basin'=32,'group'=2] {'group'}, dimensions={0}, use_global_device_ids=true | all-gather | bytes 589824 | tf_op jit(solution)/shard_map/all_gather | solution.py:55
  85.3 2.1 %fusion.2 = f32[288,1152]{1,0:T(8,128)S(1)} fusion(s32[1024]{0:T(1024)S(1)} %bitcast.73, s32[1024]{0:T(1024)S(1)} %bitcast.67, pred[1024]{0:T(1024)(128)(4,1)S(1)} %get-tuple-element.93, pred[1024]{0:T(1024)(128)(4,1)S(1)} %get-tuple-element.92, bf16[96,1024]{1,0:T(8,128)(2,1)S(1)} %get-tuple-element.70, bf16[96,1024]{1,0:T(8,128)(2,1)S(1)} %get-tuple-element.69, ...), kind=kOutput, calls=%fused_computation.5 | convolution fusion | flops 690683904 | bytes 1927168 | tf_op jit(solution)/shard_map/dot_general | solution.py:211
  89.5 4.7 %collective-permute-start.11 = (f32[96,128]{1,0:T(8,128)S(1)}, f32[96,128]{1,0:T(8,128)S(1)}, u32[]{:S(2)}, u32[]{:S(2)}) collective-permute-start(f32[96,128]{1,0:T(8,128)S(1)} %slice.293), channel_id=1, source_target_pairs={{66,0},{68,2},{70,4},{72,6},{74,8},{76,10},{78,12},{80,14},{82,16}... | collective-permute-start | bytes 147464 | tf_op jit(solution)/shard_map/ppermute | solution.py:25
  100.8 4.6 %collective-permute-start.4 = (f32[48,1024]{1,0:T(8,128)S(1)}, f32[48,1024]{1,0:T(8,128)S(1)}, u32[]{:S(2)}, u32[]{:S(2)}) collective-permute-start(f32[48,1024]{1,0:T(8,128)S(1)} %constant_dynamic-slice_fusion.4), channel_id=1, source_target_pairs={{0,64},{64,128},{128,192},{1,65},{65,129},{129,193},{2,66},{66,130... | collective-permute-start | bytes 589832 | tf_op jit(solution)/shard_map/ppermute | solution.py:16
  107.4 2.5 %collective-permute-done.4 = f32[48,1024]{1,0:T(8,128)S(1)} collective-permute-done((f32[48,1024]{1,0:T(8,128)S(1)}, f32[48,1024]{1,0:T(8,128)S(1)}, u32[]{:S(2)}, u32[]{:S(2)}) %collective-permute-start.4) | collective-permute-done | bytes 196640 | tf_op jit(solution)/shard_map/ppermute | solution.py:16
  112.0 2.5 %collective-permute-done.5 = f32[96,128]{1,0:T(8,128)S(1)} collective-permute-done((f32[96,128]{1,0:T(8,128)S(1)}, f32[96,128]{1,0:T(8,128)S(1)}, u32[]{:S(2)}, u32[]{:S(2)}) %collective-permute-start.5) | collective-permute-done | bytes 49184 | tf_op jit(solution)/shard_map/ppermute | solution.py:25
  119.6 2.1 %shard_map.98 = f32[96,1024]{1,0:T(8,128)} custom-call(f32[1,1024]{1,0:T(1,128)} %get-tuple-element.91.retain_ref, f32[96,1024]{1,0:T(8,128)} %add_add_fusion.drive_ref), custom_call_target="tpu_custom_call" | custom-call | flops 196608 | bytes 790528 | tf_op jit(solution)/shard_map/pallas_call | solution.py:88
  125.3 5.1 %collective-permute-done.12 = f32[16,4,16,2]{2,1,0,3:T(4,128)S(1)} collective-permute-done((f32[16,4,16,2]{2,1,0,3:T(4,128)S(1)}, f32[16,4,16,2]{2,1,0,3:T(4,128)S(1)}, u32[]{:S(2)}, u32[]{:S(2)}) %collective-permute-start.12) | collective-permute-done | bytes 8224 | tf_op jit(solution)/shard_map/ppermute | solution.py:30
  130.7 3.8 %collective-permute-done.13 = f32[8,4,16,2]{2,1,0,3:T(4,128)S(1)} collective-permute-done((f32[8,4,16,2]{2,1,0,3:T(4,128)S(1)}, f32[8,4,16,2]{2,1,0,3:T(4,128)S(1)}, u32[]{:S(2)}, u32[]{:S(2)}) %collective-permute-start.13) | collective-permute-done | bytes 4128 | tf_op jit(solution)/shard_map/ppermute | solution.py:30
  135.2 7.0 %collective-permute-done.14 = f32[4,4,16,2]{2,1,0,3:T(4,128)S(1)} collective-permute-done((f32[4,4,16,2]{2,1,0,3:T(4,128)S(1)}, f32[4,4,16,2]{2,1,0,3:T(4,128)S(1)}, u32[]{:S(2)}, u32[]{:S(2)}) %collective-permute-start.14) | collective-permute-done | bytes 2080 | tf_op jit(solution)/shard_map/ppermute | solution.py:30
  142.4 4.5 %collective-permute-done.15 = f32[2,4,16,2]{2,1,0,3:T(4,128)S(1)} collective-permute-done((f32[2,4,16,2]{2,1,0,3:T(4,128)S(1)}, f32[2,4,16,2]{2,1,0,3:T(4,128)S(1)}, u32[]{:S(2)}, u32[]{:S(2)}) %collective-permute-start.15) | collective-permute-done | bytes 1056 | tf_op jit(solution)/shard_map/ppermute | solution.py:30
  147.0 3.6 %collective-permute-done.16 = f32[1,4,16,2]{2,1,0,3:T(4,128)S(1)} collective-permute-done((f32[1,4,16,2]{2,1,0,3:T(4,128)S(1)}, f32[1,4,16,2]{2,1,0,3:T(4,128)S(1)}, u32[]{:S(2)}, u32[]{:S(2)}) %collective-permute-start.16) | collective-permute-done | bytes 544 | tf_op jit(solution)/shard_map/ppermute | solution.py:30
  150.6 3.6 %collective-permute-done.17 = f32[4,16,2]{1,0,2:T(4,128)S(1)} collective-permute-done((f32[4,16,2]{1,0,2:T(4,128)S(1)}, f32[4,16,2]{1,0,2:T(4,128)S(1)}, u32[]{:S(2)}, u32[]{:S(2)}) %collective-permute-start.17) | collective-permute-done | bytes 544 | tf_op jit(solution)/shard_map/ppermute | solution.py:30
  155.8 3.5 %collective-permute-done.18 = f32[4,16,2]{1,0,2:T(4,128)S(1)} collective-permute-done((f32[4,16,2]{1,0,2:T(4,128)S(1)}, f32[4,16,2]{1,0,2:T(4,128)S(1)}, u32[]{:S(2)}, u32[]{:S(2)}) %collective-permute-start.18) | collective-permute-done | bytes 544 | tf_op jit(solution)/shard_map/ppermute | solution.py:30
  (132 shorter events, 73.0 us)
Async XLA Ops:
  1.5 3.4 %copy-start.4 = (f32[48,1024]{1,0:T(8,128)S(1)}, f32[48,1024]{1,0:T(8,128)}, u32[]{:S(2)}) copy-start(f32[48,1024]{1,0:T(8,128)} %param.15) | copy-start | bytes 589828
  10.4 2.2 %copy-start.6 = (s32[2,1024]{1,0:T(2,128)S(1)}, s32[2,1024]{1,0:T(2,128)}, u32[]{:S(2)}) copy-start(s32[2,1024]{1,0:T(2,128)} %param.18) | copy-start | bytes 24580
  10.4 2.3 %copy-start.7 = (s32[1024]{0:T(1024)S(1)}, s32[1024]{0:T(1024)}, u32[]{:S(2)}) copy-start(s32[1024]{0:T(1024)} %param.19) | copy-start | bytes 12292
  14.8 2.6 %copy-start.5 = (f32[48,1024]{1,0:T(8,128)S(1)}, f32[48,1024]{1,0:T(8,128)}, u32[]{:S(2)}) copy-start(f32[48,1024]{1,0:T(8,128)} %param.14) | copy-start | bytes 589828
  14.9 14.8 %collective-permute-start.6 = (f32[48,1024]{1,0:T(8,128)S(1)}, f32[48,1024]{1,0:T(8,128)S(1)}, u32[]{:S(2)}, u32[]{:S(2)}) collective-permute-start(f32[48,1024]{1,0:T(8,128)S(1)} %constant_dynamic-slice_fusion.2), channel_id=1, source_target_pairs={{64,0},{128,64},{192,128},{65,1},{129,65},{193,129},{66,2},{130,66... | collective-permute-start | bytes 589832 | tf_op jit(solution)/shard_map/ppermute | solution.py:16
  20.3 11.5 %collective-permute-start.7 = (f32[96,128]{1,0:T(8,128)S(1)}, f32[96,128]{1,0:T(8,128)S(1)}, u32[]{:S(2)}, u32[]{:S(2)}) collective-permute-start(f32[96,128]{1,0:T(8,128)S(1)} %slice.279), channel_id=1, source_target_pairs={{66,0},{68,2},{70,4},{72,6},{74,8},{76,10},{78,12},{80,14},{82,16}... | collective-permute-start | bytes 147464 | tf_op jit(solution)/shard_map/ppermute | solution.py:25
  34.4 9.6 %collective-permute-start = (f32[48,1024]{1,0:T(8,128)S(1)}, f32[48,1024]{1,0:T(8,128)S(1)}, u32[]{:S(2)}, u32[]{:S(2)}) collective-permute-start(f32[48,1024]{1,0:T(8,128)S(1)} %constant_dynamic-slice_fusion.6), channel_id=1, source_target_pairs={{0,64},{64,128},{128,192},{1,65},{65,129},{129,193},{2,66},{66,130... | collective-permute-start | bytes 589832 | tf_op jit(solution)/shard_map/ppermute | solution.py:16
  38.9 9.0 %collective-permute-start.1 = (f32[96,128]{1,0:T(8,128)S(1)}, f32[96,128]{1,0:T(8,128)S(1)}, u32[]{:S(2)}, u32[]{:S(2)}) collective-permute-start(f32[96,128]{1,0:T(8,128)S(1)} %slice.258), channel_id=1, source_target_pairs={{0,66},{2,68},{4,70},{6,72},{8,74},{10,76},{12,78},{14,80},{16,82}... | collective-permute-start | bytes 147464 | tf_op jit(solution)/shard_map/ppermute | solution.py:25
  54.4 8.5 %collective-permute-start.8 = (f32[48,1024]{1,0:T(8,128)S(1)}, f32[48,1024]{1,0:T(8,128)S(1)}, u32[]{:S(2)}, u32[]{:S(2)}) collective-permute-start(f32[48,1024]{1,0:T(8,128)S(1)} %constant_dynamic-slice_fusion.1), channel_id=1, source_target_pairs={{64,0},{128,64},{192,128},{65,1},{129,65},{193,129},{66,2},{130,66... | collective-permute-start | bytes 589832 | tf_op jit(solution)/shard_map/ppermute | solution.py:16
  56.4 8.6 %collective-permute-start.9 = (f32[96,128]{1,0:T(8,128)S(1)}, f32[96,128]{1,0:T(8,128)S(1)}, u32[]{:S(2)}, u32[]{:S(2)}) collective-permute-start(f32[96,128]{1,0:T(8,128)S(1)} %slice.286), channel_id=1, source_target_pairs={{66,0},{68,2},{70,4},{72,6},{74,8},{76,10},{78,12},{80,14},{82,16}... | collective-permute-start | bytes 147464 | tf_op jit(solution)/shard_map/ppermute | solution.py:25
  67.5 9.6 %collective-permute-start.2 = (f32[48,1024]{1,0:T(8,128)S(1)}, f32[48,1024]{1,0:T(8,128)S(1)}, u32[]{:S(2)}, u32[]{:S(2)}) collective-permute-start(f32[48,1024]{1,0:T(8,128)S(1)} %constant_dynamic-slice_fusion.5), channel_id=1, source_target_pairs={{0,64},{64,128},{128,192},{1,65},{65,129},{129,193},{2,66},{66,130... | collective-permute-start | bytes 589832 | tf_op jit(solution)/shard_map/ppermute | solution.py:16
  72.1 9.0 %collective-permute-start.3 = (f32[96,128]{1,0:T(8,128)S(1)}, f32[96,128]{1,0:T(8,128)S(1)}, u32[]{:S(2)}, u32[]{:S(2)}) collective-permute-start(f32[96,128]{1,0:T(8,128)S(1)} %slice.263), channel_id=1, source_target_pairs={{0,66},{2,68},{4,70},{6,72},{8,74},{10,76},{12,78},{14,80},{16,82}... | collective-permute-start | bytes 147464 | tf_op jit(solution)/shard_map/ppermute | solution.py:25
  87.6 8.7 %collective-permute-start.10 = (f32[48,1024]{1,0:T(8,128)S(1)}, f32[48,1024]{1,0:T(8,128)S(1)}, u32[]{:S(2)}, u32[]{:S(2)}) collective-permute-start(f32[48,1024]{1,0:T(8,128)S(1)} %constant_dynamic-slice_fusion), channel_id=1, source_target_pairs={{64,0},{128,64},{192,128},{65,1},{129,65},{193,129},{66,2},{130,66... | collective-permute-start | bytes 589832 | tf_op jit(solution)/shard_map/ppermute | solution.py:16
  89.5 8.8 %collective-permute-start.11 = (f32[96,128]{1,0:T(8,128)S(1)}, f32[96,128]{1,0:T(8,128)S(1)}, u32[]{:S(2)}, u32[]{:S(2)}) collective-permute-start(f32[96,128]{1,0:T(8,128)S(1)} %slice.293), channel_id=1, source_target_pairs={{66,0},{68,2},{70,4},{72,6},{74,8},{76,10},{78,12},{80,14},{82,16}... | collective-permute-start | bytes 147464 | tf_op jit(solution)/shard_map/ppermute | solution.py:25
  100.8 9.0 %collective-permute-start.4 = (f32[48,1024]{1,0:T(8,128)S(1)}, f32[48,1024]{1,0:T(8,128)S(1)}, u32[]{:S(2)}, u32[]{:S(2)}) collective-permute-start(f32[48,1024]{1,0:T(8,128)S(1)} %constant_dynamic-slice_fusion.4), channel_id=1, source_target_pairs={{0,64},{64,128},{128,192},{1,65},{65,129},{129,193},{2,66},{66,130... | collective-permute-start | bytes 589832 | tf_op jit(solution)/shard_map/ppermute | solution.py:16
  105.4 9.0 %collective-permute-start.5 = (f32[96,128]{1,0:T(8,128)S(1)}, f32[96,128]{1,0:T(8,128)S(1)}, u32[]{:S(2)}, u32[]{:S(2)}) collective-permute-start(f32[96,128]{1,0:T(8,128)S(1)} %slice.268), channel_id=1, source_target_pairs={{0,66},{2,68},{4,70},{6,72},{8,74},{10,76},{12,78},{14,80},{16,82}... | collective-permute-start | bytes 147464 | tf_op jit(solution)/shard_map/ppermute | solution.py:25
  119.6 3.1 %copy-start.3 = (f32[96,1024]{1,0:T(8,128)S(1)}, f32[96,1024]{1,0:T(8,128)}, u32[]{:S(2)}) copy-start(f32[96,1024]{1,0:T(8,128)} %shard_map.102) | copy-start | bytes 1179652
  124.3 6.2 %collective-permute-start.12 = (f32[16,4,16,2]{2,1,0,3:T(4,128)S(1)}, f32[16,4,16,2]{2,1,0,3:T(4,128)S(1)}, u32[]{:S(2)}, u32[]{:S(2)}) collective-permute-start(f32[16,4,16,2]{2,1,0,3:T(4,128)S(1)} %bitcast.56), channel_id=1, source_target_pairs={{0,32},{2,34},{4,36},{6,38},{8,40},{10,42},{12,44},{14,46},{16,48}... | collective-permute-start | bytes 24584 | tf_op jit(solution)/shard_map/ppermute | solution.py:30
  130.5 4.0 %collective-permute-start.13 = (f32[8,4,16,2]{2,1,0,3:T(4,128)S(1)}, f32[8,4,16,2]{2,1,0,3:T(4,128)S(1)}, u32[]{:S(2)}, u32[]{:S(2)}) collective-permute-start(f32[8,4,16,2]{2,1,0,3:T(4,128)S(1)} %slice_select_fusion), channel_id=1, source_target_pairs={{0,16},{2,18},{4,20},{6,22},{8,24},{10,26},{12,28},{14,30},{16,0},... | collective-permute-start | bytes 12296 | tf_op jit(solution)/shard_map/ppermute | solution.py:30
  134.5 7.7 %collective-permute-start.14 = (f32[4,4,16,2]{2,1,0,3:T(4,128)S(1)}, f32[4,4,16,2]{2,1,0,3:T(4,128)S(1)}, u32[]{:S(2)}, u32[]{:S(2)}) collective-permute-start(f32[4,4,16,2]{2,1,0,3:T(4,128)S(1)} %slice_select_fusion.3), channel_id=1, source_target_pairs={{0,8},{2,10},{4,12},{6,14},{8,0},{10,2},{12,4},{14,6},{16,24},{18,... | collective-permute-start | bytes 6152 | tf_op jit(solution)/shard_map/ppermute | solution.py:30
  142.3 4.6 %collective-permute-start.15 = (f32[2,4,16,2]{2,1,0,3:T(4,128)S(1)}, f32[2,4,16,2]{2,1,0,3:T(4,128)S(1)}, u32[]{:S(2)}, u32[]{:S(2)}) collective-permute-start(f32[2,4,16,2]{2,1,0,3:T(4,128)S(1)} %slice_select_fusion.4), channel_id=1, source_target_pairs={{0,4},{2,6},{4,0},{6,2},{8,12},{10,14},{12,8},{14,10},{16,20},{18,... | collective-permute-start | bytes 3080 | tf_op jit(solution)/shard_map/ppermute | solution.py:30
  146.9 3.7 %collective-permute-start.16 = (f32[1,4,16,2]{2,1,0,3:T(4,128)S(1)}, f32[1,4,16,2]{2,1,0,3:T(4,128)S(1)}, u32[]{:S(2)}, u32[]{:S(2)}) collective-permute-start(f32[1,4,16,2]{2,1,0,3:T(4,128)S(1)} %slice_select_fusion.5), channel_id=1, source_target_pairs={{0,2},{2,0},{4,6},{6,4},{8,10},{10,8},{12,14},{14,12},{16,18},{18,... | collective-permute-start | bytes 1544 | tf_op jit(solution)/shard_map/ppermute | solution.py:30
  150.6 3.6 %collective-permute-start.17 = (f32[4,16,2]{1,0,2:T(4,128)S(1)}, f32[4,16,2]{1,0,2:T(4,128)S(1)}, u32[]{:S(2)}, u32[]{:S(2)}) collective-permute-start(f32[4,16,2]{1,0,2:T(4,128)S(1)} %add_bitcast_fusion), channel_id=1, source_target_pairs={{0,64},{64,0},{128,192},{192,128},{1,65},{65,1},{129,193},{193,129... | collective-permute-start | bytes 1544 | tf_op jit(solution)/shard_map/ppermute | solution.py:30
  154.2 5.1 %collective-permute-start.18 = (f32[4,16,2]{1,0,2:T(4,128)S(1)}, f32[4,16,2]{1,0,2:T(4,128)S(1)}, u32[]{:S(2)}, u32[]{:S(2)}) collective-permute-start(f32[4,16,2]{1,0,2:T(4,128)S(1)} %add.252), channel_id=1, source_target_pairs={{0,128},{64,192},{128,0},{192,64},{1,129},{65,193},{129,1},{193,65... | collective-permute-start | bytes 1544 | tf_op jit(solution)/shard_map/ppermute | solution.py:30
  (3 other events, 2.8 us)
where the time goes:
time: 161 us; the launch traced here: 160 us
  starting transfers between devices  44.6 us (28%)
  waiting for transfers between devices  39.7 us (25%)
  other arithmetic  18.8 us (12%)
  blocking collectives  16.8 us (10%)
  Pallas kernels  16.4 us (10%)
  matrix products  15 us (9%)
  local copies, waits for them, and re-layouts  6.79 us (4%)
  between operations  1.94 us (1%)
    ppermute x7, waiting for transfers between devices, exchanged(): lax.ppermute(value, axis, [(source, source ^ mask) for source in range(co...  31.2 us
    ppermute x6, starting transfers between devices, diagonal(): return lax.ppermute(value, ('level', 'basin'), pairs)  21.6 us
    ppermute x6, starting transfers between devices, shifted(): lax.ppermute(value, axis, [(source, source + steps) for source in range(l...  19.9 us
    all_gather x8, blocking collectives, whole_window(): return lax.all_gather(value, 'group', axis=0, tiled=True)  16.8 us
    pallas_call x8, Pallas kernels, recurrence(): pl.pallas_call(functools.partial(recurrence_kernel, reverse=reverse), out...  16.4 us
    mul x4, other arithmetic, body(): adjoint_load = live_mask * (cotangent_all + adjoint_down)  6.4 us
    dot_general x3, matrix products, body(): lax.dot_general(split_three(to_inflow), confluence, (((1,), (1,)), ((), (...  6.26 us
    dot_general x3, matrix products, body(): jnp.dot(split_three(source), confluence, preferred_element_type=jnp.float32)  5.99 us
  transfers between devices with their start and end apart: 19, of which 11 were waited for; matrix products, arithmetic and copies ran while one was open for 3% of the time, Pallas kernels for 6%

commit v1 on v0

--- a/solution.py
+++ b/solution.py
@@ -236,10 +236,13 @@
     )
     local_grad = jnp.transpose(summed.reshape(regions, param_count, attr_count), (0, 2, 1))
     basins = lax.axis_size("basin")
-    owned_share = scattered_sum(
-        local_grad.reshape(basins, owned_rows, attr_count, param_count), "basin"
-    )
-    grad_net = butterfly_sum(owned_share, "level")
+    share_size = owned_rows * attr_count * param_count
+    replicated = jnp.broadcast_to(
+        local_grad.reshape(1, basins, share_size), (levels, basins, share_size)
+    ).reshape(levels * basins, share_size)
+    grad_net = jnp.sum(
+        lax.all_to_all(replicated, ("level", "basin"), 0, 0, tiled=True), axis=0
+    ).reshape(owned_rows, attr_count, param_count)
     return (own_half(outflow), grad_net)
 
 

time: 161 us -> 152 us (0.944)
  the two profiles are of different devices: /device:TPU:26 before, /device:TPU:1 now
where the time goes in v1:
time: 152 us; the launch traced here: 150 us
  starting transfers between devices  46.9 us (31%)
  blocking collectives  26.5 us (17%)
  other arithmetic  18.5 us (12%)
  waiting for transfers between devices  16.6 us (11%)
  Pallas kernels  16.4 us (11%)
  matrix products  14.3 us (9%)
  local copies, waits for them, and re-layouts  9.22 us (6%)
  between operations  1.93 us (1%)
    all_gather x8, blocking collectives, whole_window(): return lax.all_gather(value, 'group', axis=0, tiled=True)  26.5 us
    all_to_all x1, starting transfers between devices, body(): lax.all_to_all(replicated, ('level', 'basin'), 0, 0, tiled=True)  19.2 us
    pallas_call x8, Pallas kernels, recurrence(): pl.pallas_call(functools.partial(recurrence_kernel, reverse=reverse), out...  16.4 us
    ppermute x6, starting transfers between devices, diagonal(): return lax.ppermute(value, ('level', 'basin'), pairs)  15.9 us
    ppermute x6, starting transfers between devices, shifted(): lax.ppermute(value, axis, [(source, source + steps) for source in range(l...  11.8 us
    all_to_all x1, waiting for transfers between devices, body(): lax.all_to_all(replicated, ('level', 'basin'), 0, 0, tiled=True)  9.89 us
    ppermute x6, waiting for transfers between devices, shifted(): lax.ppermute(value, axis, [(source, source + steps) for source in range(l...  6.72 us
    mul x4, other arithmetic, body(): adjoint_load = live_mask * (cotangent_all + adjoint_down)  6.37 us
  transfers between devices with their start and end apart: 13, of which 3 were waited for; matrix products, arithmetic and copies ran while one was open for 3% of the time, Pallas kernels for 7%

profile of v1, /device:TPU:1, one launch (start us, length us, event | category | flops | bytes accessed | tf_op | source)
XLA Modules:
  0.0 150.3 jit_solution(10657663081746285073)
XLA Ops:
  2.8 5.1 %all_gather.28 = f32[96,1024]{1,0:T(8,128)S(1)} all-gather(f32[48,1024]{1,0:T(8,128)} %param.15), channel_id=1, replica_groups=mesh['level'=4,'basin'=32,'group'=2] {'group'}, dimensions={0}, use_global_device_ids=true | all-gather | bytes 589824 | tf_op jit(solution)/shard_map/all_gather | solution.py:55
  15.5 2.1 %fusion.5 = f32[288,1152]{1,0:T(8,128)S(1)} fusion(s32[1024]{0:T(1024)S(1)} %bitcast.65, s32[1024]{0:T(1024)S(1)} %bitcast.59, pred[1024]{0:T(1024)(128)(4,1)S(1)} %get-tuple-element.93, pred[1024]{0:T(1024)(128)(4,1)S(1)} %get-tuple-element.92, bf16[96,1024]{1,0:T(8,128)(2,1)S(1)} %get-tuple-element.76, bf16[96,1024]{1,0:T(8,128)(2,1)S(1)} %get-tuple-element.75, ...), kind=kOutput, calls=%fused_computation.9 | convolution fusion | flops 690683904 | bytes 1927168 | tf_op jit(solution)/shard_map/dot_general | solution.py:211
  19.1 2.1 %all_gather.24 = f32[96,1024]{1,0:T(8,128)S(1)} all-gather(f32[48,1024]{1,0:T(8,128)S(1)} %copy-done.4), channel_id=1, replica_groups=mesh['level'=4,'basin'=32,'group'=2] {'group'}, dimensions={0}, use_global_device_ids=true | all-gather | bytes 589824 | tf_op jit(solution)/shard_map/all_gather | solution.py:55
  25.9 2.7 %all_gather.29 = f32[96,1024]{1,0:T(8,128)S(1)} all-gather(f32[48,1024]{1,0:T(8,128)S(1)} %collective-permute-done.6), channel_id=1, replica_groups=mesh['level'=4,'basin'=32,'group'=2] {'group'}, dimensions={0}, use_global_device_ids=true | all-gather | bytes 589824 | tf_op jit(solution)/shard_map/all_gather | solution.py:55
  31.2 3.6 %collective-permute-start = (f32[48,1024]{1,0:T(8,128)S(1)}, f32[48,1024]{1,0:T(8,128)S(1)}, u32[]{:S(2)}, u32[]{:S(2)}) collective-permute-start(f32[48,1024]{1,0:T(8,128)S(1)} %constant_dynamic-slice_fusion.6), channel_id=1, source_target_pairs={{0,64},{64,128},{128,192},{1,65},{65,129},{129,193},{2,66},{66,130... | collective-permute-start | bytes 589832 | tf_op jit(solution)/shard_map/ppermute | solution.py:16
  34.8 2.1 %shard_map.100 = f32[96,1024]{1,0:T(8,128)} custom-call(f32[1,1024]{1,0:T(1,128)} %get-tuple-element.91.retain_ref, f32[96,1024]{1,0:T(8,128)} %get-tuple-element.87.drive_ref), custom_call_target="tpu_custom_call" | custom-call | flops 196608 | bytes 790528 | tf_op jit(solution)/shard_map/pallas_call | solution.py:88
  36.9 5.2 %collective-permute-start.1 = (f32[96,128]{1,0:T(8,128)S(1)}, f32[96,128]{1,0:T(8,128)S(1)}, u32[]{:S(2)}, u32[]{:S(2)}) collective-permute-start(f32[96,128]{1,0:T(8,128)S(1)} %slice.216), channel_id=1, source_target_pairs={{0,66},{2,68},{4,70},{6,72},{8,74},{10,76},{12,78},{14,80},{16,82}... | collective-permute-start | bytes 147464 | tf_op jit(solution)/shard_map/ppermute | solution.py:25
  43.1 2.6 %all_gather.25 = f32[96,1024]{1,0:T(8,128)S(1)} all-gather(f32[48,1024]{1,0:T(8,128)S(1)} %collective-permute-done), channel_id=1, replica_groups=mesh['level'=4,'basin'=32,'group'=2] {'group'}, dimensions={0}, use_global_device_ids=true | all-gather | bytes 589824 | tf_op jit(solution)/shard_map/all_gather | solution.py:55
  50.0 2.1 %fusion.4 = f32[288,1152]{1,0:T(8,128)S(1)} fusion(s32[1024]{0:T(1024)S(1)} %bitcast.67, s32[1024]{0:T(1024)S(1)} %bitcast.61, pred[1024]{0:T(1024)(128)(4,1)S(1)} %get-tuple-element.93, pred[1024]{0:T(1024)(128)(4,1)S(1)} %get-tuple-element.92, bf16[96,1024]{1,0:T(8,128)(2,1)S(1)} %get-tuple-element.74, bf16[96,1024]{1,0:T(8,128)(2,1)S(1)} %get-tuple-element.73, ...), kind=kOutput, calls=%fused_computation.8 | convolution fusion | flops 690683904 | bytes 1927168 | tf_op jit(solution)/shard_map/dot_general | solution.py:211
  56.9 3.4 %collective-permute-done.8 = f32[48,1024]{1,0:T(8,128)S(1)} collective-permute-done((f32[48,1024]{1,0:T(8,128)S(1)}, f32[48,1024]{1,0:T(8,128)S(1)}, u32[]{:S(2)}, u32[]{:S(2)}) %collective-permute-start.8) | collective-permute-done | bytes 196640 | tf_op jit(solution)/shard_map/ppermute | solution.py:16
  60.3 2.9 %all_gather.30 = f32[96,1024]{1,0:T(8,128)S(1)} all-gather(f32[48,1024]{1,0:T(8,128)S(1)} %collective-permute-done.8), channel_id=1, replica_groups=mesh['level'=4,'basin'=32,'group'=2] {'group'}, dimensions={0}, use_global_device_ids=true | all-gather | bytes 589824 | tf_op jit(solution)/shard_map/all_gather | solution.py:55
  65.7 2.1 %collective-permute-start.2 = (f32[48,1024]{1,0:T(8,128)S(1)}, f32[48,1024]{1,0:T(8,128)S(1)}, u32[]{:S(2)}, u32[]{:S(2)}) collective-permute-start(f32[48,1024]{1,0:T(8,128)S(1)} %constant_dynamic-slice_fusion.5), channel_id=1, source_target_pairs={{0,64},{64,128},{128,192},{1,65},{65,129},{129,193},{2,66},{66,130... | collective-permute-start | bytes 589832 | tf_op jit(solution)/shard_map/ppermute | solution.py:16
  67.9 2.1 %shard_map.101 = f32[96,1024]{1,0:T(8,128)} custom-call(f32[1,1024]{1,0:T(1,128)} %get-tuple-element.91.retain_ref, f32[96,1024]{1,0:T(8,128)} %get-tuple-element.85.drive_ref), custom_call_target="tpu_custom_call" | custom-call | flops 196608 | bytes 790528 | tf_op jit(solution)/shard_map/pallas_call | solution.py:88
  69.9 3.1 %collective-permute-start.3 = (f32[96,128]{1,0:T(8,128)S(1)}, f32[96,128]{1,0:T(8,128)S(1)}, u32[]{:S(2)}, u32[]{:S(2)}) collective-permute-start(f32[96,128]{1,0:T(8,128)S(1)} %slice.221), channel_id=1, source_target_pairs={{0,66},{2,68},{4,70},{6,72},{8,74},{10,76},{12,78},{14,80},{16,82}... | collective-permute-start | bytes 147464 | tf_op jit(solution)/shard_map/ppermute | solution.py:25
  74.1 4.5 %all_gather.26 = f32[96,1024]{1,0:T(8,128)S(1)} all-gather(f32[48,1024]{1,0:T(8,128)S(1)} %collective-permute-done.2), channel_id=1, replica_groups=mesh['level'=4,'basin'=32,'group'=2] {'group'}, dimensions={0}, use_global_device_ids=true | all-gather | bytes 589824 | tf_op jit(solution)/shard_map/all_gather | solution.py:55
  83.0 2.1 %fusion.3 = f32[288,1152]{1,0:T(8,128)S(1)} fusion(s32[1024]{0:T(1024)S(1)} %bitcast.69, s32[1024]{0:T(1024)S(1)} %bitcast.63, pred[1024]{0:T(1024)(128)(4,1)S(1)} %get-tuple-element.93, pred[1024]{0:T(1024)(128)(4,1)S(1)} %get-tuple-element.92, bf16[96,1024]{1,0:T(8,128)(2,1)S(1)} %get-tuple-element.72, bf16[96,1024]{1,0:T(8,128)(2,1)S(1)} %get-tuple-element.71, ...), kind=kOutput, calls=%fused_computation.7 | convolution fusion | flops 690683904 | bytes 1927168 | tf_op jit(solution)/shard_map/dot_general | solution.py:211
  89.8 3.3 %collective-permute-done.10 = f32[48,1024]{1,0:T(8,128)S(1)} collective-permute-done((f32[48,1024]{1,0:T(8,128)S(1)}, f32[48,1024]{1,0:T(8,128)S(1)}, u32[]{:S(2)}, u32[]{:S(2)}) %collective-permute-start.10) | collective-permute-done | bytes 196640 | tf_op jit(solution)/shard_map/ppermute | solution.py:16
  93.2 2.9 %all_gather.31 = f32[96,1024]{1,0:T(8,128)S(1)} all-gather(f32[48,1024]{1,0:T(8,128)S(1)} %collective-permute-done.10), channel_id=1, replica_groups=mesh['level'=4,'basin'=32,'group'=2] {'group'}, dimensions={0}, use_global_device_ids=true | all-gather | bytes 589824 | tf_op jit(solution)/shard_map/all_gather | solution.py:55
  98.7 2.1 %collective-permute-start.4 = (f32[48,1024]{1,0:T(8,128)S(1)}, f32[48,1024]{1,0:T(8,128)S(1)}, u32[]{:S(2)}, u32[]{:S(2)}) collective-permute-start(f32[48,1024]{1,0:T(8,128)S(1)} %constant_dynamic-slice_fusion.4), channel_id=1, source_target_pairs={{0,64},{64,128},{128,192},{1,65},{65,129},{129,193},{2,66},{66,130... | collective-permute-start | bytes 589832 | tf_op jit(solution)/shard_map/ppermute | solution.py:16
  100.8 3.8 %collective-permute-start.5 = (f32[96,128]{1,0:T(8,128)S(1)}, f32[96,128]{1,0:T(8,128)S(1)}, u32[]{:S(2)}, u32[]{:S(2)}) collective-permute-start(f32[96,128]{1,0:T(8,128)S(1)} %slice.226), channel_id=1, source_target_pairs={{0,66},{2,68},{4,70},{6,72},{8,74},{10,76},{12,78},{14,80},{16,82}... | collective-permute-start | bytes 147464 | tf_op jit(solution)/shard_map/ppermute | solution.py:25
  104.6 3.5 %all_gather.27 = f32[96,1024]{1,0:T(8,128)S(1)} all-gather(f32[48,1024]{1,0:T(8,128)S(1)} %collective-permute-done.4), channel_id=1, replica_groups=mesh['level'=4,'basin'=32,'group'=2] {'group'}, dimensions={0}, use_global_device_ids=true | all-gather | bytes 589824 | tf_op jit(solution)/shard_map/all_gather | solution.py:55
  113.4 2.1 %shard_map.98 = f32[96,1024]{1,0:T(8,128)} custom-call(f32[1,1024]{1,0:T(1,128)} %get-tuple-element.91.retain_ref, f32[96,1024]{1,0:T(8,128)} %add_add_fusion.drive_ref), custom_call_target="tpu_custom_call" | custom-call | flops 196608 | bytes 790528 | tf_op jit(solution)/shard_map/pallas_call | solution.py:88
  119.5 19.2 %all-to-all-start = ((f32[128,1,128]{2,1,0:T(1,128)}), f32[128,1,128]{2,1,0:T(1,128)S(1)}, u32[]{:S(2)}, u32[]{:S(2)}) async-start(f32[128,1,128]{2,1,0:T(1,128)} %bitcast.16), calls=%async_computation | async-start | bytes 131072 | tf_op jit(solution)/shard_map/all_to_all | solution.py:244
  139.5 9.9 %all-to-all-done = f32[128,1,128]{2,1,0:T(1,128)S(1)} async-done(((f32[128,1,128]{2,1,0:T(1,128)}), f32[128,1,128]{2,1,0:T(1,128)S(1)}, u32[]{:S(2)}, u32[]{:S(2)}) %all-to-all-start) | async-done | bytes 65568 | tf_op jit(solution)/shard_map/all_to_all | solution.py:244
  (106 shorter events, 53.6 us)
Async XLA Ops:
  0.6 8.1 %copy-start = (f32[16,1024]{1,0:T(8,128)S(1)}, f32[16,1024]{1,0:T(8,128)}, u32[]{:S(2)}) copy-start(f32[16,1024]{1,0:T(8,128)} %param.16) | copy-start | bytes 196612
  0.6 8.1 %copy-start.5 = (f32[128,16,2]{0,2,1:T(2,128)S(1)}, f32[128,16,2]{0,2,1:T(2,128)}, u32[]{:S(2)}) copy-start(f32[128,16,2]{0,2,1:T(2,128)} %param.21) | copy-start | bytes 49156
  17.6 1.5 copy-start.4
  17.7 8.2 %collective-permute-start.6 = (f32[48,1024]{1,0:T(8,128)S(1)}, f32[48,1024]{1,0:T(8,128)S(1)}, u32[]{:S(2)}, u32[]{:S(2)}) collective-permute-start(f32[48,1024]{1,0:T(8,128)S(1)} %constant_dynamic-slice_fusion.2), channel_id=1, source_target_pairs={{64,0},{128,64},{192,128},{65,1},{129,65},{193,129},{66,2},{130,66... | collective-permute-start | bytes 589832 | tf_op jit(solution)/shard_map/ppermute | solution.py:16
  22.0 6.7 %collective-permute-start.7 = (f32[96,128]{1,0:T(8,128)S(1)}, f32[96,128]{1,0:T(8,128)S(1)}, u32[]{:S(2)}, u32[]{:S(2)}) collective-permute-start(f32[96,128]{1,0:T(8,128)S(1)} %slice.237), channel_id=1, source_target_pairs={{66,0},{68,2},{70,4},{72,6},{74,8},{76,10},{78,12},{80,14},{82,16}... | collective-permute-start | bytes 147464 | tf_op jit(solution)/shard_map/ppermute | solution.py:25
  31.2 11.9 %collective-permute-start = (f32[48,1024]{1,0:T(8,128)S(1)}, f32[48,1024]{1,0:T(8,128)S(1)}, u32[]{:S(2)}, u32[]{:S(2)}) collective-permute-start(f32[48,1024]{1,0:T(8,128)S(1)} %constant_dynamic-slice_fusion.6), channel_id=1, source_target_pairs={{0,64},{64,128},{128,192},{1,65},{65,129},{129,193},{2,66},{66,130... | collective-permute-start | bytes 589832 | tf_op jit(solution)/shard_map/ppermute | solution.py:16
  36.9 8.9 %collective-permute-start.1 = (f32[96,128]{1,0:T(8,128)S(1)}, f32[96,128]{1,0:T(8,128)S(1)}, u32[]{:S(2)}, u32[]{:S(2)}) collective-permute-start(f32[96,128]{1,0:T(8,128)S(1)} %slice.216), channel_id=1, source_target_pairs={{0,66},{2,68},{4,70},{6,72},{8,74},{10,76},{12,78},{14,80},{16,82}... | collective-permute-start | bytes 147464 | tf_op jit(solution)/shard_map/ppermute | solution.py:25
  47.9 1.0 copy-start.1
  52.3 8.0 %collective-permute-start.8 = (f32[48,1024]{1,0:T(8,128)S(1)}, f32[48,1024]{1,0:T(8,128)S(1)}, u32[]{:S(2)}, u32[]{:S(2)}) collective-permute-start(f32[48,1024]{1,0:T(8,128)S(1)} %constant_dynamic-slice_fusion.1), channel_id=1, source_target_pairs={{64,0},{128,64},{192,128},{65,1},{129,65},{193,129},{66,2},{130,66... | collective-permute-start | bytes 589832 | tf_op jit(solution)/shard_map/ppermute | solution.py:16
  55.6 7.6 %collective-permute-start.9 = (f32[96,128]{1,0:T(8,128)S(1)}, f32[96,128]{1,0:T(8,128)S(1)}, u32[]{:S(2)}, u32[]{:S(2)}) collective-permute-start(f32[96,128]{1,0:T(8,128)S(1)} %slice.244), channel_id=1, source_target_pairs={{66,0},{68,2},{70,4},{72,6},{74,8},{76,10},{78,12},{80,14},{82,16}... | collective-permute-start | bytes 147464 | tf_op jit(solution)/shard_map/ppermute | solution.py:25
  65.7 8.4 %collective-permute-start.2 = (f32[48,1024]{1,0:T(8,128)S(1)}, f32[48,1024]{1,0:T(8,128)S(1)}, u32[]{:S(2)}, u32[]{:S(2)}) collective-permute-start(f32[48,1024]{1,0:T(8,128)S(1)} %constant_dynamic-slice_fusion.5), channel_id=1, source_target_pairs={{0,64},{64,128},{128,192},{1,65},{65,129},{129,193},{2,66},{66,130... | collective-permute-start | bytes 589832 | tf_op jit(solution)/shard_map/ppermute | solution.py:16
  69.9 8.7 %collective-permute-start.3 = (f32[96,128]{1,0:T(8,128)S(1)}, f32[96,128]{1,0:T(8,128)S(1)}, u32[]{:S(2)}, u32[]{:S(2)}) collective-permute-start(f32[96,128]{1,0:T(8,128)S(1)} %slice.221), channel_id=1, source_target_pairs={{0,66},{2,68},{4,70},{6,72},{8,74},{10,76},{12,78},{14,80},{16,82}... | collective-permute-start | bytes 147464 | tf_op jit(solution)/shard_map/ppermute | solution.py:25
  80.8 1.0 copy-start.2
  85.2 8.0 %collective-permute-start.10 = (f32[48,1024]{1,0:T(8,128)S(1)}, f32[48,1024]{1,0:T(8,128)S(1)}, u32[]{:S(2)}, u32[]{:S(2)}) collective-permute-start(f32[48,1024]{1,0:T(8,128)S(1)} %constant_dynamic-slice_fusion), channel_id=1, source_target_pairs={{64,0},{128,64},{192,128},{65,1},{129,65},{193,129},{66,2},{130,66... | collective-permute-start | bytes 589832 | tf_op jit(solution)/shard_map/ppermute | solution.py:16
  88.5 7.6 %collective-permute-start.11 = (f32[96,128]{1,0:T(8,128)S(1)}, f32[96,128]{1,0:T(8,128)S(1)}, u32[]{:S(2)}, u32[]{:S(2)}) collective-permute-start(f32[96,128]{1,0:T(8,128)S(1)} %slice.251), channel_id=1, source_target_pairs={{66,0},{68,2},{70,4},{72,6},{74,8},{76,10},{78,12},{80,14},{82,16}... | collective-permute-start | bytes 147464 | tf_op jit(solution)/shard_map/ppermute | solution.py:25
  98.7 6.0 %collective-permute-start.4 = (f32[48,1024]{1,0:T(8,128)S(1)}, f32[48,1024]{1,0:T(8,128)S(1)}, u32[]{:S(2)}, u32[]{:S(2)}) collective-permute-start(f32[48,1024]{1,0:T(8,128)S(1)} %constant_dynamic-slice_fusion.4), channel_id=1, source_target_pairs={{0,64},{64,128},{128,192},{1,65},{65,129},{129,193},{2,66},{66,130... | collective-permute-start | bytes 589832 | tf_op jit(solution)/shard_map/ppermute | solution.py:16
  100.8 7.3 %collective-permute-start.5 = (f32[96,128]{1,0:T(8,128)S(1)}, f32[96,128]{1,0:T(8,128)S(1)}, u32[]{:S(2)}, u32[]{:S(2)}) collective-permute-start(f32[96,128]{1,0:T(8,128)S(1)} %slice.226), channel_id=1, source_target_pairs={{0,66},{2,68},{4,70},{6,72},{8,74},{10,76},{12,78},{14,80},{16,82}... | collective-permute-start | bytes 147464 | tf_op jit(solution)/shard_map/ppermute | solution.py:25
  113.4 3.1 %copy-start.3 = (f32[96,1024]{1,0:T(8,128)S(1)}, f32[96,1024]{1,0:T(8,128)}, u32[]{:S(2)}) copy-start(f32[96,1024]{1,0:T(8,128)} %shard_map.102) | copy-start | bytes 1179652
  119.5 29.8 %all-to-all-start = ((f32[128,1,128]{2,1,0:T(1,128)}), f32[128,1,128]{2,1,0:T(1,128)S(1)}, u32[]{:S(2)}, u32[]{:S(2)}) async-start(f32[128,1,128]{2,1,0:T(1,128)} %bitcast.16), calls=%async_computation | async-start | bytes 131072 | tf_op jit(solution)/shard_map/all_to_all | solution.py:244

commit v2 on v1

--- a/solution.py
+++ b/solution.py
@@ -94,6 +94,112 @@
             flops=2 * steps * width, transcendentals=0, bytes_accessed=8 * steps * width + 4 * width
         ),
     )(retain_row, drive)
+
+
+def forward_kernel(*refs, has_inflow):
+    if has_inflow:
+        coef_ref, product_ref, lateral_ref, out_ref, outlet_ref, inflow_ref = refs
+    else:
+        coef_ref, lateral_ref, out_ref, outlet_ref = refs
+    steps = lateral_ref.shape[0]
+    narrow = outlet_ref.shape[1]
+    gain_now, gain_prev, gain_side = coef_ref[0:1, :], coef_ref[1:2, :], coef_ref[2:3, :]
+    keep, live = coef_ref[3:4, :], coef_ref[4:5, :]
+
+    def advance(hour, carry):
+        state, before = carry
+        side_in = lateral_ref[pl.ds(hour, 1), :]
+        if has_inflow:
+            now = (
+                product_ref[pl.ds(hour, 1), :] + product_ref[pl.ds(hour + steps, 1), :]
+            ) + product_ref[pl.ds(hour + 2 * steps, 1), :]
+            inflow_ref[pl.ds(hour, 1), :] = now
+            drive = (gain_now * now + gain_prev * before) + gain_side * side_in
+        else:
+            now = before
+            drive = gain_side * side_in
+        state = keep * state + drive
+        flow = state * live
+        out_ref[pl.ds(hour, 1), :] = flow
+        outlet_ref[pl.ds(hour, 1), :] = flow[:, :narrow]
+        return state, now
+
+    zero = jnp.zeros_like(keep)
+    lax.fori_loop(0, steps, advance, (zero, zero), unroll=8)
+
+
+def backward_kernel(*refs, has_down, emit):
+    refs = list(refs)
+    coef_ref, cot_ref = refs[0], refs[1]
+    rest = refs[2:]
+    if has_down:
+        down_ref, side_ref = rest[0], rest[1]
+        rest = rest[2:]
+    adj_ref = rest[0]
+    piece_ref = rest[1] if emit else None
+    steps = cot_ref.shape[0]
+    gain_now, gain_prev = coef_ref[0:1, :], coef_ref[1:2, :]
+    keep, live = coef_ref[3:4, :], coef_ref[4:5, :]
+
+    def advance(position, carry):
+        hour = steps - 1 - position
+        state, later = carry
+        load = cot_ref[pl.ds(hour, 1), :]
+        if has_down:
+            down = down_ref[pl.ds(hour, 1), :]
+            side = side_ref[pl.ds(hour, 1), :]
+            narrow = side.shape[1]
+            down = jnp.concatenate([down[:, :narrow] + side, down[:, narrow:]], axis=1)
+            load = load + down
+        state = keep * state + live * load
+        adj_ref[pl.ds(hour, 1), :] = state
+        if emit:
+            remainder = gain_now * state + gain_prev * later
+            for piece_at in range(3):
+                piece = remainder.astype(jnp.bfloat16).astype(jnp.float32)
+                piece_ref[pl.ds(hour + piece_at * steps, 1), :] = piece
+                remainder = remainder - piece
+        return state, state
+
+    zero = jnp.zeros_like(keep)
+    lax.fori_loop(0, steps, advance, (zero, zero), unroll=8)
+
+
+def vmem_call(kernel, outs, *args):
+    steps, width = outs[0]
+    return pl.pallas_call(
+        kernel,
+        out_shape=[jax.ShapeDtypeStruct(shape, jnp.float32) for shape in outs],
+        in_specs=[pl.BlockSpec(memory_space=pltpu.VMEM)] * len(args),
+        out_specs=[pl.BlockSpec(memory_space=pltpu.VMEM)] * len(outs),
+        cost_estimate=pl.CostEstimate(
+            flops=10 * steps * width,
+            transcendentals=0,
+            bytes_accessed=4 * (sum(a.size for a in args) + sum(r * c for r, c in outs)),
+        ),
+    )(*args)
+
+
+def routed(coef, lateral_all, product=None):
+    steps, width = lateral_all.shape
+    narrow = width // 8
+    if product is None:
+        kernel = functools.partial(forward_kernel, has_inflow=False)
+        flow, outlet = vmem_call(kernel, [(steps, width), (steps, narrow)], coef, lateral_all)
+        return flow, outlet, None
+    kernel = functools.partial(forward_kernel, has_inflow=True)
+    return vmem_call(
+        kernel, [(steps, width), (steps, narrow), (steps, width)], coef, product, lateral_all
+    )
+
+
+def adjoined(coef, cotangent_all, down=None, side=None, emit=True):
+    steps, width = cotangent_all.shape
+    kernel = functools.partial(backward_kernel, has_down=down is not None, emit=emit)
+    args = (coef, cotangent_all) if down is None else (coef, cotangent_all, down, side)
+    outs = [(steps, width)] + ([(3 * steps, width)] if emit else [])
+    results = vmem_call(kernel, outs, *args)
+    return results[0], (results[1] if emit else None)
 
 
 def split_three(value):
@@ -166,9 +272,12 @@
     )
     coef_set, coef_pull = jax.vjp(coefficients, raw_params)
     gain_now, gain_prev, retain, gain_side = coef_set
+    zero_row = jnp.zeros((reach_dev,), jnp.float32)
+    coef = jnp.stack(
+        [gain_now, gain_prev, gain_side, retain, live_mask, zero_row, zero_row, zero_row], axis=0
+    )
     lateral_all = whole_window(lateral)
     cotangent_all = whole_window(cotangent)
-    steps_all = lateral_all.shape[0]
     source_ids = lax.broadcasted_iota(jnp.int32, (reach_dev + outlets, reach_dev), 0)
     confluence = jnp.zeros((reach_dev + outlets, reach_dev), jnp.float32)
     for upslot in range(up_count):
@@ -176,50 +285,35 @@
             (source_ids == feeders[upslot][None, :]) & (upslot < feeder_count)[None, :]
         ).astype(jnp.float32)
     confluence = confluence.astype(jnp.bfloat16)
-    retain_row = retain[None, :]
-    zero_flow = jnp.zeros((steps_all, reach_dev), jnp.float32)
-    zero_row = jnp.zeros((1, reach_dev), jnp.float32)
 
     def own_half(value):
         return lax.dynamic_slice_in_dim(value, mine * steps_dev, steps_dev, axis=0)
 
-    def route_level(inflow):
-        inflow_before = jnp.concatenate([zero_row, inflow[:-1]], axis=0)
-        drive = gain_now * inflow + gain_prev * inflow_before + gain_side * lateral_all
-        flow = recurrence(retain_row, drive)
-        return flow * live_mask
-
-    inflow = zero_flow
-    outflow = route_level(inflow)
+    outflow, outlet_flow, inflow = routed(coef, lateral_all)
     for level_step in range(levels - 1):
         upper_flow = whole_window(shifted(own_half(outflow), "level", 1))
-        side_flow = diagonal(outflow[:, :outlets], 1)
+        side_flow = diagonal(outlet_flow, 1)
         source = jnp.concatenate([upper_flow, side_flow], axis=1)
-        inflow = joined_three(
-            jnp.dot(split_three(source), confluence, preferred_element_type=jnp.float32)
+        product = jnp.dot(split_three(source), confluence, preferred_element_type=jnp.float32)
+        outflow, outlet_flow, inflow = routed(coef, lateral_all, product)
+    adjoint, pieces = adjoined(coef, cotangent_all)
+    for level_step in range(1, levels):
+        spread = joined_three(
+            lax.dot_general(
+                pieces.astype(jnp.bfloat16),
+                confluence,
+                (((1,), (1,)), ((), ())),
+                preferred_element_type=jnp.float32,
+            )
         )
-        outflow = route_level(inflow)
-    adjoint_down = zero_flow
-    adjoint = zero_flow
-    for level_step in range(levels):
-        adjoint_load = live_mask * (cotangent_all + adjoint_down)
-        adjoint = recurrence(retain_row, adjoint_load, reverse=True)
-        if level_step + 1 < levels:
-            later_adj = jnp.concatenate([adjoint[1:], zero_row], axis=0)
-            to_inflow = gain_now * adjoint + gain_prev * later_adj
-            spread = joined_three(
-                lax.dot_general(
-                    split_three(to_inflow),
-                    confluence,
-                    (((1,), (1,)), ((), ())),
-                    preferred_element_type=jnp.float32,
-                )
-            )
-            returned = diagonal(spread[:, reach_dev:], -1)
-            own_part = whole_window(shifted(own_half(spread[:, :reach_dev]), "level", -1))
-            adjoint_down = own_part.at[:, :outlets].add(returned)
-    flow_before = jnp.concatenate([zero_row, outflow[:-1]], axis=0)
-    inflow_before = jnp.concatenate([zero_row, inflow[:-1]], axis=0)
+        returned = diagonal(spread[:, reach_dev:], -1)
+        own_part = whole_window(shifted(own_half(spread[:, :reach_dev]), "level", -1))
+        adjoint, pieces = adjoined(
+            coef, cotangent_all, own_part, returned, emit=level_step + 1 < levels
+        )
+    zero_first = jnp.zeros((1, reach_dev), jnp.float32)
+    flow_before = jnp.concatenate([zero_first, outflow[:-1]], axis=0)
+    inflow_before = jnp.concatenate([zero_first, inflow[:-1]], axis=0)
     coef_grads = (
         jnp.sum(adjoint * inflow, axis=0),
         jnp.sum(adjoint * inflow_before, axis=0),

time: 152 us -> 150 us (0.987)
  other arithmetic: 18.5 us -> 2.9 us
  Pallas kernels: 16.4 us -> 26.2 us
  starting transfers between devices: 46.9 us -> 55.1 us
  matrix products: 14.3 us -> 21.9 us
  waiting for transfers between devices: 16.6 us -> 9.92 us
  blocking collectives: 26.5 us -> 22.3 us
    pallas_call x8, Pallas kernels: 16.4 us -> 26.2 us  [vmem_call(): pl.pallas_call(kernel, out_shape=[jax.ShapeDtypeStruct(shape, jnp.float32...]
    mul x5 -> x0, other arithmetic: 7.39 us -> none  [the longest x4 6.37 us: body(): adjoint_load = live_mask * (cotangent_all + adjoint_down)]
    ppermute x6, waiting for transfers between devices: 6.72 us -> 0.02 us  [shifted(): lax.ppermute(value, axis, [(source, source + steps) for source in range(l...]
    all_gather x8, blocking collectives: 26.5 us -> 22.3 us  [whole_window(): return lax.all_gather(value, 'group', axis=0, tiled=True)]
    another operation x10 -> x3, other arithmetic: 4.34 us -> 0.28 us
    ppermute x6, starting transfers between devices: 15.9 us -> 19.9 us  [diagonal(): return lax.ppermute(value, ('level', 'basin'), pairs)]
    dot_general x3, matrix products: 6.26 us -> 10.1 us  [body(): lax.dot_general(pieces.astype(jnp.bfloat16), confluence, (((1,), (1,)), (...]
    dot_general x3, matrix products: 5.98 us -> 9.11 us  [body(): jnp.dot(split_three(source), confluence, preferred_element_type=jnp.float32)]
  transfers between devices with their start and end apart: 13 -> 13, of which waited for: 3 -> 1; matrix products, arithmetic and copies ran while one was open for 3% -> 11% of each run, Pallas kernels for 7% -> 11%
where the time goes in v2:
time: 150 us; the launch traced here: 149 us
  starting transfers between devices  55.1 us (37%)
  Pallas kernels  26.2 us (17%)
  blocking collectives  22.3 us (15%)
  matrix products  21.9 us (15%)
  waiting for transfers between devices  9.92 us (7%)
  local copies, waits for them, and re-layouts  8.81 us (6%)
  other arithmetic  2.9 us (2%)
  between operations  1.87 us (1%)
    pallas_call x8, Pallas kernels, vmem_call(): pl.pallas_call(kernel, out_shape=[jax.ShapeDtypeStruct(shape, jnp.float32...  26.2 us
    all_gather x8, blocking collectives, whole_window(): return lax.all_gather(value, 'group', axis=0, tiled=True)  22.3 us
    all_to_all x1, starting transfers between devices, body(): lax.all_to_all(replicated, ('level', 'basin'), 0, 0, tiled=True)  21 us
    ppermute x6, starting transfers between devices, diagonal(): return lax.ppermute(value, ('level', 'basin'), pairs)  19.9 us
    ppermute x6, starting transfers between devices, shifted(): lax.ppermute(value, axis, [(source, source + steps) for source in range(l...  14.2 us
    dot_general x3, matrix products, body(): lax.dot_general(pieces.astype(jnp.bfloat16), confluence, (((1,), (1,)), (...  10.1 us
    all_to_all x1, waiting for transfers between devices, body(): lax.all_to_all(replicated, ('level', 'basin'), 0, 0, tiled=True)  9.89 us
    dot_general x3, matrix products, body(): jnp.dot(split_three(source), confluence, preferred_element_type=jnp.float32)  9.11 us
  transfers between devices with their start and end apart: 13, of which 1 were waited for; matrix products, arithmetic and copies ran while one was open for 11% of the time, Pallas kernels for 11%

profile of v2, /device:TPU:1, one launch (start us, length us, event | category | flops | bytes accessed | tf_op | source)
XLA Modules:
  0.0 149.1 jit_solution(5875446148006689422)
XLA Ops:
  4.1 5.0 %all_gather.28.refs_1_ = f32[96,1024]{1,0:T(8,128)} all-gather(f32[48,1024]{1,0:T(8,128)S(1)} %copy-done.4), channel_id=1, replica_groups=mesh['level'=4,'basin'=32,'group'=2] {'group'}, dimensions={0}, use_global_device_ids=true | all-gather | bytes 589824 | tf_op jit(solution)/shard_map/all_gather | solution.py:55
  9.9 4.0 %shard_map.99 = (f32[96,1024]{1,0:T(8,128)}, f32[288,1024]{1,0:T(8,128)}) custom-call(f32[8,1024]{1,0:T(8,128)} %stack.5.refs_0_, f32[96,1024]{1,0:T(8,128)} %all_gather.28.refs_1_), custom_call_target="tpu_custom_call" | custom-call | flops 983040 | bytes 1998848 | tf_op jit(solution)/shard_map/pallas_call | solution.py:170
  13.9 3.4 %fusion.5 = f32[288,1152]{1,0:T(8,128)S(1)} fusion(s32[1024]{0:T(1024)S(1)} %bitcast.43, s32[1024]{0:T(1024)S(1)} %bitcast.37, pred[1024]{0:T(1024)(128)(4,1)S(1)} %get-tuple-element.57, pred[1024]{0:T(1024)(128)(4,1)S(1)} %get-tuple-element.56, f32[288,1024]{1,0:T(8,128)} %get-tuple-element.20), kind=kOutput, calls=%fused_computation.9 | convolution fusion | flops 689209344 | bytes 2516992 | tf_op jit(solution)/shard_map/dot_general | solution.py:302
  25.3 4.3 %collective-permute-start = (f32[48,1024]{1,0:T(8,128)S(1)}, f32[48,1024]{1,0:T(8,128)S(1)}, u32[]{:S(2)}, u32[]{:S(2)}) collective-permute-start(f32[48,1024]{1,0:T(8,128)S(1)} %constant_dynamic-slice_fusion.6), channel_id=1, source_target_pairs={{0,64},{64,128},{128,192},{1,65},{65,129},{129,193},{2,66},{66,130... | collective-permute-start | bytes 589832 | tf_op jit(solution)/shard_map/ppermute | solution.py:16
  29.5 5.2 %collective-permute-start.1 = (f32[96,128]{1,0:T(8,128)}, f32[96,128]{1,0:T(8,128)S(1)}, u32[]{:S(2)}, u32[]{:S(2)}) collective-permute-start(f32[96,128]{1,0:T(8,128)} %get-tuple-element.14), channel_id=1, source_target_pairs={{0,66},{2,68},{4,70},{6,72},{8,74},{10,76},{12,78},{14,80},{16,82}... | collective-permute-start | bytes 147464 | tf_op jit(solution)/shard_map/ppermute | solution.py:25
  34.7 2.8 %all_gather.29.refs_2_ = f32[96,1024]{1,0:T(8,128)} all-gather(f32[48,1024]{1,0:T(8,128)S(1)} %collective-permute-done.6), channel_id=1, replica_groups=mesh['level'=4,'basin'=32,'group'=2] {'group'}, dimensions={0}, use_global_device_ids=true | all-gather | bytes 589824 | tf_op jit(solution)/shard_map/all_gather | solution.py:55
  38.1 4.5 %shard_map.100 = (f32[96,1024]{1,0:T(8,128)}, f32[288,1024]{1,0:T(8,128)}) custom-call(f32[8,1024]{1,0:T(8,128)} %stack.5.refs_0_, f32[96,1024]{1,0:T(8,128)} %all_gather.28.refs_1_, f32[96,1024]{1,0:T(8,128)} %all_gather.29.refs_2_, f32[96,128]{1,0:T(8,128)} %copy-done.8), custom_call_target="tpu_custom_call" | custom-call | flops 983040 | bytes 2441216 | tf_op jit(solution)/shard_map/pallas_call | solution.py:170
  42.6 3.4 %fusion.4 = f32[288,1152]{1,0:T(8,128)S(1)} fusion(s32[1024]{0:T(1024)S(1)} %bitcast.44, s32[1024]{0:T(1024)S(1)} %bitcast.38, pred[1024]{0:T(1024)(128)(4,1)S(1)} %get-tuple-element.57, pred[1024]{0:T(1024)(128)(4,1)S(1)} %get-tuple-element.56, f32[288,1024]{1,0:T(8,128)} %get-tuple-element.21), kind=kOutput, calls=%fused_computation.8 | convolution fusion | flops 689209344 | bytes 2516992 | tf_op jit(solution)/shard_map/dot_general | solution.py:302
  51.0 3.0 %fusion.8.refs_1_ = f32[288,1024]{1,0:T(8,128)} fusion(s32[1024]{0:T(1024)S(1)} %bitcast.45, s32[1024]{0:T(1024)S(1)} %bitcast.39, pred[1024]{0:T(1024)(128)(4,1)S(1)} %get-tuple-element.57, pred[1024]{0:T(1024)(128)(4,1)S(1)} %get-tuple-element.56, bf16[96,1152]{1,0:T(8,128)(2,1)S(1)} %get-tuple-element.50, bf16[96,1152]{1,0:T(8,128)(2,1)S(1)} %get-tuple-element.51, ...), kind=kOutput, calls=%fused_computation.12 | convolution fusion | flops 690905088 | bytes 1853440 | tf_op jit(solution)/shard_map/dot_general | solution.py:297
  54.0 2.9 %shard_map.96 = (f32[96,1024]{1,0:T(8,128)}, f32[96,128]{1,0:T(8,128)}, f32[96,1024]{1,0:T(8,128)}) custom-call(f32[8,1024]{1,0:T(8,128)} %stack.5.refs_0_, f32[288,1024]{1,0:T(8,128)} %fusion.8.refs_1_, f32[96,1024]{1,0:T(8,128)} %all_gather.24.refs_1_.refs_2_), custom_call_target="tpu_custom_call" | custom-call | flops 983040 | bytes 2441216 | tf_op jit(solution)/shard_map/pallas_call | solution.py:170
  57.8 4.3 %collective-permute-start.2 = (f32[48,1024]{1,0:T(8,128)S(1)}, f32[48,1024]{1,0:T(8,128)S(1)}, u32[]{:S(2)}, u32[]{:S(2)}) collective-permute-start(f32[48,1024]{1,0:T(8,128)S(1)} %constant_dynamic-slice_fusion.5), channel_id=1, source_target_pairs={{0,64},{64,128},{128,192},{1,65},{65,129},{129,193},{2,66},{66,130... | collective-permute-start | bytes 589832 | tf_op jit(solution)/shard_map/ppermute | solution.py:16
  62.1 5.2 %collective-permute-start.3 = (f32[96,128]{1,0:T(8,128)}, f32[96,128]{1,0:T(8,128)S(1)}, u32[]{:S(2)}, u32[]{:S(2)}) collective-permute-start(f32[96,128]{1,0:T(8,128)} %get-tuple-element.16), channel_id=1, source_target_pairs={{0,66},{2,68},{4,70},{6,72},{8,74},{10,76},{12,78},{14,80},{16,82}... | collective-permute-start | bytes 147464 | tf_op jit(solution)/shard_map/ppermute | solution.py:25
  67.3 2.8 %all_gather.30.refs_2_ = f32[96,1024]{1,0:T(8,128)} all-gather(f32[48,1024]{1,0:T(8,128)S(1)} %collective-permute-done.8), channel_id=1, replica_groups=mesh['level'=4,'basin'=32,'group'=2] {'group'}, dimensions={0}, use_global_device_ids=true | all-gather | bytes 589824 | tf_op jit(solution)/shard_map/all_gather | solution.py:55
  70.7 4.5 %shard_map.101 = (f32[96,1024]{1,0:T(8,128)}, f32[288,1024]{1,0:T(8,128)}) custom-call(f32[8,1024]{1,0:T(8,128)} %stack.5.refs_0_, f32[96,1024]{1,0:T(8,128)} %all_gather.28.refs_1_, f32[96,1024]{1,0:T(8,128)} %all_gather.30.refs_2_, f32[96,128]{1,0:T(8,128)} %copy-done.7), custom_call_target="tpu_custom_call" | custom-call | flops 983040 | bytes 2441216 | tf_op jit(solution)/shard_map/pallas_call | solution.py:170
  75.2 3.4 %fusion.3 = f32[288,1152]{1,0:T(8,128)S(1)} fusion(s32[1024]{0:T(1024)S(1)} %bitcast.46, s32[1024]{0:T(1024)S(1)} %bitcast.40, pred[1024]{0:T(1024)(128)(4,1)S(1)} %get-tuple-element.57, pred[1024]{0:T(1024)(128)(4,1)S(1)} %get-tuple-element.56, f32[288,1024]{1,0:T(8,128)} %get-tuple-element.22), kind=kOutput, calls=%fused_computation.7 | convolution fusion | flops 689209344 | bytes 2516992 | tf_op jit(solution)/shard_map/dot_general | solution.py:302
  81.0 3.0 %fusion.7.refs_1_ = f32[288,1024]{1,0:T(8,128)} fusion(s32[1024]{0:T(1024)S(1)} %bitcast.47, s32[1024]{0:T(1024)S(1)} %bitcast.41, pred[1024]{0:T(1024)(128)(4,1)S(1)} %get-tuple-element.57, pred[1024]{0:T(1024)(128)(4,1)S(1)} %get-tuple-element.56, bf16[96,1152]{1,0:T(8,128)(2,1)S(1)} %get-tuple-element.47, bf16[96,1152]{1,0:T(8,128)(2,1)S(1)} %get-tuple-element.48, ...), kind=kOutput, calls=%fused_computation.11 | convolution fusion | flops 690905088 | bytes 1853440 | tf_op jit(solution)/shard_map/dot_general | solution.py:297
  84.0 2.9 %shard_map.97 = (f32[96,1024]{1,0:T(8,128)}, f32[96,128]{1,0:T(8,128)}, f32[96,1024]{1,0:T(8,128)}) custom-call(f32[8,1024]{1,0:T(8,128)} %stack.5.refs_0_, f32[288,1024]{1,0:T(8,128)} %fusion.7.refs_1_, f32[96,1024]{1,0:T(8,128)} %all_gather.24.refs_1_.refs_2_), custom_call_target="tpu_custom_call" | custom-call | flops 983040 | bytes 2441216 | tf_op jit(solution)/shard_map/pallas_call | solution.py:170
  92.4 5.7 %collective-permute-start.5 = (f32[96,128]{1,0:T(8,128)S(1)}, f32[96,128]{1,0:T(8,128)S(1)}, u32[]{:S(2)}, u32[]{:S(2)}) collective-permute-start(f32[96,128]{1,0:T(8,128)S(1)} %copy-done.11), channel_id=1, source_target_pairs={{0,66},{2,68},{4,70},{6,72},{8,74},{10,76},{12,78},{14,80},{16,82}... | collective-permute-start | bytes 147464 | tf_op jit(solution)/shard_map/ppermute | solution.py:25
  98.2 2.9 %all_gather.27 = f32[96,1024]{1,0:T(8,128)S(1)} all-gather(f32[48,1024]{1,0:T(8,128)S(1)} %collective-permute-done.4), channel_id=1, replica_groups=mesh['level'=4,'basin'=32,'group'=2] {'group'}, dimensions={0}, use_global_device_ids=true | all-gather | bytes 589824 | tf_op jit(solution)/shard_map/all_gather | solution.py:55
  101.3 3.0 %fusion.6.refs_1_ = f32[288,1024]{1,0:T(8,128)} fusion(s32[1024]{0:T(1024)S(1)} %bitcast.48, s32[1024]{0:T(1024)S(1)} %bitcast.42, pred[1024]{0:T(1024)(128)(4,1)S(1)} %get-tuple-element.57, pred[1024]{0:T(1024)(128)(4,1)S(1)} %get-tuple-element.56, bf16[96,1152]{1,0:T(8,128)(2,1)S(1)} %get-tuple-element.44, bf16[96,1152]{1,0:T(8,128)(2,1)S(1)} %get-tuple-element.45, ...), kind=kOutput, calls=%fused_computation.10 | convolution fusion | flops 690905088 | bytes 1853440 | tf_op jit(solution)/shard_map/dot_general | solution.py:297
  106.5 3.0 %shard_map.98 = (f32[96,1024]{1,0:T(8,128)}, f32[96,128]{1,0:T(8,128)}, f32[96,1024]{1,0:T(8,128)}) custom-call(f32[8,1024]{1,0:T(8,128)} %stack.5.refs_0_, f32[288,1024]{1,0:T(8,128)} %fusion.6.refs_1_, f32[96,1024]{1,0:T(8,128)} %all_gather.24.refs_1_.refs_2_), custom_call_target="tpu_custom_call" | custom-call | flops 983040 | bytes 2441216 | tf_op jit(solution)/shard_map/pallas_call | solution.py:170
  110.1 2.5 %shard_map.102 = f32[96,1024]{1,0:T(8,128)} custom-call(f32[8,1024]{1,0:T(8,128)} %stack.5.refs_0_, f32[96,1024]{1,0:T(8,128)} %all_gather.28.refs_1_, f32[96,1024]{1,0:T(8,128)} %all_gather.31.refs_2_, f32[96,128]{1,0:T(8,128)} %copy-done.6), custom_call_target="tpu_custom_call" | custom-call | flops 983040 | bytes 1261568 | tf_op jit(solution)/shard_map/pallas_call | solution.py:170
  116.5 21.0 %all-to-all-start = ((f32[128,1,128]{2,1,0:T(1,128)}), f32[128,1,128]{2,1,0:T(1,128)S(1)}, u32[]{:S(2)}, u32[]{:S(2)}) async-start(f32[128,1,128]{2,1,0:T(1,128)} %bitcast.13), calls=%async_computation | async-start | bytes 131072 | tf_op jit(solution)/shard_map/all_to_all | solution.py:338
  138.2 9.9 %all-to-all-done = f32[128,1,128]{2,1,0:T(1,128)S(1)} async-done(((f32[128,1,128]{2,1,0:T(1,128)}), f32[128,1,128]{2,1,0:T(1,128)S(1)}, u32[]{:S(2)}, u32[]{:S(2)}) %all-to-all-start) | async-done | bytes 65568 | tf_op jit(solution)/shard_map/all_to_all | solution.py:338
  (95 shorter events, 34.8 us)
Async XLA Ops:
  0.6 0.9 copy-start
  0.6 3.5 %copy-start.4 = (f32[48,1024]{1,0:T(8,128)S(1)}, f32[48,1024]{1,0:T(8,128)}, u32[]{:S(2)}) copy-start(f32[48,1024]{1,0:T(8,128)} %param.9) | copy-start | bytes 589828
  0.7 8.5 %copy-start.9 = (s32[2,1024]{1,0:T(2,128)S(1)}, s32[2,1024]{1,0:T(2,128)}, u32[]{:S(2)}) copy-start(s32[2,1024]{1,0:T(2,128)} %param.12) | copy-start | bytes 24580
  0.7 8.5 %copy-start.10 = (s32[1024]{0:T(1024)S(1)}, s32[1024]{0:T(1024)}, u32[]{:S(2)}) copy-start(s32[1024]{0:T(1024)} %param.13) | copy-start | bytes 12292
  17.3 2.8 %copy-start.5 = (f32[48,1024]{1,0:T(8,128)S(1)}, f32[48,1024]{1,0:T(8,128)}, u32[]{:S(2)}) copy-start(f32[48,1024]{1,0:T(8,128)} %param.8) | copy-start | bytes 589828
  17.4 17.3 %collective-permute-start.6 = (f32[48,1024]{1,0:T(8,128)S(1)}, f32[48,1024]{1,0:T(8,128)S(1)}, u32[]{:S(2)}, u32[]{:S(2)}) collective-permute-start(f32[48,1024]{1,0:T(8,128)S(1)} %constant_dynamic-slice_fusion.2), channel_id=1, source_target_pairs={{64,0},{128,64},{192,128},{65,1},{129,65},{193,129},{66,2},{130,66... | collective-permute-start | bytes 589832 | tf_op jit(solution)/shard_map/ppermute | solution.py:16
  18.7 18.8 %collective-permute-start.7 = (f32[96,128]{1,0:T(8,128)S(1)}, f32[96,128]{1,0:T(8,128)S(1)}, u32[]{:S(2)}, u32[]{:S(2)}) collective-permute-start(f32[96,128]{1,0:T(8,128)S(1)} %slice.90), channel_id=1, source_target_pairs={{66,0},{68,2},{70,4},{72,6},{74,8},{76,10},{78,12},{80,14},{82,16}... | collective-permute-start | bytes 147464 | tf_op jit(solution)/shard_map/ppermute | solution.py:25
  25.3 23.4 %collective-permute-start = (f32[48,1024]{1,0:T(8,128)S(1)}, f32[48,1024]{1,0:T(8,128)S(1)}, u32[]{:S(2)}, u32[]{:S(2)}) collective-permute-start(f32[48,1024]{1,0:T(8,128)S(1)} %constant_dynamic-slice_fusion.6), channel_id=1, source_target_pairs={{0,64},{64,128},{128,192},{1,65},{65,129},{129,193},{2,66},{66,130... | collective-permute-start | bytes 589832 | tf_op jit(solution)/shard_map/ppermute | solution.py:16
  29.5 21.3 %collective-permute-start.1 = (f32[96,128]{1,0:T(8,128)}, f32[96,128]{1,0:T(8,128)S(1)}, u32[]{:S(2)}, u32[]{:S(2)}) collective-permute-start(f32[96,128]{1,0:T(8,128)} %get-tuple-element.14), channel_id=1, source_target_pairs={{0,66},{2,68},{4,70},{6,72},{8,74},{10,76},{12,78},{14,80},{16,82}... | collective-permute-start | bytes 147464 | tf_op jit(solution)/shard_map/ppermute | solution.py:25
  37.5 0.6 copy-start.8
  46.1 21.2 %collective-permute-start.8 = (f32[48,1024]{1,0:T(8,128)S(1)}, f32[48,1024]{1,0:T(8,128)S(1)}, u32[]{:S(2)}, u32[]{:S(2)}) collective-permute-start(f32[48,1024]{1,0:T(8,128)S(1)} %constant_dynamic-slice_fusion.1), channel_id=1, source_target_pairs={{64,0},{128,64},{192,128},{65,1},{129,65},{193,129},{66,2},{130,66... | collective-permute-start | bytes 589832 | tf_op jit(solution)/shard_map/ppermute | solution.py:16
  47.4 22.7 %collective-permute-start.9 = (f32[96,128]{1,0:T(8,128)S(1)}, f32[96,128]{1,0:T(8,128)S(1)}, u32[]{:S(2)}, u32[]{:S(2)}) collective-permute-start(f32[96,128]{1,0:T(8,128)S(1)} %slice.95), channel_id=1, source_target_pairs={{66,0},{68,2},{70,4},{72,6},{74,8},{76,10},{78,12},{80,14},{82,16}... | collective-permute-start | bytes 147464 | tf_op jit(solution)/shard_map/ppermute | solution.py:25
  57.8 20.7 %collective-permute-start.2 = (f32[48,1024]{1,0:T(8,128)S(1)}, f32[48,1024]{1,0:T(8,128)S(1)}, u32[]{:S(2)}, u32[]{:S(2)}) collective-permute-start(f32[48,1024]{1,0:T(8,128)S(1)} %constant_dynamic-slice_fusion.5), channel_id=1, source_target_pairs={{0,64},{64,128},{128,192},{1,65},{65,129},{129,193},{2,66},{66,130... | collective-permute-start | bytes 589832 | tf_op jit(solution)/shard_map/ppermute | solution.py:16
  62.1 18.7 %collective-permute-start.3 = (f32[96,128]{1,0:T(8,128)}, f32[96,128]{1,0:T(8,128)S(1)}, u32[]{:S(2)}, u32[]{:S(2)}) collective-permute-start(f32[96,128]{1,0:T(8,128)} %get-tuple-element.16), channel_id=1, source_target_pairs={{0,66},{2,68},{4,70},{6,72},{8,74},{10,76},{12,78},{14,80},{16,82}... | collective-permute-start | bytes 147464 | tf_op jit(solution)/shard_map/ppermute | solution.py:25
  87.9 4.6 %copy-start.11 = (f32[96,128]{1,0:T(8,128)S(1)}, f32[96,128]{1,0:T(8,128)}, u32[]{:S(2)}) copy-start(f32[96,128]{1,0:T(8,128)} %get-tuple-element.18) | copy-start | bytes 147460
  87.9 10.3 %collective-permute-start.4 = (f32[48,1024]{1,0:T(8,128)S(1)}, f32[48,1024]{1,0:T(8,128)S(1)}, u32[]{:S(2)}, u32[]{:S(2)}) collective-permute-start(f32[48,1024]{1,0:T(8,128)S(1)} %constant_dynamic-slice_fusion.4), channel_id=1, source_target_pairs={{0,64},{64,128},{128,192},{1,65},{65,129},{129,193},{2,66},{66,130... | collective-permute-start | bytes 589832 | tf_op jit(solution)/shard_map/ppermute | solution.py:16
  89.8 14.5 %collective-permute-start.10 = (f32[48,1024]{1,0:T(8,128)S(1)}, f32[48,1024]{1,0:T(8,128)S(1)}, u32[]{:S(2)}, u32[]{:S(2)}) collective-permute-start(f32[48,1024]{1,0:T(8,128)S(1)} %constant_dynamic-slice_fusion), channel_id=1, source_target_pairs={{64,0},{128,64},{192,128},{65,1},{129,65},{193,129},{66,2},{130,66... | collective-permute-start | bytes 589832 | tf_op jit(solution)/shard_map/ppermute | solution.py:16
  91.1 18.4 %collective-permute-start.11 = (f32[96,128]{1,0:T(8,128)S(1)}, f32[96,128]{1,0:T(8,128)S(1)}, u32[]{:S(2)}, u32[]{:S(2)}) collective-permute-start(f32[96,128]{1,0:T(8,128)S(1)} %slice.100), channel_id=1, source_target_pairs={{66,0},{68,2},{70,4},{72,6},{74,8},{76,10},{78,12},{80,14},{82,16}... | collective-permute-start | bytes 147464 | tf_op jit(solution)/shard_map/ppermute | solution.py:25
  92.4 8.7 %collective-permute-start.5 = (f32[96,128]{1,0:T(8,128)S(1)}, f32[96,128]{1,0:T(8,128)S(1)}, u32[]{:S(2)}, u32[]{:S(2)}) collective-permute-start(f32[96,128]{1,0:T(8,128)S(1)} %copy-done.11), channel_id=1, source_target_pairs={{0,66},{2,68},{4,70},{6,72},{8,74},{10,76},{12,78},{14,80},{16,82}... | collective-permute-start | bytes 147464 | tf_op jit(solution)/shard_map/ppermute | solution.py:25
  106.5 6.1 %copy-start.1 = (f32[96,1024]{1,0:T(8,128)S(1)}, f32[96,1024]{1,0:T(8,128)}, u32[]{:S(2)}) copy-start(f32[96,1024]{1,0:T(8,128)} %all_gather.24.refs_1_.refs_2_) | copy-start | bytes 1179652
  109.5 3.1 %copy-start.2 = (f32[96,1024]{1,0:T(8,128)S(1)}, f32[96,1024]{1,0:T(8,128)}, u32[]{:S(2)}) copy-start(f32[96,1024]{1,0:T(8,128)} %get-tuple-element.23) | copy-start | bytes 1179652
  109.5 3.1 %copy-start.3 = (f32[96,1024]{1,0:T(8,128)S(1)}, f32[96,1024]{1,0:T(8,128)}, u32[]{:S(2)}) copy-start(f32[96,1024]{1,0:T(8,128)} %get-tuple-element.19) | copy-start | bytes 1179652
  109.5 0.6 copy-start.6
  116.5 31.6 %all-to-all-start = ((f32[128,1,128]{2,1,0:T(1,128)}), f32[128,1,128]{2,1,0:T(1,128)S(1)}, u32[]{:S(2)}, u32[]{:S(2)}) async-start(f32[128,1,128]{2,1,0:T(1,128)} %bitcast.13), calls=%async_computation | async-start | bytes 131072 | tf_op jit(solution)/shard_map/all_to_all | solution.py:338
  (1 other events, 0.6 us)

commit v3 on v2

--- a/solution.py
+++ b/solution.py
@@ -246,6 +246,31 @@
     return stack_affine(affine_join(split_affine(earlier), split_affine(latter)))
 
 
+def linear_pairs(steps_up, steps_side, core):
+    levels, basins, groups = (
+        lax.axis_size("level"),
+        lax.axis_size("basin"),
+        lax.axis_size("group"),
+    )
+    pairs = []
+    for level in range(levels):
+        for basin in range(basins):
+            target_level, target_basin = level + steps_up, basin + steps_side
+            if 0 <= target_level < levels and 0 <= target_basin < basins:
+                pairs.append(
+                    (
+                        (level * basins + basin) * groups + core,
+                        (target_level * basins + target_basin) * groups + core,
+                    )
+                )
+    return pairs
+
+
+def both_ways(value, side_steps):
+    pairs = linear_pairs(1, side_steps, 0) + linear_pairs(-1, -side_steps, 1)
+    return lax.ppermute(value, ("level", "basin", "group"), pairs)
+
+
 def body(lateral, cotangent, attributes, region, feeders, feeder_count, live_blocks, net_weight):
     steps_dev, reach_dev = lateral.shape
     outlets = reach_dev // 8
@@ -278,6 +303,7 @@
     )
     lateral_all = whole_window(lateral)
     cotangent_all = whole_window(cotangent)
+    steps_all = lateral_all.shape[0]
     source_ids = lax.broadcasted_iota(jnp.int32, (reach_dev + outlets, reach_dev), 0)
     confluence = jnp.zeros((reach_dev + outlets, reach_dev), jnp.float32)
     for upslot in range(up_count):
@@ -285,19 +311,9 @@
             (source_ids == feeders[upslot][None, :]) & (upslot < feeder_count)[None, :]
         ).astype(jnp.float32)
     confluence = confluence.astype(jnp.bfloat16)
-
-    def own_half(value):
-        return lax.dynamic_slice_in_dim(value, mine * steps_dev, steps_dev, axis=0)
-
-    outflow, outlet_flow, inflow = routed(coef, lateral_all)
-    for level_step in range(levels - 1):
-        upper_flow = whole_window(shifted(own_half(outflow), "level", 1))
-        side_flow = diagonal(outlet_flow, 1)
-        source = jnp.concatenate([upper_flow, side_flow], axis=1)
-        product = jnp.dot(split_three(source), confluence, preferred_element_type=jnp.float32)
-        outflow, outlet_flow, inflow = routed(coef, lateral_all, product)
-    adjoint, pieces = adjoined(coef, cotangent_all)
-    for level_step in range(1, levels):
+    zero_flow = jnp.zeros((steps_all, reach_dev), jnp.float32)
+
+    def spread_of(pieces):
         spread = joined_three(
             lax.dot_general(
                 pieces.astype(jnp.bfloat16),
@@ -306,11 +322,48 @@
                 preferred_element_type=jnp.float32,
             )
         )
-        returned = diagonal(spread[:, reach_dev:], -1)
-        own_part = whole_window(shifted(own_half(spread[:, :reach_dev]), "level", -1))
-        adjoint, pieces = adjoined(
-            coef, cotangent_all, own_part, returned, emit=level_step + 1 < levels
+        return spread[:, :reach_dev], spread[:, reach_dev:]
+
+    def forward_first(operands):
+        flow, outlet, unused = routed(coef, lateral_all)
+        return flow, outlet, jnp.stack([flow, zero_flow], axis=0)
+
+    def backward_first(operands):
+        adjoint, pieces = adjoined(coef, cotangent_all)
+        own, side = spread_of(pieces)
+        return own, side, jnp.stack([adjoint, zero_flow], axis=0)
+
+    def forward_step(operands):
+        upper, side = operands
+        source = jnp.concatenate([upper, side], axis=1)
+        product = jnp.dot(split_three(source), confluence, preferred_element_type=jnp.float32)
+        flow, outlet, inflow = routed(coef, lateral_all, product)
+        return flow, outlet, jnp.stack([flow, inflow], axis=0)
+
+    def backward_step(operands):
+        upper, side = operands
+        adjoint, pieces = adjoined(coef, cotangent_all, upper, side)
+        own, side = spread_of(pieces)
+        return own, side, jnp.stack([adjoint, zero_flow], axis=0)
+
+    def backward_last(operands):
+        upper, side = operands
+        adjoint, unused = adjoined(coef, cotangent_all, upper, side, emit=False)
+        return zero_flow, side, jnp.stack([adjoint, zero_flow], axis=0)
+
+    message, outlet_message, kept = lax.cond(mine == 0, forward_first, backward_first, None)
+    for level_step in range(1, levels):
+        upper = both_ways(message, 0)
+        side = both_ways(outlet_message, 1)
+        later = backward_step if level_step + 1 < levels else backward_last
+        message, outlet_message, kept = lax.cond(
+            mine == 0, forward_step, later, (upper, side)
         )
+    other = lax.ppermute(kept, "group", [(0, 1), (1, 0)])
+    forward_kept = jnp.where(mine == 0, kept, other)
+    backward_kept = jnp.where(mine == 0, other, kept)
+    outflow, inflow = forward_kept[0], forward_kept[1]
+    adjoint = backward_kept[0]
     zero_first = jnp.zeros((1, reach_dev), jnp.float32)
     flow_before = jnp.concatenate([zero_first, outflow[:-1]], axis=0)
     inflow_before = jnp.concatenate([zero_first, inflow[:-1]], axis=0)
@@ -337,7 +390,8 @@
     grad_net = jnp.sum(
         lax.all_to_all(replicated, ("level", "basin"), 0, 0, tiled=True), axis=0
     ).reshape(owned_rows, attr_count, param_count)
-    return (own_half(outflow), grad_net)
+    own_hours = lax.dynamic_slice_in_dim(outflow, mine * steps_dev, steps_dev, axis=0)
+    return (own_hours, grad_net)
 
 
 def solution(mesh):

time: 150 us -> 102 us (0.68)
  starting transfers between devices: 55.1 us -> 22.3 us
  waiting for transfers between devices: 9.92 us -> 31.7 us
  blocking collectives: 22.3 us -> 7.41 us
  matrix products: 21.9 us -> 8.68 us
  Pallas kernels: 26.2 us -> 14.1 us
  other arithmetic: 2.9 us -> 5.01 us
    ppermute x12 -> x7, starting transfers between devices: 34.1 us -> 7.99 us  [the longest x6 7.72 us: both_ways(): return lax.ppermute(value, ('level', 'basin', 'group'), pairs)]
    ppermute x12 -> x7, waiting for transfers between devices: 0.03 us -> 21.9 us  [the longest x6 20.2 us: both_ways(): return lax.ppermute(value, ('level', 'basin', 'group'), pairs)]
    all_gather x8 -> x2, blocking collectives: 22.3 us -> 7.41 us  [whole_window(): return lax.all_gather(value, 'group', axis=0, tiled=True)]
    dot_general x6 -> x3, matrix products: 19.2 us -> 6.69 us  [spread_of(): lax.dot_general(pieces.astype(jnp.bfloat16), confluence, (((1,), (1,)), (...]
    pallas_call x8 -> x4, Pallas kernels: 26.2 us -> 14.1 us  [vmem_call(): pl.pallas_call(kernel, out_shape=[jax.ShapeDtypeStruct(shape, jnp.float32...]
    all_to_all x1, starting transfers between devices: 21 us -> 14.3 us  [body(): lax.all_to_all(replicated, ('level', 'basin'), 0, 0, tiled=True)]
    dynamic_slice x7 -> x1, local copies, waits for them, and re-layouts: 3.58 us -> 0.7 us  [body(): lax.dynamic_slice_in_dim(outflow, mine * steps_dev, steps_dev, axis=0)]
    slice x6 -> x8, local copies, waits for them, and re-layouts: 0.1 us -> 2.51 us  [the longest x6 2.42 us: spread_of(): return (spread[:, :reach_dev], spread[:, reach_dev:])]
  transfers between devices with their start and end apart: 13 -> 8, of which waited for: 1 -> 8; matrix products, arithmetic and copies ran while one was open for 11% -> 1% of each run, Pallas kernels for 11% -> 0%
where the time goes in v3:
time: 102 us; the launch traced here: 101 us
  waiting for transfers between devices  31.7 us (31%)
  starting transfers between devices  22.3 us (22%)
  Pallas kernels  14.1 us (14%)
  local copies, waits for them, and re-layouts  10 us (10%)
  matrix products  8.68 us (9%)
  blocking collectives  7.41 us (7%)
  other arithmetic  5.01 us (5%)
  between operations  1.56 us (2%)
    ppermute x6, waiting for transfers between devices, both_ways(): return lax.ppermute(value, ('level', 'basin', 'group'), pairs)  20.2 us
    all_to_all x1, starting transfers between devices, body(): lax.all_to_all(replicated, ('level', 'basin'), 0, 0, tiled=True)  14.3 us
    pallas_call x4, Pallas kernels, vmem_call(): pl.pallas_call(kernel, out_shape=[jax.ShapeDtypeStruct(shape, jnp.float32...  14.1 us
    all_to_all x1, waiting for transfers between devices, body(): lax.all_to_all(replicated, ('level', 'basin'), 0, 0, tiled=True)  9.85 us
    ppermute x6, starting transfers between devices, both_ways(): return lax.ppermute(value, ('level', 'basin', 'group'), pairs)  7.72 us
    all_gather x2, blocking collectives, whole_window(): return lax.all_gather(value, 'group', axis=0, tiled=True)  7.41 us
    dot_general x3, matrix products, spread_of(): lax.dot_general(pieces.astype(jnp.bfloat16), confluence, (((1,), (1,)), (...  6.69 us
    slice x6, local copies, waits for them, and re-layouts, spread_of(): return (spread[:, :reach_dev], spread[:, reach_dev:])  2.42 us
  transfers between devices with their start and end apart: 8, of which 8 were waited for; matrix products, arithmetic and copies ran while one was open for 1% of the time, Pallas kernels for 0%

profile of v3, /device:TPU:1, one launch (start us, length us, event | category | flops | bytes accessed | tf_op | source)
XLA Modules:
  0.0 100.9 jit_solution(11941726379899978612)
XLA Ops:
  2.8 5.1 %all_gather.7 = f32[96,1024]{1,0:T(8,128)S(1)} all-gather(f32[48,1024]{1,0:T(8,128)} %param.16), channel_id=1, replica_groups=mesh['level'=4,'basin'=32,'group'=2] {'group'}, dimensions={0}, use_global_device_ids=true | all-gather | bytes 589824 | tf_op jit(solution)/shard_map/all_gather | solution.py:55
  8.0 2.3 %all_gather.6 = f32[96,1024]{1,0:T(8,128)S(1)} all-gather(f32[48,1024]{1,0:T(8,128)} %param.17), channel_id=1, replica_groups=mesh['level'=4,'basin'=32,'group'=2] {'group'}, dimensions={0}, use_global_device_ids=true | all-gather | bytes 589824 | tf_op jit(solution)/shard_map/all_gather | solution.py:55
  10.2 1.5 %fusion.40 = (f32[128,1024]{1,0:T(8,128)}, f32[1024,128]{0,1:T(8,128)S(1)}) fusion(s32[1024]{0:T(1024)} %param.19), kind=kLoop, calls=%fused_computation.71 | loop fusion | flops 393216 | bytes 1052672 | tf_op jit(solution)/shard_map/convert_element_type | solution.py:285
  13.0 1.9 %add_convert_fusion = bf16[1152,1024]{1,0:T(8,128)(2,1)S(1)} fusion(s32[1024]{0:T(1024)S(1)} %bitcast.55, s32[1024]{0:T(1024)S(1)} %bitcast.54, pred[1024]{0:T(1024)(128)(4,1)S(1)} %get-tuple-element.163, pred[1024]{0:T(1024)(128)(4,1)S(1)} %get-tuple-element.162), kind=kLoop, calls=%fused_computation.58 | loop fusion | flops 9437184 | bytes 2369536 | tf_op jit(solution)/shard_map/convert_element_type | solution.py:313
  14.9 6.1 %conditional.4 = ((f32[96,1024]{1,0:T(8,128)}, f32[96,128]{1,0:T(8,128)S(1)})) conditional(s32[]{:T(128)} %convert_element_type.44, (f32[8,1024]{1,0:T(8,128)S(1)}, f32[96,1024]{1,0:T(8,128)S(1)}, bf16[1152,1024]{1,0:T(8,128)(2,1)S(1)}) %tuple.37, (f32[8,1024]{1,0:T(8,128)S(1)}, f32[96,1024]{1,0:T(8,128)S(1)}) %tuple.38), branch_computations={%region_0.0_spmd, %region_1.0_spmd} | conditional | flops 680976384 | bytes 9519128 | solution.py:354
  14.9 3.0 %branch_0_fun.4 = (f32[96,1024]{1,0:T(8,128)}, f32[288,1024]{1,0:T(8,128)}) custom-call(f32[8,1024]{1,0:T(8,128)S(1)} %get-tuple-element.62.refs_0_, f32[96,1024]{1,0:T(8,128)S(1)} %get-tuple-element.72.refs_1_), custom_call_target="tpu_custom_call" | custom-call | flops 983040 | bytes 1998848 | tf_op jit(solution)/shard_map/cond/branch_0_fun/pallas_call | solution.py:170
  17.9 2.2 %fusion = f32[288,1152]{1,0:T(8,128)S(1)} fusion(bf16[1152,1024]{1,0:T(8,128)(2,1)S(1)} %get-tuple-element.74, f32[288,1024]{1,0:T(8,128)} %get-tuple-element.73), kind=kOutput, calls=%fused_computation | convolution fusion | flops 679772160 | bytes 4866048 | tf_op jit(solution)/shard_map/cond/branch_0_fun/dot_general | solution.py:318
  23.6 4.5 %collective-permute-done.1 = f32[96,128]{1,0:T(8,128)S(1)} collective-permute-done((f32[96,128]{1,0:T(8,128)S(1)}, f32[96,128]{1,0:T(8,128)S(1)}, u32[]{:S(2)}, u32[]{:S(2)}) %collective-permute-start.1) | collective-permute-done | bytes 49184 | tf_op jit(solution)/shard_map/ppermute | solution.py:271
  28.2 2.2 %collective-permute-done = f32[96,1024]{1,0:T(8,128)} collective-permute-done((f32[96,1024]{1,0:T(8,128)}, f32[96,1024]{1,0:T(8,128)}, u32[]{:S(2)}, u32[]{:S(2)}) %collective-permute-start) | collective-permute-done | bytes 393248 | tf_op jit(solution)/shard_map/ppermute | solution.py:271
  30.4 7.5 %conditional.5 = (f32[96,1024]{1,0:T(8,128)}, f32[96,128]{1,0:T(8,128)S(1)}) conditional(s32[]{:T(128)} %convert_element_type.44, (f32[8,1024]{1,0:T(8,128)S(1)}, f32[96,1024]{1,0:T(8,128)S(1)}, f32[96,1024]{1,0:T(8,128)}, f32[96,128]{1,0:T(8,128)S(1)}, bf16[1152,1024]{1,0:T(8,128)(2,1)S(1)}) %tuple.39, (f32[96,1024]{1,0:T(8,128)}, ...), branch_computations={%region_2.0_spmd, %region_3.0_spmd} | conditional | flops 683335680 | bytes 9961488 | solution.py:359
  30.4 4.4 %branch_0_fun.5 = (f32[96,1024]{1,0:T(8,128)}, f32[288,1024]{1,0:T(8,128)}) custom-call(f32[8,1024]{1,0:T(8,128)S(1)} %get-tuple-element.77.refs_0_, f32[96,1024]{1,0:T(8,128)S(1)} %get-tuple-element.78.refs_1_, f32[96,1024]{1,0:T(8,128)} %get-tuple-element.79.refs_2_, f32[96,128]{1,0:T(8,128)S(1)} %get-tuple-element.80.refs_3_), custom_call_target="tpu_custom_call" | custom-call | flops 983040 | bytes 2441216 | tf_op jit(solution)/shard_map/cond/branch_0_fun/pallas_call | solution.py:170
  34.8 2.2 %fusion.2 = f32[288,1152]{1,0:T(8,128)S(1)} fusion(bf16[1152,1024]{1,0:T(8,128)(2,1)S(1)} %get-tuple-element.82, f32[288,1024]{1,0:T(8,128)} %get-tuple-element.81), kind=kOutput, calls=%fused_computation.4 | convolution fusion | flops 679772160 | bytes 4866048 | tf_op jit(solution)/shard_map/cond/branch_0_fun/dot_general | solution.py:318
  40.5 4.5 %collective-permute-done.3 = f32[96,128]{1,0:T(8,128)S(1)} collective-permute-done((f32[96,128]{1,0:T(8,128)S(1)}, f32[96,128]{1,0:T(8,128)S(1)}, u32[]{:S(2)}, u32[]{:S(2)}) %collective-permute-start.3) | collective-permute-done | bytes 49184 | tf_op jit(solution)/shard_map/ppermute | solution.py:271
  45.1 2.2 %collective-permute-done.2 = f32[96,1024]{1,0:T(8,128)} collective-permute-done((f32[96,1024]{1,0:T(8,128)}, f32[96,1024]{1,0:T(8,128)}, u32[]{:S(2)}, u32[]{:S(2)}) %collective-permute-start.2) | collective-permute-done | bytes 393248 | tf_op jit(solution)/shard_map/ppermute | solution.py:271
  47.3 7.5 %conditional.6 = (f32[96,1024]{1,0:T(8,128)}, f32[96,128]{1,0:T(8,128)S(1)}) conditional(s32[]{:T(128)} %convert_element_type.44, (f32[8,1024]{1,0:T(8,128)S(1)}, f32[96,1024]{1,0:T(8,128)S(1)}, f32[96,1024]{1,0:T(8,128)}, f32[96,128]{1,0:T(8,128)S(1)}, bf16[1152,1024]{1,0:T(8,128)(2,1)S(1)}) %tuple.41, (f32[96,1024]{1,0:T(8,128)}, ...), branch_computations={%region_4.0_spmd, %region_5.0_spmd} | conditional | flops 683335680 | bytes 9961488 | solution.py:359
  47.3 4.4 %branch_0_fun.6 = (f32[96,1024]{1,0:T(8,128)}, f32[288,1024]{1,0:T(8,128)}) custom-call(f32[8,1024]{1,0:T(8,128)S(1)} %get-tuple-element.90.refs_0_, f32[96,1024]{1,0:T(8,128)S(1)} %get-tuple-element.91.refs_1_, f32[96,1024]{1,0:T(8,128)} %get-tuple-element.92.refs_2_, f32[96,128]{1,0:T(8,128)S(1)} %get-tuple-element.93.refs_3_), custom_call_target="tpu_custom_call" | custom-call | flops 983040 | bytes 2441216 | tf_op jit(solution)/shard_map/cond/branch_0_fun/pallas_call | solution.py:170
  51.7 2.2 %fusion.13 = f32[288,1152]{1,0:T(8,128)S(1)} fusion(bf16[1152,1024]{1,0:T(8,128)(2,1)S(1)} %get-tuple-element.95, f32[288,1024]{1,0:T(8,128)} %get-tuple-element.94), kind=kOutput, calls=%fused_computation.23 | convolution fusion | flops 679772160 | bytes 4866048 | tf_op jit(solution)/shard_map/cond/branch_0_fun/dot_general | solution.py:318
  57.4 4.5 %collective-permute-done.5 = f32[96,128]{1,0:T(8,128)S(1)} collective-permute-done((f32[96,128]{1,0:T(8,128)S(1)}, f32[96,128]{1,0:T(8,128)S(1)}, u32[]{:S(2)}, u32[]{:S(2)}) %collective-permute-start.5) | collective-permute-done | bytes 49184 | tf_op jit(solution)/shard_map/ppermute | solution.py:271
  61.9 2.1 %collective-permute-done.4 = f32[96,1024]{1,0:T(8,128)S(1)} collective-permute-done((f32[96,1024]{1,0:T(8,128)}, f32[96,1024]{1,0:T(8,128)S(1)}, u32[]{:S(2)}, u32[]{:S(2)}) %collective-permute-start.4) | collective-permute-done | bytes 393248 | tf_op jit(solution)/shard_map/ppermute | solution.py:271
  64.0 4.1 %conditional.7 = (f32[2,96,1024]{2,1,0:T(8,128)S(1)}) conditional(s32[]{:T(128)} %convert_element_type.44, (f32[8,1024]{1,0:T(8,128)S(1)}, f32[96,1024]{1,0:T(8,128)S(1)}, f32[96,1024]{1,0:T(8,128)S(1)}, f32[96,128]{1,0:T(8,128)S(1)}) %tuple.43, (f32[96,1024]{1,0:T(8,128)S(1)}, f32[96,128]{1,0:T(8,128)S(1)}, bf16[1152,1024]{1,0:T(8,128)(2,1)S(1)}, ...), branch_computations={%region_6.0_spmd, %region_7.0_spmd} | conditional | flops 683532288 | bytes 11780132 | solution.py:359
  64.8 2.3 %branch_0_fun.7 = f32[96,1024]{1,0:T(8,128)} custom-call(f32[8,1024]{1,0:T(8,128)S(1)} %get-tuple-element.103.refs_0_, f32[96,1024]{1,0:T(8,128)S(1)} %get-tuple-element.104.refs_1_, f32[96,1024]{1,0:T(8,128)} %copy-done.4, f32[96,128]{1,0:T(8,128)S(1)} %get-tuple-element.106.refs_3_), custom_call_target="tpu_custom_call" | custom-call | flops 983040 | bytes 1261568 | tf_op jit(solution)/shard_map/cond/branch_0_fun/pallas_call | solution.py:170
  69.1 1.7 %collective-permute-done.6 = f32[2,96,1024]{2,1,0:T(8,128)S(1)} collective-permute-done((f32[2,96,1024]{2,1,0:T(8,128)S(1)}, f32[2,96,1024]{2,1,0:T(8,128)S(1)}, u32[]{:S(2)}, u32[]{:S(2)}) %collective-permute-start.6) | collective-permute-done | bytes 786464 | tf_op jit(solution)/shard_map/ppermute | solution.py:362
  75.0 14.3 %all-to-all-start = ((f32[128,1,128]{2,1,0:T(1,128)}), f32[128,1,128]{2,1,0:T(1,128)S(1)}, u32[]{:S(2)}, u32[]{:S(2)}) async-start(f32[128,1,128]{2,1,0:T(1,128)} %bitcast.21), calls=%async_computation | async-start | bytes 131072 | tf_op jit(solution)/shard_map/all_to_all | solution.py:391
  90.0 9.8 %all-to-all-done = f32[128,1,128]{2,1,0:T(1,128)S(1)} async-done(((f32[128,1,128]{2,1,0:T(1,128)}), f32[128,1,128]{2,1,0:T(1,128)S(1)}, u32[]{:S(2)}, u32[]{:S(2)}) %all-to-all-start) | async-done | bytes 65568 | tf_op jit(solution)/shard_map/all_to_all | solution.py:391
  (54 shorter events, 21.6 us)
Async XLA Ops:
  0.6 11.2 %copy-start = (f32[16,1024]{1,0:T(8,128)S(1)}, f32[16,1024]{1,0:T(8,128)}, u32[]{:S(2)}) copy-start(f32[16,1024]{1,0:T(8,128)} %param.18) | copy-start | bytes 196612
  0.6 11.1 %copy-start.6 = (f32[128,16,2]{0,2,1:T(2,128)S(1)}, f32[128,16,2]{0,2,1:T(2,128)}, u32[]{:S(2)}) copy-start(f32[128,16,2]{0,2,1:T(2,128)} %param.23) | copy-start | bytes 49156
  21.1 9.4 %collective-permute-start = (f32[96,1024]{1,0:T(8,128)}, f32[96,1024]{1,0:T(8,128)}, u32[]{:S(2)}, u32[]{:S(2)}) collective-permute-start(f32[96,1024]{1,0:T(8,128)} %get-tuple-element.122), channel_id=1, source_target_pairs={{0,64},{2,66},{4,68},{6,70},{8,72},{10,74},{12,76},{14,78},{16,80}... | collective-permute-start | bytes 1179656 | tf_op jit(solution)/shard_map/ppermute | solution.py:271
  22.3 5.8 %collective-permute-start.1 = (f32[96,128]{1,0:T(8,128)S(1)}, f32[96,128]{1,0:T(8,128)S(1)}, u32[]{:S(2)}, u32[]{:S(2)}) collective-permute-start(f32[96,128]{1,0:T(8,128)S(1)} %get-tuple-element.123), channel_id=1, source_target_pairs={{0,66},{2,68},{4,70},{6,72},{8,74},{10,76},{12,78},{14,80},{16,82}... | collective-permute-start | bytes 147464 | tf_op jit(solution)/shard_map/ppermute | solution.py:271
  37.9 9.4 %collective-permute-start.2 = (f32[96,1024]{1,0:T(8,128)}, f32[96,1024]{1,0:T(8,128)}, u32[]{:S(2)}, u32[]{:S(2)}) collective-permute-start(f32[96,1024]{1,0:T(8,128)} %get-tuple-element.124), channel_id=1, source_target_pairs={{0,64},{2,66},{4,68},{6,70},{8,72},{10,74},{12,76},{14,78},{16,80}... | collective-permute-start | bytes 1179656 | tf_op jit(solution)/shard_map/ppermute | solution.py:271
  39.2 5.8 %collective-permute-start.3 = (f32[96,128]{1,0:T(8,128)S(1)}, f32[96,128]{1,0:T(8,128)S(1)}, u32[]{:S(2)}, u32[]{:S(2)}) collective-permute-start(f32[96,128]{1,0:T(8,128)S(1)} %get-tuple-element.125), channel_id=1, source_target_pairs={{0,66},{2,68},{4,70},{6,72},{8,74},{10,76},{12,78},{14,80},{16,82}... | collective-permute-start | bytes 147464 | tf_op jit(solution)/shard_map/ppermute | solution.py:271
  54.8 9.2 %collective-permute-start.4 = (f32[96,1024]{1,0:T(8,128)}, f32[96,1024]{1,0:T(8,128)S(1)}, u32[]{:S(2)}, u32[]{:S(2)}) collective-permute-start(f32[96,1024]{1,0:T(8,128)} %get-tuple-element.126), channel_id=1, source_target_pairs={{0,64},{2,66},{4,68},{6,70},{8,72},{10,74},{12,76},{14,78},{16,80}... | collective-permute-start | bytes 1179656 | tf_op jit(solution)/shard_map/ppermute | solution.py:271
  56.1 5.8 %collective-permute-start.5 = (f32[96,128]{1,0:T(8,128)S(1)}, f32[96,128]{1,0:T(8,128)S(1)}, u32[]{:S(2)}, u32[]{:S(2)}) collective-permute-start(f32[96,128]{1,0:T(8,128)S(1)} %get-tuple-element.127), channel_id=1, source_target_pairs={{0,66},{2,68},{4,70},{6,72},{8,74},{10,76},{12,78},{14,80},{16,82}... | collective-permute-start | bytes 147464 | tf_op jit(solution)/shard_map/ppermute | solution.py:271
  64.0 0.8 copy-start.4
  68.2 0.9 copy-start.1
  68.2 2.6 %collective-permute-start.6 = (f32[2,96,1024]{2,1,0:T(8,128)S(1)}, f32[2,96,1024]{2,1,0:T(8,128)S(1)}, u32[]{:S(2)}, u32[]{:S(2)}) collective-permute-start(f32[2,96,1024]{2,1,0:T(8,128)S(1)} %get-tuple-element.178), channel_id=1, source_target_pairs={{0,1},{1,0},{2,3},{3,2},{4,5},{5,4},{6,7},{7,6},{8,9},{9,8},{10,11... | collective-permute-start | bytes 2359304 | tf_op jit(solution)/shard_map/ppermute | solution.py:362
  70.9 1.1 %copy-start.2 = (f32[2,96,1024]{2,1,0:T(8,128)S(1)}, f32[2,96,1024]{2,1,0:T(8,128)}, u32[]{:S(2)}) copy-start(f32[2,96,1024]{2,1,0:T(8,128)} %copy-done.1) | copy-start | bytes 2359300
  71.0 1.4 %copy-start.3 = (f32[128,1024]{1,0:T(8,128)S(1)}, f32[128,1024]{1,0:T(8,128)}, u32[]{:S(2)}) copy-start(f32[128,1024]{1,0:T(8,128)} %get-tuple-element.160) | copy-start | bytes 1572868
  75.0 24.9 %all-to-all-start = ((f32[128,1,128]{2,1,0:T(1,128)}), f32[128,1,128]{2,1,0:T(1,128)S(1)}, u32[]{:S(2)}, u32[]{:S(2)}) async-start(f32[128,1,128]{2,1,0:T(1,128)} %bitcast.21), calls=%async_computation | async-start | bytes 131072 | tf_op jit(solution)/shard_map/all_to_all | solution.py:391

commit v4 on v3

--- a/solution.py
+++ b/solution.py
@@ -8,6 +8,7 @@
 from jax.experimental.pallas import tpu as pltpu
 
 BLOCK = 128
+PIECES = 2
 
 
 def shifted(value, axis, steps):
@@ -110,9 +111,9 @@
         state, before = carry
         side_in = lateral_ref[pl.ds(hour, 1), :]
         if has_inflow:
-            now = (
-                product_ref[pl.ds(hour, 1), :] + product_ref[pl.ds(hour + steps, 1), :]
-            ) + product_ref[pl.ds(hour + 2 * steps, 1), :]
+            now = product_ref[pl.ds(hour, 1), :]
+            for piece_at in range(1, PIECES):
+                now = now + product_ref[pl.ds(hour + piece_at * steps, 1), :]
             inflow_ref[pl.ds(hour, 1), :] = now
             drive = (gain_now * now + gain_prev * before) + gain_side * side_in
         else:
@@ -155,7 +156,7 @@
         adj_ref[pl.ds(hour, 1), :] = state
         if emit:
             remainder = gain_now * state + gain_prev * later
-            for piece_at in range(3):
+            for piece_at in range(PIECES):
                 piece = remainder.astype(jnp.bfloat16).astype(jnp.float32)
                 piece_ref[pl.ds(hour + piece_at * steps, 1), :] = piece
                 remainder = remainder - piece
@@ -197,7 +198,7 @@
     steps, width = cotangent_all.shape
     kernel = functools.partial(backward_kernel, has_down=down is not None, emit=emit)
     args = (coef, cotangent_all) if down is None else (coef, cotangent_all, down, side)
-    outs = [(steps, width)] + ([(3 * steps, width)] if emit else [])
+    outs = [(steps, width)] + ([(PIECES * steps, width)] if emit else [])
     results = vmem_call(kernel, outs, *args)
     return results[0], (results[1] if emit else None)
 
@@ -205,7 +206,7 @@
 def split_three(value):
     pieces = []
     rest = value
-    for _ in range(3):
+    for _ in range(PIECES):
         piece = lax.reduce_precision(rest, exponent_bits=8, mantissa_bits=7)
         pieces.append(piece)
         rest = rest - piece
@@ -213,8 +214,11 @@
 
 
 def joined_three(product):
-    rows = product.shape[0] // 3
-    return (product[:rows] + product[rows : 2 * rows]) + product[2 * rows :]
+    rows = product.shape[0] // PIECES
+    total = product[:rows]
+    for piece_at in range(1, PIECES):
+        total = total + product[piece_at * rows : (piece_at + 1) * rows]
+    return total
 
 
 def coefficients(raw_params):
@@ -301,9 +305,15 @@
     coef = jnp.stack(
         [gain_now, gain_prev, gain_side, retain, live_mask, zero_row, zero_row, zero_row], axis=0
     )
-    lateral_all = whole_window(lateral)
-    cotangent_all = whole_window(cotangent)
-    steps_all = lateral_all.shape[0]
+    arrived = lax.ppermute(jnp.where(mine == 0, cotangent, lateral), "group", [(0, 1), (1, 0)])
+    window = jnp.where(
+        mine == 0,
+        jnp.concatenate([lateral, arrived], axis=0),
+        jnp.concatenate([arrived, cotangent], axis=0),
+    )
+    lateral_all = window
+    cotangent_all = window
+    steps_all = window.shape[0]
     source_ids = lax.broadcasted_iota(jnp.int32, (reach_dev + outlets, reach_dev), 0)
     confluence = jnp.zeros((reach_dev + outlets, reach_dev), jnp.float32)
     for upslot in range(up_count):
@@ -326,43 +336,44 @@
 
     def forward_first(operands):
         flow, outlet, unused = routed(coef, lateral_all)
-        return flow, outlet, jnp.stack([flow, zero_flow], axis=0)
+        return flow, outlet, flow, zero_flow, lateral_all
 
     def backward_first(operands):
         adjoint, pieces = adjoined(coef, cotangent_all)
         own, side = spread_of(pieces)
-        return own, side, jnp.stack([adjoint, zero_flow], axis=0)
+        return own, side, adjoint, zero_flow, zero_flow
 
     def forward_step(operands):
         upper, side = operands
         source = jnp.concatenate([upper, side], axis=1)
         product = jnp.dot(split_three(source), confluence, preferred_element_type=jnp.float32)
         flow, outlet, inflow = routed(coef, lateral_all, product)
-        return flow, outlet, jnp.stack([flow, inflow], axis=0)
+        return flow, outlet, flow, inflow, lateral_all
 
     def backward_step(operands):
         upper, side = operands
         adjoint, pieces = adjoined(coef, cotangent_all, upper, side)
         own, side = spread_of(pieces)
-        return own, side, jnp.stack([adjoint, zero_flow], axis=0)
+        return own, side, adjoint, zero_flow, zero_flow
 
     def backward_last(operands):
         upper, side = operands
         adjoint, unused = adjoined(coef, cotangent_all, upper, side, emit=False)
-        return zero_flow, side, jnp.stack([adjoint, zero_flow], axis=0)
-
-    message, outlet_message, kept = lax.cond(mine == 0, forward_first, backward_first, None)
+        return zero_flow, side, adjoint, zero_flow, zero_flow
+
+    message, outlet_message, *kept = lax.cond(mine == 0, forward_first, backward_first, None)
     for level_step in range(1, levels):
         upper = both_ways(message, 0)
         side = both_ways(outlet_message, 1)
         later = backward_step if level_step + 1 < levels else backward_last
-        message, outlet_message, kept = lax.cond(
+        message, outlet_message, *kept = lax.cond(
             mine == 0, forward_step, later, (upper, side)
         )
+    kept = jnp.stack(kept, axis=0)
     other = lax.ppermute(kept, "group", [(0, 1), (1, 0)])
     forward_kept = jnp.where(mine == 0, kept, other)
     backward_kept = jnp.where(mine == 0, other, kept)
-    outflow, inflow = forward_kept[0], forward_kept[1]
+    outflow, inflow, lateral_all = forward_kept[0], forward_kept[1], forward_kept[2]
     adjoint = backward_kept[0]
     zero_first = jnp.zeros((1, reach_dev), jnp.float32)
     flow_before = jnp.concatenate([zero_first, outflow[:-1]], axis=0)

time: 102 us -> 95.4 us (0.935)
  blocking collectives: 7.41 us -> 0 us
  Pallas kernels: 14.1 us -> 10.8 us
  starting transfers between devices: 22.3 us -> 25.3 us
  local copies, waits for them, and re-layouts: 10 us -> 8.4 us
  other arithmetic: 5.01 us -> 6.58 us
  waiting for transfers between devices: 31.7 us -> 33 us
    all_gather x2 -> x0, blocking collectives: 7.41 us -> none  [whole_window(): return lax.all_gather(value, 'group', axis=0, tiled=True)]
    ppermute x0 -> x1, starting transfers between devices: none -> 3.28 us  [body(): lax.ppermute(jnp.where(mine == 0, cotangent, lateral), 'group', [(0, 1),...]
    pallas_call x4, Pallas kernels: 14.1 us -> 10.8 us  [vmem_call(): pl.pallas_call(kernel, out_shape=[jax.ShapeDtypeStruct(shape, jnp.float32...]
    select_n x0 -> x2, other arithmetic: none -> 2.26 us  [the longest x1 1.27 us: body(): jnp.where(mine == 0, jnp.concatenate([lateral, arrived], axis=0), jnp.con...]
    unnamed x11 -> x5, local copies, waits for them, and re-layouts: 2.36 us -> 0.76 us
    ppermute x1, waiting for transfers between devices: 1.67 us -> 2.83 us  [body(): other = lax.ppermute(kept, 'group', [(0, 1), (1, 0)])]
  transfers between devices with their start and end apart: 8 -> 9, of which waited for: 8 -> 8; matrix products, arithmetic and copies ran while one was open for 1% -> 7% of each run, Pallas kernels for 0% -> 0%
where the time goes in v4:
time: 95.4 us; the launch traced here: 94.6 us
  waiting for transfers between devices  33 us (35%)
  starting transfers between devices  25.3 us (27%)
  Pallas kernels  10.8 us (11%)
  matrix products  8.89 us (9%)
  local copies, waits for them, and re-layouts  8.4 us (9%)
  other arithmetic  6.58 us (7%)
  between operations  1.54 us (2%)
    ppermute x6, waiting for transfers between devices, both_ways(): return lax.ppermute(value, ('level', 'basin', 'group'), pairs)  20.3 us
    all_to_all x1, starting transfers between devices, body(): lax.all_to_all(replicated, ('level', 'basin'), 0, 0, tiled=True)  14.2 us
    pallas_call x4, Pallas kernels, vmem_call(): pl.pallas_call(kernel, out_shape=[jax.ShapeDtypeStruct(shape, jnp.float32...  10.8 us
    all_to_all x1, waiting for transfers between devices, body(): lax.all_to_all(replicated, ('level', 'basin'), 0, 0, tiled=True)  9.85 us
    ppermute x6, starting transfers between devices, both_ways(): return lax.ppermute(value, ('level', 'basin', 'group'), pairs)  7.72 us
    dot_general x3, matrix products, spread_of(): lax.dot_general(pieces.astype(jnp.bfloat16), confluence, (((1,), (1,)), (...  6.18 us
    ppermute x1, starting transfers between devices, body(): lax.ppermute(jnp.where(mine == 0, cotangent, lateral), 'group', [(0, 1),...  3.28 us
    ppermute x1, waiting for transfers between devices, body(): other = lax.ppermute(kept, 'group', [(0, 1), (1, 0)])  2.83 us
  transfers between devices with their start and end apart: 9, of which 8 were waited for; matrix products, arithmetic and copies ran while one was open for 7% of the time, Pallas kernels for 0%

profile of v4, /device:TPU:1, one launch (start us, length us, event | category | flops | bytes accessed | tf_op | source)
XLA Modules:
  0.0 94.6 jit_solution(6911456170485351175)
XLA Ops:
  1.6 3.3 %collective-permute-start = (f32[48,1024]{1,0:T(8,128)S(1)}, f32[48,1024]{1,0:T(8,128)}, u32[]{:S(2)}, u32[]{:S(2)}) collective-permute-start(f32[48,1024]{1,0:T(8,128)S(1)} %broadcast_select_fusion.1), channel_id=1, source_target_pairs={{0,1},{1,0},{2,3},{3,2},{4,5},{5,4},{6,7},{7,6},{8,9},{9,8},{10,11... | collective-permute-start | bytes 589832 | tf_op jit(solution)/shard_map/ppermute | solution.py:308
  7.9 1.8 %fusion.30 = f32[1024,2]{0,1:T(2,128)S(1)} fusion(f32[1024,128]{0,1:T(8,128)S(1)} %get-tuple-element.164, f32[16,1024]{1,0:T(8,128)S(1)} %copy-done, f32[128,2,16]{0,1,2:T(2,128)} %bitcast.68), kind=kOutput, calls=%fused_computation.49 | convolution fusion | flops 50853888 | bytes 614400 | tf_op jit(solution)/shard_map/dot_general | solution.py:290
  9.8 1.9 %add_convert_fusion = bf16[1152,1024]{1,0:T(8,128)(2,1)S(1)} fusion(s32[1024]{0:T(1024)S(1)} %bitcast.63, s32[1024]{0:T(1024)S(1)} %bitcast.62, pred[1024]{0:T(1024)(128)(4,1)S(1)} %get-tuple-element.166, pred[1024]{0:T(1024)(128)(4,1)S(1)} %get-tuple-element.165), kind=kLoop, calls=%fused_computation.42 | loop fusion | flops 9437184 | bytes 2369536 | tf_op jit(solution)/shard_map/convert_element_type | solution.py:323
  13.0 5.2 %conditional.4 = ((f32[96,1024]{1,0:T(8,128)}, f32[96,128]{1,0:T(8,128)S(1)})) conditional(s32[]{:T(128)} %convert_element_type.44, (f32[8,1024]{1,0:T(8,128)S(1)}, f32[96,1024]{1,0:T(8,128)S(1)}, bf16[1152,1024]{1,0:T(8,128)(2,1)S(1)}) %tuple.45, (f32[8,1024]{1,0:T(8,128)S(1)}, f32[96,1024]{1,0:T(8,128)S(1)}) %tuple.46), branch_computations={%region_0.1_spmd, %region_1.2_spmd} | conditional | flops 454275072 | bytes 7847960 | solution.py:364
  13.0 2.3 %branch_0_fun.4 = (f32[96,1024]{1,0:T(8,128)}, f32[192,1024]{1,0:T(8,128)}) custom-call(f32[8,1024]{1,0:T(8,128)S(1)} %get-tuple-element.71.refs_0_, f32[96,1024]{1,0:T(8,128)S(1)} %get-tuple-element.72.refs_1_), custom_call_target="tpu_custom_call" | custom-call | flops 983040 | bytes 1605632 | tf_op jit(solution)/shard_map/cond/branch_0_fun/pallas_call | solution.py:171
  15.3 2.1 %fusion = f32[192,1152]{1,0:T(8,128)S(1)} fusion(bf16[1152,1024]{1,0:T(8,128)(2,1)S(1)} %get-tuple-element.74, f32[192,1024]{1,0:T(8,128)} %get-tuple-element.73), kind=kOutput, calls=%fused_computation.1 | convolution fusion | flops 453181440 | bytes 4030464 | tf_op jit(solution)/shard_map/cond/branch_0_fun/dot_general | solution.py:328
  19.5 1.3 %collective-permute-start.2 = (f32[96,128]{1,0:T(8,128)S(1)}, f32[96,128]{1,0:T(8,128)S(1)}, u32[]{:S(2)}, u32[]{:S(2)}) collective-permute-start(f32[96,128]{1,0:T(8,128)S(1)} %get-tuple-element.126), channel_id=1, source_target_pairs={{0,66},{2,68},{4,70},{6,72},{8,74},{10,76},{12,78},{14,80},{16,82}... | collective-permute-start | bytes 147464 | tf_op jit(solution)/shard_map/ppermute | solution.py:275
  20.8 4.5 %collective-permute-done.2 = f32[96,128]{1,0:T(8,128)S(1)} collective-permute-done((f32[96,128]{1,0:T(8,128)S(1)}, f32[96,128]{1,0:T(8,128)S(1)}, u32[]{:S(2)}, u32[]{:S(2)}) %collective-permute-start.2) | collective-permute-done | bytes 49184 | tf_op jit(solution)/shard_map/ppermute | solution.py:275
  25.3 2.2 %collective-permute-done.1 = f32[96,1024]{1,0:T(8,128)} collective-permute-done((f32[96,1024]{1,0:T(8,128)}, f32[96,1024]{1,0:T(8,128)}, u32[]{:S(2)}, u32[]{:S(2)}) %collective-permute-start.1) | collective-permute-done | bytes 393248 | tf_op jit(solution)/shard_map/ppermute | solution.py:275
  27.6 6.5 %conditional.5 = (f32[96,1024]{1,0:T(8,128)}, f32[96,128]{1,0:T(8,128)S(1)}) conditional(s32[]{:T(128)} %convert_element_type.44, (f32[8,1024]{1,0:T(8,128)S(1)}, f32[96,1024]{1,0:T(8,128)S(1)}, f32[96,1024]{1,0:T(8,128)}, f32[96,128]{1,0:T(8,128)S(1)}, bf16[1152,1024]{1,0:T(8,128)(2,1)S(1)}) %tuple.47, (f32[96,1024]{1,0:T(8,128)}, ...), branch_computations={%region_2.3_spmd, %region_3.4_spmd} | conditional | flops 455405568 | bytes 8290320 | solution.py:369
  27.6 3.5 %branch_0_fun.5 = (f32[96,1024]{1,0:T(8,128)}, f32[192,1024]{1,0:T(8,128)}) custom-call(f32[8,1024]{1,0:T(8,128)S(1)} %get-tuple-element.77.refs_0_, f32[96,1024]{1,0:T(8,128)S(1)} %get-tuple-element.78.refs_1_, f32[96,1024]{1,0:T(8,128)} %get-tuple-element.79.refs_2_, f32[96,128]{1,0:T(8,128)S(1)} %get-tuple-element.80.refs_3_), custom_call_target="tpu_custom_call" | custom-call | flops 983040 | bytes 2048000 | tf_op jit(solution)/shard_map/cond/branch_0_fun/pallas_call | solution.py:171
  31.1 2.1 %fusion.2 = f32[192,1152]{1,0:T(8,128)S(1)} fusion(bf16[1152,1024]{1,0:T(8,128)(2,1)S(1)} %get-tuple-element.82, f32[192,1024]{1,0:T(8,128)} %get-tuple-element.81), kind=kOutput, calls=%fused_computation.4 | convolution fusion | flops 453181440 | bytes 4030464 | tf_op jit(solution)/shard_map/cond/branch_0_fun/dot_general | solution.py:328
  36.6 4.5 %collective-permute-done.4 = f32[96,128]{1,0:T(8,128)S(1)} collective-permute-done((f32[96,128]{1,0:T(8,128)S(1)}, f32[96,128]{1,0:T(8,128)S(1)}, u32[]{:S(2)}, u32[]{:S(2)}) %collective-permute-start.4) | collective-permute-done | bytes 49184 | tf_op jit(solution)/shard_map/ppermute | solution.py:275
  41.2 2.2 %collective-permute-done.3 = f32[96,1024]{1,0:T(8,128)} collective-permute-done((f32[96,1024]{1,0:T(8,128)}, f32[96,1024]{1,0:T(8,128)}, u32[]{:S(2)}, u32[]{:S(2)}) %collective-permute-start.3) | collective-permute-done | bytes 393248 | tf_op jit(solution)/shard_map/ppermute | solution.py:275
  43.4 6.5 %conditional.6 = (f32[96,1024]{1,0:T(8,128)}, f32[96,128]{1,0:T(8,128)S(1)}) conditional(s32[]{:T(128)} %convert_element_type.44, (f32[8,1024]{1,0:T(8,128)S(1)}, f32[96,1024]{1,0:T(8,128)S(1)}, f32[96,1024]{1,0:T(8,128)}, f32[96,128]{1,0:T(8,128)S(1)}, bf16[1152,1024]{1,0:T(8,128)(2,1)S(1)}) %tuple.49, (f32[96,1024]{1,0:T(8,128)}, ...), branch_computations={%region_4.5_spmd, %region_5.6_spmd} | conditional | flops 455405568 | bytes 8290320 | solution.py:369
  43.4 3.5 %branch_0_fun.6 = (f32[96,1024]{1,0:T(8,128)}, f32[192,1024]{1,0:T(8,128)}) custom-call(f32[8,1024]{1,0:T(8,128)S(1)} %get-tuple-element.90.refs_0_, f32[96,1024]{1,0:T(8,128)S(1)} %get-tuple-element.91.refs_1_, f32[96,1024]{1,0:T(8,128)} %get-tuple-element.92.refs_2_, f32[96,128]{1,0:T(8,128)S(1)} %get-tuple-element.93.refs_3_), custom_call_target="tpu_custom_call" | custom-call | flops 983040 | bytes 2048000 | tf_op jit(solution)/shard_map/cond/branch_0_fun/pallas_call | solution.py:171
  46.9 2.1 %fusion.11 = f32[192,1152]{1,0:T(8,128)S(1)} fusion(bf16[1152,1024]{1,0:T(8,128)(2,1)S(1)} %get-tuple-element.95, f32[192,1024]{1,0:T(8,128)} %get-tuple-element.94), kind=kOutput, calls=%fused_computation.18 | convolution fusion | flops 453181440 | bytes 4030464 | tf_op jit(solution)/shard_map/cond/branch_0_fun/dot_general | solution.py:328
  52.4 4.5 %collective-permute-done.6 = f32[96,128]{1,0:T(8,128)S(1)} collective-permute-done((f32[96,128]{1,0:T(8,128)S(1)}, f32[96,128]{1,0:T(8,128)S(1)}, u32[]{:S(2)}, u32[]{:S(2)}) %collective-permute-start.6) | collective-permute-done | bytes 49184 | tf_op jit(solution)/shard_map/ppermute | solution.py:275
  57.0 2.2 %collective-permute-done.5 = f32[96,1024]{1,0:T(8,128)} collective-permute-done((f32[96,1024]{1,0:T(8,128)}, f32[96,1024]{1,0:T(8,128)}, u32[]{:S(2)}, u32[]{:S(2)}) %collective-permute-start.5) | collective-permute-done | bytes 393248 | tf_op jit(solution)/shard_map/ppermute | solution.py:275
  59.2 2.4 %conditional.7 = (f32[1,96,1024]{2,1,0:T(8,128)S(1)}, f32[1,96,1024]{2,1,0:T(8,128)S(1)}, f32[1,96,1024]{2,1,0:T(8,128)}) conditional(s32[]{:T(128)} %convert_element_type.44, (f32[8,1024]{1,0:T(8,128)S(1)}, f32[96,1024]{1,0:T(8,128)S(1)}, f32[96,1024]{1,0:T(8,128)}, f32[96,128]{1,0:T(8,128)S(1)}) %tuple.51, (f32[96,1024]{1,0:T(8,128)}, ...), branch_computations={%region_6.7_spmd, %region_7.8_spmd} | conditional | flops 455405568 | bytes 8192024 | solution.py:369
  59.2 1.5 %branch_0_fun.7 = f32[96,1024]{1,0:T(8,128)S(1)} custom-call(f32[8,1024]{1,0:T(8,128)S(1)} %get-tuple-element.103.refs_0_, f32[96,1024]{1,0:T(8,128)S(1)} %get-tuple-element.104.refs_1_, f32[96,1024]{1,0:T(8,128)} %get-tuple-element.105.refs_2_, f32[96,128]{1,0:T(8,128)S(1)} %get-tuple-element.106.refs_3_), custom_call_target="tpu_custom_call" | custom-call | flops 983040 | bytes 1261568 | tf_op jit(solution)/shard_map/cond/branch_0_fun/pallas_call | solution.py:171
  62.8 2.8 %collective-permute-done.7 = f32[3,96,1024]{2,1,0:T(8,128)S(1)} collective-permute-done((f32[3,96,1024]{2,1,0:T(8,128)S(1)}, f32[3,96,1024]{2,1,0:T(8,128)S(1)}, u32[]{:S(2)}, u32[]{:S(2)}) %collective-permute-start.7) | collective-permute-done | bytes 1179680 | tf_op jit(solution)/shard_map/ppermute | solution.py:373
  68.9 14.2 %all-to-all-start = ((f32[128,1,128]{2,1,0:T(1,128)}), f32[128,1,128]{2,1,0:T(1,128)S(1)}, u32[]{:S(2)}, u32[]{:S(2)}) async-start(f32[128,1,128]{2,1,0:T(1,128)} %bitcast.23), calls=%async_computation | async-start | bytes 131072 | tf_op jit(solution)/shard_map/all_to_all | solution.py:402
  83.8 9.8 %all-to-all-done = f32[128,1,128]{2,1,0:T(1,128)S(1)} async-done(((f32[128,1,128]{2,1,0:T(1,128)}), f32[128,1,128]{2,1,0:T(1,128)S(1)}, u32[]{:S(2)}, u32[]{:S(2)}) %all-to-all-start) | async-done | bytes 65568 | tf_op jit(solution)/shard_map/all_to_all | solution.py:402
  (50 shorter events, 20.6 us)
Async XLA Ops:
  0.6 7.3 %copy-start = (f32[16,1024]{1,0:T(8,128)S(1)}, f32[16,1024]{1,0:T(8,128)}, u32[]{:S(2)}) copy-start(f32[16,1024]{1,0:T(8,128)} %param.18) | copy-start | bytes 196612
  1.6 10.1 %collective-permute-start = (f32[48,1024]{1,0:T(8,128)S(1)}, f32[48,1024]{1,0:T(8,128)}, u32[]{:S(2)}, u32[]{:S(2)}) collective-permute-start(f32[48,1024]{1,0:T(8,128)S(1)} %broadcast_select_fusion.1), channel_id=1, source_target_pairs={{0,1},{1,0},{2,3},{3,2},{4,5},{5,4},{6,7},{7,6},{8,9},{9,8},{10,11... | collective-permute-start | bytes 589832 | tf_op jit(solution)/shard_map/ppermute | solution.py:308
  18.2 9.4 %collective-permute-start.1 = (f32[96,1024]{1,0:T(8,128)}, f32[96,1024]{1,0:T(8,128)}, u32[]{:S(2)}, u32[]{:S(2)}) collective-permute-start(f32[96,1024]{1,0:T(8,128)} %get-tuple-element.125), channel_id=1, source_target_pairs={{0,64},{2,66},{4,68},{6,70},{8,72},{10,74},{12,76},{14,78},{16,80}... | collective-permute-start | bytes 1179656 | tf_op jit(solution)/shard_map/ppermute | solution.py:275
  19.5 5.8 %collective-permute-start.2 = (f32[96,128]{1,0:T(8,128)S(1)}, f32[96,128]{1,0:T(8,128)S(1)}, u32[]{:S(2)}, u32[]{:S(2)}) collective-permute-start(f32[96,128]{1,0:T(8,128)S(1)} %get-tuple-element.126), channel_id=1, source_target_pairs={{0,66},{2,68},{4,70},{6,72},{8,74},{10,76},{12,78},{14,80},{16,82}... | collective-permute-start | bytes 147464 | tf_op jit(solution)/shard_map/ppermute | solution.py:275
  34.0 9.4 %collective-permute-start.3 = (f32[96,1024]{1,0:T(8,128)}, f32[96,1024]{1,0:T(8,128)}, u32[]{:S(2)}, u32[]{:S(2)}) collective-permute-start(f32[96,1024]{1,0:T(8,128)} %get-tuple-element.127), channel_id=1, source_target_pairs={{0,64},{2,66},{4,68},{6,70},{8,72},{10,74},{12,76},{14,78},{16,80}... | collective-permute-start | bytes 1179656 | tf_op jit(solution)/shard_map/ppermute | solution.py:275
  35.3 5.8 %collective-permute-start.4 = (f32[96,128]{1,0:T(8,128)S(1)}, f32[96,128]{1,0:T(8,128)S(1)}, u32[]{:S(2)}, u32[]{:S(2)}) collective-permute-start(f32[96,128]{1,0:T(8,128)S(1)} %get-tuple-element.128), channel_id=1, source_target_pairs={{0,66},{2,68},{4,70},{6,72},{8,74},{10,76},{12,78},{14,80},{16,82}... | collective-permute-start | bytes 147464 | tf_op jit(solution)/shard_map/ppermute | solution.py:275
  49.8 9.4 %collective-permute-start.5 = (f32[96,1024]{1,0:T(8,128)}, f32[96,1024]{1,0:T(8,128)}, u32[]{:S(2)}, u32[]{:S(2)}) collective-permute-start(f32[96,1024]{1,0:T(8,128)} %get-tuple-element.129), channel_id=1, source_target_pairs={{0,64},{2,66},{4,68},{6,70},{8,72},{10,74},{12,76},{14,78},{16,80}... | collective-permute-start | bytes 1179656 | tf_op jit(solution)/shard_map/ppermute | solution.py:275
  51.1 5.8 %collective-permute-start.6 = (f32[96,128]{1,0:T(8,128)S(1)}, f32[96,128]{1,0:T(8,128)S(1)}, u32[]{:S(2)}, u32[]{:S(2)}) collective-permute-start(f32[96,128]{1,0:T(8,128)S(1)} %get-tuple-element.130), channel_id=1, source_target_pairs={{0,66},{2,68},{4,70},{6,72},{8,74},{10,76},{12,78},{14,80},{16,82}... | collective-permute-start | bytes 147464 | tf_op jit(solution)/shard_map/ppermute | solution.py:275
  62.7 2.9 %collective-permute-start.7 = (f32[3,96,1024]{2,1,0:T(8,128)S(1)}, f32[3,96,1024]{2,1,0:T(8,128)S(1)}, u32[]{:S(2)}, u32[]{:S(2)}) collective-permute-start(f32[3,96,1024]{2,1,0:T(8,128)S(1)} %constant_dynamic-update-slice_fusion.6), channel_id=1, source_target_pairs={{0,1},{1,0},{2,3},{3,2},{4,5},{5,4},{6,7},{7,6},{8,9},{9,8},{10,11... | collective-permute-start | bytes 3538952 | tf_op jit(solution)/shard_map/ppermute | solution.py:373
  68.9 24.8 %all-to-all-start = ((f32[128,1,128]{2,1,0:T(1,128)}), f32[128,1,128]{2,1,0:T(1,128)S(1)}, u32[]{:S(2)}, u32[]{:S(2)}) async-start(f32[128,1,128]{2,1,0:T(1,128)} %bitcast.23), calls=%async_computation | async-start | bytes 131072 | tf_op jit(solution)/shard_map/all_to_all | solution.py:402

commit v5 on v4

--- a/solution.py
+++ b/solution.py
@@ -99,17 +99,18 @@
 
 def forward_kernel(*refs, has_inflow):
     if has_inflow:
-        coef_ref, product_ref, lateral_ref, out_ref, outlet_ref, inflow_ref = refs
+        coef_ref, product_ref, early_ref, late_ref, out_ref, outlet_ref, inflow_ref = refs
     else:
-        coef_ref, lateral_ref, out_ref, outlet_ref = refs
-    steps = lateral_ref.shape[0]
+        coef_ref, early_ref, late_ref, out_ref, outlet_ref = refs
+    half = early_ref.shape[0]
+    steps = 2 * half
     narrow = outlet_ref.shape[1]
     gain_now, gain_prev, gain_side = coef_ref[0:1, :], coef_ref[1:2, :], coef_ref[2:3, :]
     keep, live = coef_ref[3:4, :], coef_ref[4:5, :]
 
-    def advance(hour, carry):
+    def advance(hour, carry, side_ref, side_at):
         state, before = carry
-        side_in = lateral_ref[pl.ds(hour, 1), :]
+        side_in = side_ref[pl.ds(side_at, 1), :]
         if has_inflow:
             now = product_ref[pl.ds(hour, 1), :]
             for piece_at in range(1, PIECES):
@@ -126,26 +127,35 @@
         return state, now
 
     zero = jnp.zeros_like(keep)
-    lax.fori_loop(0, steps, advance, (zero, zero), unroll=8)
+    carry = lax.fori_loop(
+        0, half, lambda hour, carry: advance(hour, carry, early_ref, hour), (zero, zero), unroll=8
+    )
+    lax.fori_loop(
+        0,
+        half,
+        lambda position, carry: advance(position + half, carry, late_ref, position),
+        carry,
+        unroll=8,
+    )
 
 
 def backward_kernel(*refs, has_down, emit):
     refs = list(refs)
-    coef_ref, cot_ref = refs[0], refs[1]
-    rest = refs[2:]
+    coef_ref, early_ref, late_ref = refs[0], refs[1], refs[2]
+    rest = refs[3:]
     if has_down:
         down_ref, side_ref = rest[0], rest[1]
         rest = rest[2:]
     adj_ref = rest[0]
     piece_ref = rest[1] if emit else None
-    steps = cot_ref.shape[0]
+    half = early_ref.shape[0]
+    steps = 2 * half
     gain_now, gain_prev = coef_ref[0:1, :], coef_ref[1:2, :]
     keep, live = coef_ref[3:4, :], coef_ref[4:5, :]
 
-    def advance(position, carry):
-        hour = steps - 1 - position
+    def advance(hour, carry, cot_ref, cot_at):
         state, later = carry
-        load = cot_ref[pl.ds(hour, 1), :]
+        load = cot_ref[pl.ds(cot_at, 1), :]
         if has_down:
             down = down_ref[pl.ds(hour, 1), :]
             side = side_ref[pl.ds(hour, 1), :]
@@ -163,7 +173,20 @@
         return state, state
 
     zero = jnp.zeros_like(keep)
-    lax.fori_loop(0, steps, advance, (zero, zero), unroll=8)
+    carry = lax.fori_loop(
+        0,
+        half,
+        lambda position, carry: advance(steps - 1 - position, carry, late_ref, half - 1 - position),
+        (zero, zero),
+        unroll=8,
+    )
+    lax.fori_loop(
+        0,
+        half,
+        lambda position, carry: advance(half - 1 - position, carry, early_ref, half - 1 - position),
+        carry,
+        unroll=8,
+    )
 
 
 def vmem_call(kernel, outs, *args):
@@ -181,23 +204,25 @@
     )(*args)
 
 
-def routed(coef, lateral_all, product=None):
-    steps, width = lateral_all.shape
+def routed(coef, early, late, product=None):
+    half, width = early.shape
+    steps = 2 * half
     narrow = width // 8
     if product is None:
         kernel = functools.partial(forward_kernel, has_inflow=False)
-        flow, outlet = vmem_call(kernel, [(steps, width), (steps, narrow)], coef, lateral_all)
+        flow, outlet = vmem_call(kernel, [(steps, width), (steps, narrow)], coef, early, late)
         return flow, outlet, None
     kernel = functools.partial(forward_kernel, has_inflow=True)
     return vmem_call(
-        kernel, [(steps, width), (steps, narrow), (steps, width)], coef, product, lateral_all
-    )
-
-
-def adjoined(coef, cotangent_all, down=None, side=None, emit=True):
-    steps, width = cotangent_all.shape
+        kernel, [(steps, width), (steps, narrow), (steps, width)], coef, product, early, late
+    )
+
+
+def adjoined(coef, early, late, down=None, side=None, emit=True):
+    half, width = early.shape
+    steps = 2 * half
     kernel = functools.partial(backward_kernel, has_down=down is not None, emit=emit)
-    args = (coef, cotangent_all) if down is None else (coef, cotangent_all, down, side)
+    args = (coef, early, late) if down is None else (coef, early, late, down, side)
     outs = [(steps, width)] + ([(PIECES * steps, width)] if emit else [])
     results = vmem_call(kernel, outs, *args)
     return results[0], (results[1] if emit else None)
@@ -305,15 +330,9 @@
     coef = jnp.stack(
         [gain_now, gain_prev, gain_side, retain, live_mask, zero_row, zero_row, zero_row], axis=0
     )
-    arrived = lax.ppermute(jnp.where(mine == 0, cotangent, lateral), "group", [(0, 1), (1, 0)])
-    window = jnp.where(
-        mine == 0,
-        jnp.concatenate([lateral, arrived], axis=0),
-        jnp.concatenate([arrived, cotangent], axis=0),
-    )
-    lateral_all = window
-    cotangent_all = window
-    steps_all = window.shape[0]
+    late_lateral = lax.ppermute(lateral, "group", [(1, 0)])
+    early_cotangent = lax.ppermute(cotangent, "group", [(0, 1)])
+    steps_all = 2 * steps_dev
     source_ids = lax.broadcasted_iota(jnp.int32, (reach_dev + outlets, reach_dev), 0)
     confluence = jnp.zeros((reach_dev + outlets, reach_dev), jnp.float32)
     for upslot in range(up_count):
@@ -335,11 +354,11 @@
         return spread[:, :reach_dev], spread[:, reach_dev:]
 
     def forward_first(operands):
-        flow, outlet, unused = routed(coef, lateral_all)
-        return flow, outlet, flow, zero_flow, lateral_all
+        flow, outlet, unused = routed(coef, lateral, late_lateral)
+        return flow, outlet, flow, zero_flow, zero_flow
 
     def backward_first(operands):
-        adjoint, pieces = adjoined(coef, cotangent_all)
+        adjoint, pieces = adjoined(coef, early_cotangent, cotangent)
         own, side = spread_of(pieces)
         return own, side, adjoint, zero_flow, zero_flow
 
@@ -347,24 +366,25 @@
         upper, side = operands
         source = jnp.concatenate([upper, side], axis=1)
         product = jnp.dot(split_three(source), confluence, preferred_element_type=jnp.float32)
-        flow, outlet, inflow = routed(coef, lateral_all, product)
+        flow, outlet, inflow = routed(coef, lateral, late_lateral, product)
+        lateral_all = jnp.concatenate([lateral, late_lateral], axis=0)
         return flow, outlet, flow, inflow, lateral_all
 
     def backward_step(operands):
         upper, side = operands
-        adjoint, pieces = adjoined(coef, cotangent_all, upper, side)
+        adjoint, pieces = adjoined(coef, early_cotangent, cotangent, upper, side)
         own, side = spread_of(pieces)
         return own, side, adjoint, zero_flow, zero_flow
 
     def backward_last(operands):
         upper, side = operands
-        adjoint, unused = adjoined(coef, cotangent_all, upper, side, emit=False)
+        adjoint, unused = adjoined(coef, early_cotangent, cotangent, upper, side, emit=False)
         return zero_flow, side, adjoint, zero_flow, zero_flow
 
     message, outlet_message, *kept = lax.cond(mine == 0, forward_first, backward_first, None)
     for level_step in range(1, levels):
+        side = both_ways(outlet_message, 1)
         upper = both_ways(message, 0)
-        side = both_ways(outlet_message, 1)
         later = backward_step if level_step + 1 < levels else backward_last
         message, outlet_message, *kept = lax.cond(
             mine == 0, forward_step, later, (upper, side)

time: 95.4 us -> 97.7 us (1.024)
  starting transfers between devices: 25.3 us -> 30.1 us
  other arithmetic: 6.58 us -> 5.1 us
  local copies, waits for them, and re-layouts: 8.4 us -> 7.16 us
    ppermute x1 -> x2, starting transfers between devices: 3.28 us -> 6.54 us  [the longest x1 5.25 us: body(): late_lateral = lax.ppermute(lateral, 'group', [(1, 0)])]
    select_n x2 -> x0, other arithmetic: 2.26 us -> none  [the longest x1 1.27 us: body(): jnp.where(mine == 0, jnp.concatenate([lateral, arrived], axis=0), jnp.con...]
    another operation x3, local copies, waits for them, and re-layouts: 1.83 us -> 0.09 us  [body(): kept = jnp.stack(kept, axis=0)]
    all_to_all x1, starting transfers between devices: 14.2 us -> 15.6 us  [body(): lax.all_to_all(replicated, ('level', 'basin'), 0, 0, tiled=True)]
  transfers between devices with their start and end apart: 9 -> 10, of which waited for: 8 -> 8; matrix products, arithmetic and copies ran while one was open for 7% -> 8% of each run, Pallas kernels for 0% -> 0%
where the time goes in v5:
time: 97.7 us; the launch traced here: 96.9 us
  waiting for transfers between devices  33 us (34%)
  starting transfers between devices  30.1 us (31%)
  Pallas kernels  10.9 us (11%)
  matrix products  8.9 us (9%)
  local copies, waits for them, and re-layouts  7.16 us (7%)
  other arithmetic  5.1 us (5%)
  between operations  1.58 us (2%)
    ppermute x6, waiting for transfers between devices, both_ways(): return lax.ppermute(value, ('level', 'basin', 'group'), pairs)  20.3 us
    all_to_all x1, starting transfers between devices, body(): lax.all_to_all(replicated, ('level', 'basin'), 0, 0, tiled=True)  15.6 us
    pallas_call x4, Pallas kernels, vmem_call(): pl.pallas_call(kernel, out_shape=[jax.ShapeDtypeStruct(shape, jnp.float32...  10.9 us
    all_to_all x1, waiting for transfers between devices, body(): lax.all_to_all(replicated, ('level', 'basin'), 0, 0, tiled=True)  9.85 us
    ppermute x6, starting transfers between devices, both_ways(): return lax.ppermute(value, ('level', 'basin', 'group'), pairs)  7.72 us
    dot_general x3, matrix products, spread_of(): lax.dot_general(pieces.astype(jnp.bfloat16), confluence, (((1,), (1,)), (...  6.19 us
    ppermute x1, starting transfers between devices, body(): late_lateral = lax.ppermute(lateral, 'group', [(1, 0)])  5.25 us
    ppermute x1, waiting for transfers between devices, body(): other = lax.ppermute(kept, 'group', [(0, 1), (1, 0)])  2.83 us
  transfers between devices with their start and end apart: 10, of which 8 were waited for; matrix products, arithmetic and copies ran while one was open for 8% of the time, Pallas kernels for 0%

profile of v5, /device:TPU:1, one launch (start us, length us, event | category | flops | bytes accessed | tf_op | source)
XLA Modules:
  0.0 96.9 jit_solution(5350851639344654989)
XLA Ops:
  0.7 5.2 %collective-permute-start.1 = (f32[48,1024]{1,0:T(8,128)}, f32[48,1024]{1,0:T(8,128)S(1)}, u32[]{:S(2)}, u32[]{:S(2)}) collective-permute-start(f32[48,1024]{1,0:T(8,128)} %param.16), channel_id=1, source_target_pairs={{1,0},{3,2},{5,4},{7,6},{9,8},{11,10},{13,12},{15,14},{17,16},{19,... | collective-permute-start | bytes 589832 | tf_op jit(solution)/shard_map/ppermute | solution.py:333
  9.4 1.6 %fusion.34 = (f32[128,1024]{1,0:T(8,128)}, f32[1024,128]{0,1:T(8,128)S(1)}) fusion(s32[1024]{0:T(1024)} %param.19), kind=kLoop, calls=%fused_computation.57 | loop fusion | flops 393216 | bytes 1052672 | tf_op jit(solution)/shard_map/convert_element_type | solution.py:314
  10.9 1.8 %fusion.30 = f32[1024,2]{0,1:T(2,128)S(1)} fusion(f32[1024,128]{0,1:T(8,128)S(1)} %get-tuple-element.188, f32[16,1024]{1,0:T(8,128)S(1)} %copy-done, f32[128,2,16]{0,1,2:T(2,128)} %bitcast.68), kind=kOutput, calls=%fused_computation.50 | convolution fusion | flops 50853888 | bytes 614400 | tf_op jit(solution)/shard_map/dot_general | solution.py:315
  12.8 1.9 %add_convert_fusion = bf16[1152,1024]{1,0:T(8,128)(2,1)S(1)} fusion(s32[1024]{0:T(1024)S(1)} %bitcast.63, s32[1024]{0:T(1024)S(1)} %bitcast.62, pred[1024]{0:T(1024)(128)(4,1)S(1)} %get-tuple-element.190, pred[1024]{0:T(1024)(128)(4,1)S(1)} %get-tuple-element.189), kind=kLoop, calls=%fused_computation.43 | loop fusion | flops 9437184 | bytes 2369536 | tf_op jit(solution)/shard_map/convert_element_type | solution.py:342
  14.8 5.2 %conditional.4 = ((f32[96,1024]{1,0:T(8,128)}, f32[96,128]{1,0:T(8,128)S(1)})) conditional(s32[]{:T(128)} %convert_element_type.44, (f32[8,1024]{1,0:T(8,128)S(1)}, f32[48,1024]{1,0:T(8,128)S(1)}, f32[48,1024]{1,0:T(8,128)S(1)}, bf16[1152,1024]{1,0:T(8,128)(2,1)S(1)}) %tuple.88, (f32[8,1024]{1,0:T(8,128)S(1)}, f32[48,1024]{1,0:T(8,128)S(1)}, ...), branch_computations={%region_0.0_spmd, %region_1.0_spmd} | conditional | flops 454275072 | bytes 7847960 | solution.py:384
  14.8 2.3 %branch_0_fun.4 = (f32[96,1024]{1,0:T(8,128)}, f32[192,1024]{1,0:T(8,128)}) custom-call(f32[8,1024]{1,0:T(8,128)S(1)} %get-tuple-element.87.refs_0_, f32[48,1024]{1,0:T(8,128)S(1)} %get-tuple-element.88.refs_1_, f32[48,1024]{1,0:T(8,128)S(1)} %get-tuple-element.89.refs_2_), custom_call_target="tpu_custom_call" | custom-call | flops 983040 | bytes 1605632 | tf_op jit(solution)/shard_map/cond/branch_0_fun/pallas_call | solution.py:194
  17.1 2.1 %fusion = f32[192,1152]{1,0:T(8,128)S(1)} fusion(bf16[1152,1024]{1,0:T(8,128)(2,1)S(1)} %get-tuple-element.91, f32[192,1024]{1,0:T(8,128)} %get-tuple-element.90), kind=kOutput, calls=%fused_computation.1 | convolution fusion | flops 453181440 | bytes 4030464 | tf_op jit(solution)/shard_map/cond/branch_0_fun/dot_general | solution.py:347
  22.6 4.5 %collective-permute-done.3 = f32[96,128]{1,0:T(8,128)S(1)} collective-permute-done((f32[96,128]{1,0:T(8,128)S(1)}, f32[96,128]{1,0:T(8,128)S(1)}, u32[]{:S(2)}, u32[]{:S(2)}) %collective-permute-start.3) | collective-permute-done | bytes 49184 | tf_op jit(solution)/shard_map/ppermute | solution.py:300
  27.2 2.2 %collective-permute-done.2 = f32[96,1024]{1,0:T(8,128)} collective-permute-done((f32[96,1024]{1,0:T(8,128)}, f32[96,1024]{1,0:T(8,128)}, u32[]{:S(2)}, u32[]{:S(2)}) %collective-permute-start.2) | collective-permute-done | bytes 393248 | tf_op jit(solution)/shard_map/ppermute | solution.py:300
  29.4 6.5 %conditional.5 = (f32[96,1024]{1,0:T(8,128)}, f32[96,128]{1,0:T(8,128)S(1)}) conditional(s32[]{:T(128)} %convert_element_type.44, (f32[8,1024]{1,0:T(8,128)S(1)}, f32[48,1024]{1,0:T(8,128)S(1)}, f32[48,1024]{1,0:T(8,128)S(1)}, f32[96,1024]{1,0:T(8,128)}, f32[96,128]{1,0:T(8,128)S(1)}, /*index=5*/bf16[1152,1024]{1,0:T(8,128)(2,1)S(1)}) %tuple.89, ...), branch_computations={%region_2.0_spmd, %region_3.0_spmd} | conditional | flops 455405568 | bytes 8290320 | solution.py:389
  29.4 3.6 %branch_0_fun.5 = (f32[96,1024]{1,0:T(8,128)}, f32[192,1024]{1,0:T(8,128)}) custom-call(f32[8,1024]{1,0:T(8,128)S(1)} %get-tuple-element.95.refs_0_, f32[48,1024]{1,0:T(8,128)S(1)} %get-tuple-element.96.refs_1_, f32[48,1024]{1,0:T(8,128)S(1)} %get-tuple-element.97.refs_2_, f32[96,1024]{1,0:T(8,128)} %get-tuple-element.98.refs_3_, ...), custom_call_target="tpu_custom_call" | custom-call | flops 983040 | bytes 2048000 | tf_op jit(solution)/shard_map/cond/branch_0_fun/pallas_call | solution.py:194
  32.9 2.1 %fusion.2 = f32[192,1152]{1,0:T(8,128)S(1)} fusion(bf16[1152,1024]{1,0:T(8,128)(2,1)S(1)} %get-tuple-element.101, f32[192,1024]{1,0:T(8,128)} %get-tuple-element.100), kind=kOutput, calls=%fused_computation.4 | convolution fusion | flops 453181440 | bytes 4030464 | tf_op jit(solution)/shard_map/cond/branch_0_fun/dot_general | solution.py:347
  38.4 4.5 %collective-permute-done.5 = f32[96,128]{1,0:T(8,128)S(1)} collective-permute-done((f32[96,128]{1,0:T(8,128)S(1)}, f32[96,128]{1,0:T(8,128)S(1)}, u32[]{:S(2)}, u32[]{:S(2)}) %collective-permute-start.5) | collective-permute-done | bytes 49184 | tf_op jit(solution)/shard_map/ppermute | solution.py:300
  43.0 2.2 %collective-permute-done.4 = f32[96,1024]{1,0:T(8,128)} collective-permute-done((f32[96,1024]{1,0:T(8,128)}, f32[96,1024]{1,0:T(8,128)}, u32[]{:S(2)}, u32[]{:S(2)}) %collective-permute-start.4) | collective-permute-done | bytes 393248 | tf_op jit(solution)/shard_map/ppermute | solution.py:300
  45.2 6.5 %conditional.6 = (f32[96,1024]{1,0:T(8,128)}, f32[96,128]{1,0:T(8,128)S(1)}) conditional(s32[]{:T(128)} %convert_element_type.44, (f32[8,1024]{1,0:T(8,128)S(1)}, f32[48,1024]{1,0:T(8,128)S(1)}, f32[48,1024]{1,0:T(8,128)S(1)}, f32[96,1024]{1,0:T(8,128)}, f32[96,128]{1,0:T(8,128)S(1)}, /*index=5*/bf16[1152,1024]{1,0:T(8,128)(2,1)S(1)}) %tuple.90, ...), branch_computations={%region_4.0_spmd, %region_5.0_spmd} | conditional | flops 455405568 | bytes 8290320 | solution.py:389
  45.2 3.6 %branch_0_fun.6 = (f32[96,1024]{1,0:T(8,128)}, f32[192,1024]{1,0:T(8,128)}) custom-call(f32[8,1024]{1,0:T(8,128)S(1)} %get-tuple-element.110.refs_0_, f32[48,1024]{1,0:T(8,128)S(1)} %get-tuple-element.111.refs_1_, f32[48,1024]{1,0:T(8,128)S(1)} %get-tuple-element.112.refs_2_, f32[96,1024]{1,0:T(8,128)} %get-tuple-element.113.refs_3_, ...), custom_call_target="tpu_custom_call" | custom-call | flops 983040 | bytes 2048000 | tf_op jit(solution)/shard_map/cond/branch_0_fun/pallas_call | solution.py:194
  48.8 2.1 %fusion.11 = f32[192,1152]{1,0:T(8,128)S(1)} fusion(bf16[1152,1024]{1,0:T(8,128)(2,1)S(1)} %get-tuple-element.116, f32[192,1024]{1,0:T(8,128)} %get-tuple-element.115), kind=kOutput, calls=%fused_computation.18 | convolution fusion | flops 453181440 | bytes 4030464 | tf_op jit(solution)/shard_map/cond/branch_0_fun/dot_general | solution.py:347
  54.3 4.5 %collective-permute-done.7 = f32[96,128]{1,0:T(8,128)S(1)} collective-permute-done((f32[96,128]{1,0:T(8,128)S(1)}, f32[96,128]{1,0:T(8,128)S(1)}, u32[]{:S(2)}, u32[]{:S(2)}) %collective-permute-start.7) | collective-permute-done | bytes 49184 | tf_op jit(solution)/shard_map/ppermute | solution.py:300
  58.8 2.2 %collective-permute-done.6 = f32[96,1024]{1,0:T(8,128)} collective-permute-done((f32[96,1024]{1,0:T(8,128)}, f32[96,1024]{1,0:T(8,128)}, u32[]{:S(2)}, u32[]{:S(2)}) %collective-permute-start.6) | collective-permute-done | bytes 393248 | tf_op jit(solution)/shard_map/ppermute | solution.py:300
  61.0 1.6 %conditional.7 = (f32[1,96,1024]{2,1,0:T(8,128)S(1)}, f32[1,96,1024]{2,1,0:T(8,128)S(1)}, f32[1,96,1024]{2,1,0:T(8,128)S(1)}) conditional(s32[]{:T(128)} %convert_element_type.44, (f32[8,1024]{1,0:T(8,128)S(1)}, f32[48,1024]{1,0:T(8,128)S(1)}, f32[48,1024]{1,0:T(8,128)S(1)}, f32[96,1024]{1,0:T(8,128)}, f32[96,128]{1,0:T(8,128)S(1)}) %tuple.91, ...), branch_computations={%region_6.0_spmd, %region_7.0_spmd} | conditional | flops 455503872 | bytes 8192024 | solution.py:389
  61.0 1.6 %branch_0_fun.7 = f32[96,1024]{1,0:T(8,128)S(1)} custom-call(f32[8,1024]{1,0:T(8,128)S(1)} %get-tuple-element.125.refs_0_, f32[48,1024]{1,0:T(8,128)S(1)} %get-tuple-element.126.refs_1_, f32[48,1024]{1,0:T(8,128)S(1)} %get-tuple-element.127.refs_2_, f32[96,1024]{1,0:T(8,128)} %get-tuple-element.128.refs_3_, f32[96,128]{1,0:T(8,128)S(1)} %get-tuple-element.129.refs_4_), custom_call_target="tpu_custom_call" | custom-call | flops 983040 | bytes 1261568 | tf_op jit(solution)/shard_map/cond/branch_0_fun/pallas_call | solution.py:194
  63.1 2.8 %collective-permute-done.8 = f32[3,96,1024]{2,1,0:T(8,128)S(1)} collective-permute-done((f32[3,96,1024]{2,1,0:T(8,128)S(1)}, f32[3,96,1024]{2,1,0:T(8,128)S(1)}, u32[]{:S(2)}, u32[]{:S(2)}) %collective-permute-start.8) | collective-permute-done | bytes 1179680 | tf_op jit(solution)/shard_map/ppermute | solution.py:393
  69.7 15.6 %all-to-all-start = ((f32[128,1,128]{2,1,0:T(1,128)}), f32[128,1,128]{2,1,0:T(1,128)S(1)}, u32[]{:S(2)}, u32[]{:S(2)}) async-start(f32[128,1,128]{2,1,0:T(1,128)} %bitcast.23), calls=%async_computation | async-start | bytes 131072 | tf_op jit(solution)/shard_map/all_to_all | solution.py:422
  86.0 9.9 %all-to-all-done = f32[128,1,128]{2,1,0:T(1,128)S(1)} async-done(((f32[128,1,128]{2,1,0:T(1,128)}), f32[128,1,128]{2,1,0:T(1,128)S(1)}, u32[]{:S(2)}, u32[]{:S(2)}) %all-to-all-start) | async-done | bytes 65568 | tf_op jit(solution)/shard_map/all_to_all | solution.py:422
  (56 shorter events, 19.0 us)
Async XLA Ops:
  0.6 10.3 %copy-start = (f32[16,1024]{1,0:T(8,128)S(1)}, f32[16,1024]{1,0:T(8,128)}, u32[]{:S(2)}) copy-start(f32[16,1024]{1,0:T(8,128)} %param.18) | copy-start | bytes 196612
  0.6 14.1 %copy-start.1 = (f32[48,1024]{1,0:T(8,128)S(1)}, f32[48,1024]{1,0:T(8,128)}, u32[]{:S(2)}) copy-start(f32[48,1024]{1,0:T(8,128)} %param.16) | copy-start | bytes 589828
  0.7 14.1 %copy-start.2 = (f32[48,1024]{1,0:T(8,128)S(1)}, f32[48,1024]{1,0:T(8,128)}, u32[]{:S(2)}) copy-start(f32[48,1024]{1,0:T(8,128)} %param.17) | copy-start | bytes 589828
  0.7 14.1 %collective-permute-start.1 = (f32[48,1024]{1,0:T(8,128)}, f32[48,1024]{1,0:T(8,128)S(1)}, u32[]{:S(2)}, u32[]{:S(2)}) collective-permute-start(f32[48,1024]{1,0:T(8,128)} %param.16), channel_id=1, source_target_pairs={{1,0},{3,2},{5,4},{7,6},{9,8},{11,10},{13,12},{15,14},{17,16},{19,... | collective-permute-start | bytes 589832 | tf_op jit(solution)/shard_map/ppermute | solution.py:333
  5.9 8.9 %collective-permute-start = (f32[48,1024]{1,0:T(8,128)}, f32[48,1024]{1,0:T(8,128)S(1)}, u32[]{:S(2)}, u32[]{:S(2)}) collective-permute-start(f32[48,1024]{1,0:T(8,128)} %param.17), channel_id=1, source_target_pairs={{0,1},{2,3},{4,5},{6,7},{8,9},{10,11},{12,13},{14,15},{16,17},{18,... | collective-permute-start | bytes 589832 | tf_op jit(solution)/shard_map/ppermute | solution.py:334
  20.0 9.4 %collective-permute-start.2 = (f32[96,1024]{1,0:T(8,128)}, f32[96,1024]{1,0:T(8,128)}, u32[]{:S(2)}, u32[]{:S(2)}) collective-permute-start(f32[96,1024]{1,0:T(8,128)} %get-tuple-element.149), channel_id=1, source_target_pairs={{0,64},{2,66},{4,68},{6,70},{8,72},{10,74},{12,76},{14,78},{16,80}... | collective-permute-start | bytes 1179656 | tf_op jit(solution)/shard_map/ppermute | solution.py:300
  21.3 5.8 %collective-permute-start.3 = (f32[96,128]{1,0:T(8,128)S(1)}, f32[96,128]{1,0:T(8,128)S(1)}, u32[]{:S(2)}, u32[]{:S(2)}) collective-permute-start(f32[96,128]{1,0:T(8,128)S(1)} %get-tuple-element.150), channel_id=1, source_target_pairs={{0,66},{2,68},{4,70},{6,72},{8,74},{10,76},{12,78},{14,80},{16,82}... | collective-permute-start | bytes 147464 | tf_op jit(solution)/shard_map/ppermute | solution.py:300
  35.9 9.4 %collective-permute-start.4 = (f32[96,1024]{1,0:T(8,128)}, f32[96,1024]{1,0:T(8,128)}, u32[]{:S(2)}, u32[]{:S(2)}) collective-permute-start(f32[96,1024]{1,0:T(8,128)} %get-tuple-element.151), channel_id=1, source_target_pairs={{0,64},{2,66},{4,68},{6,70},{8,72},{10,74},{12,76},{14,78},{16,80}... | collective-permute-start | bytes 1179656 | tf_op jit(solution)/shard_map/ppermute | solution.py:300
  37.1 5.8 %collective-permute-start.5 = (f32[96,128]{1,0:T(8,128)S(1)}, f32[96,128]{1,0:T(8,128)S(1)}, u32[]{:S(2)}, u32[]{:S(2)}) collective-permute-start(f32[96,128]{1,0:T(8,128)S(1)} %get-tuple-element.152), channel_id=1, source_target_pairs={{0,66},{2,68},{4,70},{6,72},{8,74},{10,76},{12,78},{14,80},{16,82}... | collective-permute-start | bytes 147464 | tf_op jit(solution)/shard_map/ppermute | solution.py:300
  51.7 9.4 %collective-permute-start.6 = (f32[96,1024]{1,0:T(8,128)}, f32[96,1024]{1,0:T(8,128)}, u32[]{:S(2)}, u32[]{:S(2)}) collective-permute-start(f32[96,1024]{1,0:T(8,128)} %get-tuple-element.153), channel_id=1, source_target_pairs={{0,64},{2,66},{4,68},{6,70},{8,72},{10,74},{12,76},{14,78},{16,80}... | collective-permute-start | bytes 1179656 | tf_op jit(solution)/shard_map/ppermute | solution.py:300
  53.0 5.8 %collective-permute-start.7 = (f32[96,128]{1,0:T(8,128)S(1)}, f32[96,128]{1,0:T(8,128)S(1)}, u32[]{:S(2)}, u32[]{:S(2)}) collective-permute-start(f32[96,128]{1,0:T(8,128)S(1)} %get-tuple-element.154), channel_id=1, source_target_pairs={{0,66},{2,68},{4,70},{6,72},{8,74},{10,76},{12,78},{14,80},{16,82}... | collective-permute-start | bytes 147464 | tf_op jit(solution)/shard_map/ppermute | solution.py:300
  62.8 3.1 %collective-permute-start.8 = (f32[3,96,1024]{2,1,0:T(8,128)S(1)}, f32[3,96,1024]{2,1,0:T(8,128)S(1)}, u32[]{:S(2)}, u32[]{:S(2)}) collective-permute-start(f32[3,96,1024]{2,1,0:T(8,128)S(1)} %constant_dynamic-update-slice_fusion.6), channel_id=1, source_target_pairs={{0,1},{1,0},{2,3},{3,2},{4,5},{5,4},{6,7},{7,6},{8,9},{9,8},{10,11... | collective-permute-start | bytes 3538952 | tf_op jit(solution)/shard_map/ppermute | solution.py:393
  66.1 1.0 %copy-start.3 = (f32[128,1024]{1,0:T(8,128)S(1)}, f32[128,1024]{1,0:T(8,128)}, u32[]{:S(2)}) copy-start(f32[128,1024]{1,0:T(8,128)} %get-tuple-element.187) | copy-start | bytes 1572868
  69.7 26.1 %all-to-all-start = ((f32[128,1,128]{2,1,0:T(1,128)}), f32[128,1,128]{2,1,0:T(1,128)S(1)}, u32[]{:S(2)}, u32[]{:S(2)}) async-start(f32[128,1,128]{2,1,0:T(1,128)} %bitcast.23), calls=%async_computation | async-start | bytes 131072 | tf_op jit(solution)/shard_map/all_to_all | solution.py:422

commit v6 on v4

--- a/solution.py
+++ b/solution.py
@@ -97,24 +97,31 @@
     )(retain_row, drive)
 
 
+def split_pair(value):
+    high = value.astype(jnp.bfloat16)
+    low = (value - high.astype(jnp.float32)).astype(jnp.bfloat16)
+    return jnp.concatenate([high, low], axis=0)
+
+
 def forward_kernel(*refs, has_inflow):
     if has_inflow:
-        coef_ref, product_ref, lateral_ref, out_ref, outlet_ref, inflow_ref = refs
+        coef_ref, upper_ref, side_ref, conf_ref, lateral_ref, out_ref, outlet_ref, inflow_ref = refs
     else:
         coef_ref, lateral_ref, out_ref, outlet_ref = refs
     steps = lateral_ref.shape[0]
     narrow = outlet_ref.shape[1]
     gain_now, gain_prev, gain_side = coef_ref[0:1, :], coef_ref[1:2, :], coef_ref[2:3, :]
     keep, live = coef_ref[3:4, :], coef_ref[4:5, :]
+    if has_inflow:
+        source = jnp.concatenate([upper_ref[...], side_ref[...]], axis=1)
+        product = jnp.dot(split_pair(source), conf_ref[...], preferred_element_type=jnp.float32)
+        inflow_ref[...] = product[:steps] + product[steps:]
 
     def advance(hour, carry):
         state, before = carry
         side_in = lateral_ref[pl.ds(hour, 1), :]
         if has_inflow:
-            now = product_ref[pl.ds(hour, 1), :]
-            for piece_at in range(1, PIECES):
-                now = now + product_ref[pl.ds(hour + piece_at * steps, 1), :]
-            inflow_ref[pl.ds(hour, 1), :] = now
+            now = inflow_ref[pl.ds(hour, 1), :]
             drive = (gain_now * now + gain_prev * before) + gain_side * side_in
         else:
             now = before
@@ -136,8 +143,10 @@
     if has_down:
         down_ref, side_ref = rest[0], rest[1]
         rest = rest[2:]
-    adj_ref = rest[0]
-    piece_ref = rest[1] if emit else None
+    if emit:
+        conf_ref, adj_ref, own_ref, spill_ref, work_ref = rest
+    else:
+        (adj_ref,) = rest
     steps = cot_ref.shape[0]
     gain_now, gain_prev = coef_ref[0:1, :], coef_ref[1:2, :]
     keep, live = coef_ref[3:4, :], coef_ref[4:5, :]
@@ -155,52 +164,64 @@
         state = keep * state + live * load
         adj_ref[pl.ds(hour, 1), :] = state
         if emit:
-            remainder = gain_now * state + gain_prev * later
-            for piece_at in range(PIECES):
-                piece = remainder.astype(jnp.bfloat16).astype(jnp.float32)
-                piece_ref[pl.ds(hour + piece_at * steps, 1), :] = piece
-                remainder = remainder - piece
+            work_ref[pl.ds(hour, 1), :] = gain_now * state + gain_prev * later
         return state, state
 
     zero = jnp.zeros_like(keep)
     lax.fori_loop(0, steps, advance, (zero, zero), unroll=8)
-
-
-def vmem_call(kernel, outs, *args):
+    if emit:
+        spread = jnp.dot(split_pair(work_ref[...]), conf_ref[...], preferred_element_type=jnp.float32)
+        width = own_ref.shape[1]
+        own_ref[...] = spread[:steps, :width] + spread[steps:, :width]
+        spill_ref[...] = spread[:steps, width:] + spread[steps:, width:]
+
+
+def vmem_call(kernel, outs, *args, scratch=()):
     steps, width = outs[0]
     return pl.pallas_call(
         kernel,
         out_shape=[jax.ShapeDtypeStruct(shape, jnp.float32) for shape in outs],
         in_specs=[pl.BlockSpec(memory_space=pltpu.VMEM)] * len(args),
         out_specs=[pl.BlockSpec(memory_space=pltpu.VMEM)] * len(outs),
+        scratch_shapes=[pltpu.VMEM(shape, jnp.float32) for shape in scratch],
         cost_estimate=pl.CostEstimate(
-            flops=10 * steps * width,
+            flops=10 * steps * width + 4 * steps * width * (width + width // 8),
             transcendentals=0,
-            bytes_accessed=4 * (sum(a.size for a in args) + sum(r * c for r, c in outs)),
+            bytes_accessed=sum(a.size * a.dtype.itemsize for a in args) + 4 * sum(r * c for r, c in outs),
         ),
     )(*args)
 
 
-def routed(coef, lateral_all, product=None):
+def routed(coef, lateral_all, upper=None, side=None, confluence=None):
     steps, width = lateral_all.shape
     narrow = width // 8
-    if product is None:
+    if upper is None:
         kernel = functools.partial(forward_kernel, has_inflow=False)
         flow, outlet = vmem_call(kernel, [(steps, width), (steps, narrow)], coef, lateral_all)
         return flow, outlet, None
     kernel = functools.partial(forward_kernel, has_inflow=True)
     return vmem_call(
-        kernel, [(steps, width), (steps, narrow), (steps, width)], coef, product, lateral_all
-    )
-
-
-def adjoined(coef, cotangent_all, down=None, side=None, emit=True):
+        kernel,
+        [(steps, width), (steps, narrow), (steps, width)],
+        coef, upper, side, confluence, lateral_all,
+    )
+
+
+def adjoined(coef, cotangent_all, down=None, side=None, confluence_t=None):
     steps, width = cotangent_all.shape
+    emit = confluence_t is not None
     kernel = functools.partial(backward_kernel, has_down=down is not None, emit=emit)
     args = (coef, cotangent_all) if down is None else (coef, cotangent_all, down, side)
-    outs = [(steps, width)] + ([(PIECES * steps, width)] if emit else [])
-    results = vmem_call(kernel, outs, *args)
-    return results[0], (results[1] if emit else None)
+    if not emit:
+        return vmem_call(kernel, [(steps, width)], *args)[0], None, None
+    adjoint, own, spill = vmem_call(
+        kernel,
+        [(steps, width), (steps, width), (steps, width // 8)],
+        *args,
+        confluence_t,
+        scratch=[(steps, width)],
+    )
+    return adjoint, own, spill
 
 
 def split_three(value):
@@ -321,44 +342,36 @@
             (source_ids == feeders[upslot][None, :]) & (upslot < feeder_count)[None, :]
         ).astype(jnp.float32)
     confluence = confluence.astype(jnp.bfloat16)
+    target_ids = lax.broadcasted_iota(jnp.int32, (reach_dev, reach_dev + outlets), 1)
+    confluence_t = jnp.zeros((reach_dev, reach_dev + outlets), jnp.float32)
+    for upslot in range(up_count):
+        confluence_t = confluence_t + (
+            (target_ids == feeders[upslot][:, None]) & (upslot < feeder_count)[:, None]
+        ).astype(jnp.float32)
+    confluence_t = confluence_t.astype(jnp.bfloat16)
     zero_flow = jnp.zeros((steps_all, reach_dev), jnp.float32)
-
-    def spread_of(pieces):
-        spread = joined_three(
-            lax.dot_general(
-                pieces.astype(jnp.bfloat16),
-                confluence,
-                (((1,), (1,)), ((), ())),
-                preferred_element_type=jnp.float32,
-            )
-        )
-        return spread[:, :reach_dev], spread[:, reach_dev:]
 
     def forward_first(operands):
         flow, outlet, unused = routed(coef, lateral_all)
         return flow, outlet, flow, zero_flow, lateral_all
 
     def backward_first(operands):
-        adjoint, pieces = adjoined(coef, cotangent_all)
-        own, side = spread_of(pieces)
+        adjoint, own, side = adjoined(coef, cotangent_all, confluence_t=confluence_t)
         return own, side, adjoint, zero_flow, zero_flow
 
     def forward_step(operands):
         upper, side = operands
-        source = jnp.concatenate([upper, side], axis=1)
-        product = jnp.dot(split_three(source), confluence, preferred_element_type=jnp.float32)
-        flow, outlet, inflow = routed(coef, lateral_all, product)
+        flow, outlet, inflow = routed(coef, lateral_all, upper, side, confluence)
         return flow, outlet, flow, inflow, lateral_all
 
     def backward_step(operands):
         upper, side = operands
-        adjoint, pieces = adjoined(coef, cotangent_all, upper, side)
-        own, side = spread_of(pieces)
+        adjoint, own, side = adjoined(coef, cotangent_all, upper, side, confluence_t)
         return own, side, adjoint, zero_flow, zero_flow
 
     def backward_last(operands):
         upper, side = operands
-        adjoint, unused = adjoined(coef, cotangent_all, upper, side, emit=False)
+        adjoint, unused, unused_side = adjoined(coef, cotangent_all, upper, side)
         return zero_flow, side, adjoint, zero_flow, zero_flow
 
     message, outlet_message, *kept = lax.cond(mine == 0, forward_first, backward_first, None)

time: 95.4 us -> 90.6 us (0.950)
  starting transfers between devices: 25.3 us -> 34.2 us
  matrix products: 8.89 us -> 2.01 us
  local copies, waits for them, and re-layouts: 8.4 us -> 4.26 us
  other arithmetic: 6.58 us -> 9.83 us
  waiting for transfers between devices: 33 us -> 30 us
  Pallas kernels: 10.8 us -> 8.12 us
    ppermute x1, starting transfers between devices: 0.09 us -> 8.09 us  [body(): other = lax.ppermute(kept, 'group', [(0, 1), (1, 0)])]
    dot_general x3 -> x0, matrix products: 6.18 us -> none  [spread_of(): lax.dot_general(pieces.astype(jnp.bfloat16), confluence, (((1,), (1,)), (...]
    pallas_call x4, Pallas kernels: 10.8 us -> 8.12 us  [vmem_call(): pl.pallas_call(kernel, out_shape=[jax.ShapeDtypeStruct(shape, jnp.float32...]
    ppermute x6, waiting for transfers between devices: 20.3 us -> 17.7 us  [both_ways(): return lax.ppermute(value, ('level', 'basin', 'group'), pairs)]
    slice x7 -> x1, local copies, waits for them, and re-layouts: 3.2 us -> 0.78 us  [body(): feeders[upslot][:, None]]
    convert_element_type x0 -> x1, other arithmetic: none -> 2.05 us  [body(): confluence_t = confluence_t.astype(jnp.bfloat16)]
    another operation x3, local copies, waits for them, and re-layouts: 1.83 us -> 0.09 us  [body(): kept = jnp.stack(kept, axis=0)]
    convert_element_type x1, other arithmetic: 1.86 us -> 3.3 us  [body(): confluence = confluence.astype(jnp.bfloat16)]
  transfers between devices with their start and end apart: 9 -> 9, of which waited for: 8 -> 7; matrix products, arithmetic and copies ran while one was open for 7% -> 11% of each run, Pallas kernels for 0% -> 0%
where the time goes in v6:
time: 90.6 us; the launch traced here: 90 us
  starting transfers between devices  34.2 us (38%)
  waiting for transfers between devices  30 us (33%)
  other arithmetic  9.83 us (11%)
  Pallas kernels  8.12 us (9%)
  local copies, waits for them, and re-layouts  4.26 us (5%)
  matrix products  2.01 us (2%)
  between operations  1.55 us (2%)
    ppermute x6, waiting for transfers between devices, both_ways(): return lax.ppermute(value, ('level', 'basin', 'group'), pairs)  17.7 us
    all_to_all x1, starting transfers between devices, body(): lax.all_to_all(replicated, ('level', 'basin'), 0, 0, tiled=True)  15.1 us
    all_to_all x1, waiting for transfers between devices, body(): lax.all_to_all(replicated, ('level', 'basin'), 0, 0, tiled=True)  9.85 us
    pallas_call x4, Pallas kernels, vmem_call(): pl.pallas_call(kernel, out_shape=[jax.ShapeDtypeStruct(shape, jnp.float32...  8.12 us
    ppermute x1, starting transfers between devices, body(): other = lax.ppermute(kept, 'group', [(0, 1), (1, 0)])  8.09 us
    ppermute x6, starting transfers between devices, both_ways(): return lax.ppermute(value, ('level', 'basin', 'group'), pairs)  7.72 us
    convert_element_type x1, other arithmetic, body(): confluence = confluence.astype(jnp.bfloat16)  3.3 us
    ppermute x1, starting transfers between devices, body(): lax.ppermute(jnp.where(mine == 0, cotangent, lateral), 'group', [(0, 1),...  3.29 us
  transfers between devices with their start and end apart: 9, of which 7 were waited for; matrix products, arithmetic and copies ran while one was open for 11% of the time, Pallas kernels for 0%

profile of v6, /device:TPU:1, one launch (start us, length us, event | category | flops | bytes accessed | tf_op | source)
XLA Modules:
  0.0 90.0 jit_solution(13244346537066054043)
XLA Ops:
  1.6 3.3 %collective-permute-start = (f32[48,1024]{1,0:T(8,128)S(1)}, f32[48,1024]{1,0:T(8,128)}, u32[]{:S(2)}, u32[]{:S(2)}) collective-permute-start(f32[48,1024]{1,0:T(8,128)S(1)} %broadcast_select_fusion.1), channel_id=1, source_target_pairs={{0,1},{1,0},{2,3},{3,2},{4,5},{5,4},{6,7},{7,6},{8,9},{9,8},{10,11... | collective-permute-start | bytes 589832 | tf_op jit(solution)/shard_map/ppermute | solution.py:329
  7.9 1.1 %fusion.5 = f32[1024,2]{0,1:T(2,128)S(1)} fusion(f32[1024,128]{0,1:T(8,128)S(1)} %get-tuple-element.161, f32[16,1024]{1,0:T(8,128)S(1)} %copy-done, f32[128,2,16]{0,1,2:T(2,128)S(1)} %bitcast.64), kind=kOutput, calls=%fused_computation.12 | convolution fusion | flops 50853888 | bytes 614400 | tf_op jit(solution)/shard_map/dot_general | solution.py:311
  9.0 2.0 %add_convert_fusion.1 = bf16[1024,1152]{1,0:T(8,128)(2,1)S(1)} fusion(s32[1024]{0:T(1024)S(1)} %bitcast.57, s32[1024]{0:T(1024)S(1)} %bitcast.55, pred[1024]{0:T(1024)(128)(4,1)S(1)} %get-tuple-element.163, pred[1024]{0:T(1024)(128)(4,1)S(1)} %get-tuple-element.162), kind=kLoop, calls=%fused_computation.3 | loop fusion | flops 9437184 | bytes 2369536 | tf_op jit(solution)/shard_map/convert_element_type | solution.py:351
  11.2 1.3 %maximum_select_fusion = f32[96,1024]{1,0:T(8,128)S(1)} fusion(f32[48,1024]{1,0:T(8,128)} %collective-permute-done, f32[48,1024]{1,0:T(8,128)} %param.16, f32[48,1024]{1,0:T(8,128)} %param.17, pred[]{:T(512)S(6)} %eq.58), kind=kLoop, calls=%fused_computation.32 | loop fusion | flops 294912 | bytes 983041 | tf_op jit(solution)/shard_map/jit(_where)/select_n | solution.py:330
  12.5 1.7 %conditional.4 = ((f32[96,1024]{1,0:T(8,128)}, f32[96,128]{1,0:T(8,128)S(1)})) conditional(s32[]{:T(128)} %convert_element_type.41, (f32[8,1024]{1,0:T(8,128)S(1)}, f32[96,1024]{1,0:T(8,128)S(1)}, bf16[1024,1152]{1,0:T(8,128)(2,1)S(1)}) %tuple.45, (f32[8,1024]{1,0:T(8,128)S(1)}, f32[96,1024]{1,0:T(8,128)S(1)}) %tuple.46), branch_computations={%region_0.1_spmd, %region_1.2_spmd} | conditional | flops 453967872 | bytes 3620888 | solution.py:377
  12.5 1.7 %branch_0_fun.4 = (f32[96,1024]{1,0:T(8,128)}, f32[96,1024]{1,0:T(8,128)}, f32[96,128]{1,0:T(8,128)S(1)}) custom-call(f32[8,1024]{1,0:T(8,128)S(1)} %get-tuple-element.71.refs_0_, f32[96,1024]{1,0:T(8,128)S(1)} %get-tuple-element.72.refs_1_, bf16[1024,1152]{1,0:T(8,128)(2,1)S(1)} %get-tuple-element.73.refs_2_), custom_call_target="tpu_custom_call" | custom-call | flops 453967872 | bytes 3620864 | tf_op jit(solution)/shard_map/cond/branch_0_fun/pallas_call | solution.py:181
  14.2 1.3 %collective-permute-start.2 = (f32[96,128]{1,0:T(8,128)S(1)}, f32[96,128]{1,0:T(8,128)S(1)}, u32[]{:S(2)}, u32[]{:S(2)}) collective-permute-start(f32[96,128]{1,0:T(8,128)S(1)} %get-tuple-element.129), channel_id=1, source_target_pairs={{0,66},{2,68},{4,70},{6,72},{8,74},{10,76},{12,78},{14,80},{16,82}... | collective-permute-start | bytes 147464 | tf_op jit(solution)/shard_map/ppermute | solution.py:296
  15.5 1.3 %collective-permute-start.1 = (f32[96,1024]{1,0:T(8,128)}, f32[96,1024]{1,0:T(8,128)}, u32[]{:S(2)}, u32[]{:S(2)}) collective-permute-start(f32[96,1024]{1,0:T(8,128)} %get-tuple-element.128), channel_id=1, source_target_pairs={{0,64},{2,66},{4,68},{6,70},{8,72},{10,74},{12,76},{14,78},{16,80}... | collective-permute-start | bytes 1179656 | tf_op jit(solution)/shard_map/ppermute | solution.py:296
  16.8 3.3 %add_convert_fusion = bf16[1152,1024]{1,0:T(8,128)(2,1)} fusion(s32[1024]{0:T(1024)S(1)} %bitcast.58, s32[1024]{0:T(1024)S(1)} %bitcast.56, pred[1024]{0:T(1024)(128)(4,1)S(1)} %get-tuple-element.163, pred[1024]{0:T(1024)(128)(4,1)S(1)} %get-tuple-element.162), kind=kLoop, calls=%fused_computation | loop fusion | flops 9437184 | bytes 2369536 | tf_op jit(solution)/shard_map/convert_element_type | solution.py:344
  20.1 4.2 %collective-permute-done.1 = f32[96,1024]{1,0:T(8,128)} collective-permute-done((f32[96,1024]{1,0:T(8,128)}, f32[96,1024]{1,0:T(8,128)}, u32[]{:S(2)}, u32[]{:S(2)}) %collective-permute-start.1) | collective-permute-done | bytes 393248 | tf_op jit(solution)/shard_map/ppermute | solution.py:296
  24.3 2.9 %conditional.5 = (f32[96,1024]{1,0:T(8,128)}, f32[96,128]{1,0:T(8,128)S(1)}) conditional(s32[]{:T(128)} %convert_element_type.41, (f32[8,1024]{1,0:T(8,128)S(1)}, f32[96,1024]{1,0:T(8,128)S(1)}, f32[96,1024]{1,0:T(8,128)}, f32[96,128]{1,0:T(8,128)S(1)}, bf16[1024,1152]{1,0:T(8,128)(2,1)S(1)}) %tuple.47, (f32[8,1024]{1,0:T(8,128)S(1)}, ...), branch_computations={%region_2.3_spmd, %region_3.4_spmd} | conditional | flops 453967872 | bytes 4063248 | solution.py:382
  24.3 2.9 %branch_0_fun.5 = (f32[96,1024]{1,0:T(8,128)}, f32[96,1024]{1,0:T(8,128)}, f32[96,128]{1,0:T(8,128)S(1)}) custom-call(f32[8,1024]{1,0:T(8,128)S(1)} %get-tuple-element.78.refs_0_, f32[96,1024]{1,0:T(8,128)S(1)} %get-tuple-element.79.refs_1_, f32[96,1024]{1,0:T(8,128)} %get-tuple-element.80.refs_2_, f32[96,128]{1,0:T(8,128)S(1)} %get-tuple-element.81.refs_3_, ...), custom_call_target="tpu_custom_call" | custom-call | flops 453967872 | bytes 4063232 | tf_op jit(solution)/shard_map/cond/branch_0_fun/pallas_call | solution.py:181
  27.3 1.3 %collective-permute-start.3 = (f32[96,1024]{1,0:T(8,128)}, f32[96,1024]{1,0:T(8,128)}, u32[]{:S(2)}, u32[]{:S(2)}) collective-permute-start(f32[96,1024]{1,0:T(8,128)} %get-tuple-element.130), channel_id=1, source_target_pairs={{0,64},{2,66},{4,68},{6,70},{8,72},{10,74},{12,76},{14,78},{16,80}... | collective-permute-start | bytes 1179656 | tf_op jit(solution)/shard_map/ppermute | solution.py:296
  28.5 1.3 %collective-permute-start.4 = (f32[96,128]{1,0:T(8,128)S(1)}, f32[96,128]{1,0:T(8,128)S(1)}, u32[]{:S(2)}, u32[]{:S(2)}) collective-permute-start(f32[96,128]{1,0:T(8,128)S(1)} %get-tuple-element.131), channel_id=1, source_target_pairs={{0,66},{2,68},{4,70},{6,72},{8,74},{10,76},{12,78},{14,80},{16,82}... | collective-permute-start | bytes 147464 | tf_op jit(solution)/shard_map/ppermute | solution.py:296
  29.8 6.1 %collective-permute-done.4 = f32[96,128]{1,0:T(8,128)S(1)} collective-permute-done((f32[96,128]{1,0:T(8,128)S(1)}, f32[96,128]{1,0:T(8,128)S(1)}, u32[]{:S(2)}, u32[]{:S(2)}) %collective-permute-start.4) | collective-permute-done | bytes 49184 | tf_op jit(solution)/shard_map/ppermute | solution.py:296
  36.6 2.9 %conditional.6 = (f32[96,1024]{1,0:T(8,128)}, f32[96,128]{1,0:T(8,128)S(1)}) conditional(s32[]{:T(128)} %convert_element_type.41, (f32[8,1024]{1,0:T(8,128)S(1)}, f32[96,1024]{1,0:T(8,128)S(1)}, f32[96,1024]{1,0:T(8,128)}, f32[96,128]{1,0:T(8,128)S(1)}, bf16[1024,1152]{1,0:T(8,128)(2,1)S(1)}) %tuple.49, (f32[8,1024]{1,0:T(8,128)S(1)}, ...), branch_computations={%region_4.5_spmd, %region_5.6_spmd} | conditional | flops 453967872 | bytes 4063248 | solution.py:382
  36.6 2.9 %branch_0_fun.6 = (f32[96,1024]{1,0:T(8,128)}, f32[96,1024]{1,0:T(8,128)}, f32[96,128]{1,0:T(8,128)S(1)}) custom-call(f32[8,1024]{1,0:T(8,128)S(1)} %get-tuple-element.92.refs_0_, f32[96,1024]{1,0:T(8,128)S(1)} %get-tuple-element.93.refs_1_, f32[96,1024]{1,0:T(8,128)} %get-tuple-element.94.refs_2_, f32[96,128]{1,0:T(8,128)S(1)} %get-tuple-element.95.refs_3_, ...), custom_call_target="tpu_custom_call" | custom-call | flops 453967872 | bytes 4063232 | tf_op jit(solution)/shard_map/cond/branch_0_fun/pallas_call | solution.py:181
  39.5 1.3 %collective-permute-start.5 = (f32[96,1024]{1,0:T(8,128)}, f32[96,1024]{1,0:T(8,128)S(1)}, u32[]{:S(2)}, u32[]{:S(2)}) collective-permute-start(f32[96,1024]{1,0:T(8,128)} %get-tuple-element.132), channel_id=1, source_target_pairs={{0,64},{2,66},{4,68},{6,70},{8,72},{10,74},{12,76},{14,78},{16,80}... | collective-permute-start | bytes 1179656 | tf_op jit(solution)/shard_map/ppermute | solution.py:296
  40.8 1.3 %collective-permute-start.6 = (f32[96,128]{1,0:T(8,128)S(1)}, f32[96,128]{1,0:T(8,128)S(1)}, u32[]{:S(2)}, u32[]{:S(2)}) collective-permute-start(f32[96,128]{1,0:T(8,128)S(1)} %get-tuple-element.133), channel_id=1, source_target_pairs={{0,66},{2,68},{4,70},{6,72},{8,74},{10,76},{12,78},{14,80},{16,82}... | collective-permute-start | bytes 147464 | tf_op jit(solution)/shard_map/ppermute | solution.py:296
  42.1 6.4 %collective-permute-done.6 = f32[96,128]{1,0:T(8,128)S(1)} collective-permute-done((f32[96,128]{1,0:T(8,128)S(1)}, f32[96,128]{1,0:T(8,128)S(1)}, u32[]{:S(2)}, u32[]{:S(2)}) %collective-permute-start.6) | collective-permute-done | bytes 49184 | tf_op jit(solution)/shard_map/ppermute | solution.py:296
  49.5 8.1 %collective-permute-start.7 = (f32[3,96,1024]{2,1,0:T(8,128)S(1)}, f32[3,96,1024]{2,1,0:T(8,128)S(1)}, u32[]{:S(2)}, u32[]{:S(2)}) collective-permute-start(f32[3,96,1024]{2,1,0:T(8,128)S(1)} %constant_dynamic-update-slice_fusion), channel_id=1, source_target_pairs={{0,1},{1,0},{2,3},{3,2},{4,5},{5,4},{6,7},{7,6},{8,9},{9,8},{10,11... | collective-permute-start | bytes 3538952 | tf_op jit(solution)/shard_map/ppermute | solution.py:386
  57.6 2.5 %collective-permute-done.7 = f32[3,96,1024]{2,1,0:T(8,128)S(1)} collective-permute-done((f32[3,96,1024]{2,1,0:T(8,128)S(1)}, f32[3,96,1024]{2,1,0:T(8,128)S(1)}, u32[]{:S(2)}, u32[]{:S(2)}) %collective-permute-start.7) | collective-permute-done | bytes 1179680 | tf_op jit(solution)/shard_map/ppermute | solution.py:386
  63.3 15.1 %all-to-all-start = ((f32[128,1,128]{2,1,0:T(1,128)}), f32[128,1,128]{2,1,0:T(1,128)S(1)}, u32[]{:S(2)}, u32[]{:S(2)}) async-start(f32[128,1,128]{2,1,0:T(1,128)} %bitcast.23), calls=%async_computation | async-start | bytes 131072 | tf_op jit(solution)/shard_map/all_to_all | solution.py:415
  79.2 9.8 %all-to-all-done = f32[128,1,128]{2,1,0:T(1,128)S(1)} async-done(((f32[128,1,128]{2,1,0:T(1,128)}), f32[128,1,128]{2,1,0:T(1,128)S(1)}, u32[]{:S(2)}, u32[]{:S(2)}) %all-to-all-start) | async-done | bytes 65568 | tf_op jit(solution)/shard_map/all_to_all | solution.py:415
  (41 shorter events, 10.5 us)
Async XLA Ops:
  0.6 7.2 %copy-start = (f32[16,1024]{1,0:T(8,128)S(1)}, f32[16,1024]{1,0:T(8,128)}, u32[]{:S(2)}) copy-start(f32[16,1024]{1,0:T(8,128)} %param.18) | copy-start | bytes 196612
  0.6 7.2 %copy-start.1 = (f32[128,16,2]{0,2,1:T(2,128)S(1)}, f32[128,16,2]{0,2,1:T(2,128)}, u32[]{:S(2)}) copy-start(f32[128,16,2]{0,2,1:T(2,128)} %param.23) | copy-start | bytes 49156
  1.6 9.5 %collective-permute-start = (f32[48,1024]{1,0:T(8,128)S(1)}, f32[48,1024]{1,0:T(8,128)}, u32[]{:S(2)}, u32[]{:S(2)}) collective-permute-start(f32[48,1024]{1,0:T(8,128)S(1)} %broadcast_select_fusion.1), channel_id=1, source_target_pairs={{0,1},{1,0},{2,3},{3,2},{4,5},{5,4},{6,7},{7,6},{8,9},{9,8},{10,11... | collective-permute-start | bytes 589832 | tf_op jit(solution)/shard_map/ppermute | solution.py:329
  14.2 5.9 %collective-permute-start.2 = (f32[96,128]{1,0:T(8,128)S(1)}, f32[96,128]{1,0:T(8,128)S(1)}, u32[]{:S(2)}, u32[]{:S(2)}) collective-permute-start(f32[96,128]{1,0:T(8,128)S(1)} %get-tuple-element.129), channel_id=1, source_target_pairs={{0,66},{2,68},{4,70},{6,72},{8,74},{10,76},{12,78},{14,80},{16,82}... | collective-permute-start | bytes 147464 | tf_op jit(solution)/shard_map/ppermute | solution.py:296
  15.5 8.8 %collective-permute-start.1 = (f32[96,1024]{1,0:T(8,128)}, f32[96,1024]{1,0:T(8,128)}, u32[]{:S(2)}, u32[]{:S(2)}) collective-permute-start(f32[96,1024]{1,0:T(8,128)} %get-tuple-element.128), channel_id=1, source_target_pairs={{0,64},{2,66},{4,68},{6,70},{8,72},{10,74},{12,76},{14,78},{16,80}... | collective-permute-start | bytes 1179656 | tf_op jit(solution)/shard_map/ppermute | solution.py:296
  27.3 9.4 %collective-permute-start.3 = (f32[96,1024]{1,0:T(8,128)}, f32[96,1024]{1,0:T(8,128)}, u32[]{:S(2)}, u32[]{:S(2)}) collective-permute-start(f32[96,1024]{1,0:T(8,128)} %get-tuple-element.130), channel_id=1, source_target_pairs={{0,64},{2,66},{4,68},{6,70},{8,72},{10,74},{12,76},{14,78},{16,80}... | collective-permute-start | bytes 1179656 | tf_op jit(solution)/shard_map/ppermute | solution.py:296
  28.5 7.4 %collective-permute-start.4 = (f32[96,128]{1,0:T(8,128)S(1)}, f32[96,128]{1,0:T(8,128)S(1)}, u32[]{:S(2)}, u32[]{:S(2)}) collective-permute-start(f32[96,128]{1,0:T(8,128)S(1)} %get-tuple-element.131), channel_id=1, source_target_pairs={{0,66},{2,68},{4,70},{6,72},{8,74},{10,76},{12,78},{14,80},{16,82}... | collective-permute-start | bytes 147464 | tf_op jit(solution)/shard_map/ppermute | solution.py:296
  39.5 9.2 %collective-permute-start.5 = (f32[96,1024]{1,0:T(8,128)}, f32[96,1024]{1,0:T(8,128)S(1)}, u32[]{:S(2)}, u32[]{:S(2)}) collective-permute-start(f32[96,1024]{1,0:T(8,128)} %get-tuple-element.132), channel_id=1, source_target_pairs={{0,64},{2,66},{4,68},{6,70},{8,72},{10,74},{12,76},{14,78},{16,80}... | collective-permute-start | bytes 1179656 | tf_op jit(solution)/shard_map/ppermute | solution.py:296
  40.8 7.7 %collective-permute-start.6 = (f32[96,128]{1,0:T(8,128)S(1)}, f32[96,128]{1,0:T(8,128)S(1)}, u32[]{:S(2)}, u32[]{:S(2)}) collective-permute-start(f32[96,128]{1,0:T(8,128)S(1)} %get-tuple-element.133), channel_id=1, source_target_pairs={{0,66},{2,68},{4,70},{6,72},{8,74},{10,76},{12,78},{14,80},{16,82}... | collective-permute-start | bytes 147464 | tf_op jit(solution)/shard_map/ppermute | solution.py:296
  49.5 10.6 %collective-permute-start.7 = (f32[3,96,1024]{2,1,0:T(8,128)S(1)}, f32[3,96,1024]{2,1,0:T(8,128)S(1)}, u32[]{:S(2)}, u32[]{:S(2)}) collective-permute-start(f32[3,96,1024]{2,1,0:T(8,128)S(1)} %constant_dynamic-update-slice_fusion), channel_id=1, source_target_pairs={{0,1},{1,0},{2,3},{3,2},{4,5},{5,4},{6,7},{7,6},{8,9},{9,8},{10,11... | collective-permute-start | bytes 3538952 | tf_op jit(solution)/shard_map/ppermute | solution.py:386
  63.3 25.7 %all-to-all-start = ((f32[128,1,128]{2,1,0:T(1,128)}), f32[128,1,128]{2,1,0:T(1,128)S(1)}, u32[]{:S(2)}, u32[]{:S(2)}) async-start(f32[128,1,128]{2,1,0:T(1,128)} %bitcast.23), calls=%async_computation | async-start | bytes 131072 | tf_op jit(solution)/shard_map/all_to_all | solution.py:415

commit v7 on v6

--- a/solution.py
+++ b/solution.py
@@ -292,8 +292,10 @@
 
 
 def both_ways(value, side_steps):
-    pairs = linear_pairs(1, side_steps, 0) + linear_pairs(-1, -side_steps, 1)
-    return lax.ppermute(value, ("level", "basin", "group"), pairs)
+    axes = ("level", "basin", "group")
+    upward = lax.ppermute(value, axes, linear_pairs(1, side_steps, 0))
+    downward = lax.ppermute(value, axes, linear_pairs(-1, -side_steps, 1))
+    return jnp.where(lax.axis_index("group") == 0, upward, downward)
 
 
 def body(lateral, cotangent, attributes, region, feeders, feeder_count, live_blocks, net_weight):

time: 90.6 us -> 92.8 us (1.024)
  Pallas kernels: 8.12 us -> 11.8 us
  local copies, waits for them, and re-layouts: 4.26 us -> 7.67 us
  starting transfers between devices: 34.2 us -> 31.7 us
  waiting for transfers between devices: 30 us -> 28 us
    ppermute x1, starting transfers between devices: 8.09 us -> 1.1 us  [body(): other = lax.ppermute(kept, 'group', [(0, 1), (1, 0)])]
    ppermute x6 -> x12, starting transfers between devices: 7.72 us -> 11.8 us  [the longest x6 7.72 us: both_ways(): downward = lax.ppermute(value, axes, linear_pairs(-1, -side_steps, 1))]
    pallas_call x4, Pallas kernels: 8.12 us -> 11.8 us  [vmem_call(): pl.pallas_call(kernel, out_shape=[jax.ShapeDtypeStruct(shape, jnp.float32...]
    unnamed x7 -> x13, local copies, waits for them, and re-layouts: 0.76 us -> 3.4 us
    ppermute x6 -> x12, waiting for transfers between devices: 17.7 us -> 15.7 us  [the longest x6 15.7 us: both_ways(): downward = lax.ppermute(value, axes, linear_pairs(-1, -side_steps, 1))]
    convert_element_type x1, other arithmetic: 3.3 us -> 1.86 us  [body(): confluence = confluence.astype(jnp.bfloat16)]
    select_n x1, other arithmetic: 1.27 us -> 0.04 us  [body(): jnp.where(mine == 0, jnp.concatenate([lateral, arrived], axis=0), jnp.con...]
    convert_element_type x1, other arithmetic: 2.05 us -> 3.08 us  [body(): confluence_t = confluence_t.astype(jnp.bfloat16)]
  transfers between devices with their start and end apart: 9 -> 15, of which waited for: 7 -> 5; matrix products, arithmetic and copies ran while one was open for 11% -> 11% of each run, Pallas kernels for 0% -> 0%
where the time goes in v7:
time: 92.8 us; the launch traced here: 92.1 us
  starting transfers between devices  31.7 us (34%)
  waiting for transfers between devices  28 us (30%)
  Pallas kernels  11.8 us (13%)
  other arithmetic  9.16 us (10%)
  local copies, waits for them, and re-layouts  7.67 us (8%)
  matrix products  1.99 us (2%)
  between operations  1.68 us (2%)
    ppermute x6, waiting for transfers between devices, both_ways(): downward = lax.ppermute(value, axes, linear_pairs(-1, -side_steps, 1))  15.7 us
    all_to_all x1, starting transfers between devices, body(): lax.all_to_all(replicated, ('level', 'basin'), 0, 0, tiled=True)  15.5 us
    pallas_call x4, Pallas kernels, vmem_call(): pl.pallas_call(kernel, out_shape=[jax.ShapeDtypeStruct(shape, jnp.float32...  11.8 us
    all_to_all x1, waiting for transfers between devices, body(): lax.all_to_all(replicated, ('level', 'basin'), 0, 0, tiled=True)  9.85 us
    ppermute x6, starting transfers between devices, both_ways(): downward = lax.ppermute(value, axes, linear_pairs(-1, -side_steps, 1))  7.72 us
    ppermute x6, starting transfers between devices, both_ways(): upward = lax.ppermute(value, axes, linear_pairs(1, side_steps, 0))  4.05 us
    unnamed x13, local copies, waits for them, and re-layouts  3.4 us
    ppermute x1, starting transfers between devices, body(): lax.ppermute(jnp.where(mine == 0, cotangent, lateral), 'group', [(0, 1),...  3.29 us
  transfers between devices with their start and end apart: 15, of which 5 were waited for; matrix products, arithmetic and copies ran while one was open for 11% of the time, Pallas kernels for 0%

profile of v7, /device:TPU:1, one launch (start us, length us, event | category | flops | bytes accessed | tf_op | source)
XLA Modules:
  0.0 92.1 jit_solution(4203183682967024127)
XLA Ops:
  1.6 3.3 %collective-permute-start = (f32[48,1024]{1,0:T(8,128)S(1)}, f32[48,1024]{1,0:T(8,128)S(1)}, u32[]{:S(2)}, u32[]{:S(2)}) collective-permute-start(f32[48,1024]{1,0:T(8,128)S(1)} %broadcast_select_fusion.4), channel_id=1, source_target_pairs={{0,1},{1,0},{2,3},{3,2},{4,5},{5,4},{6,7},{7,6},{8,9},{9,8},{10,11... | collective-permute-start | bytes 589832 | tf_op jit(solution)/shard_map/ppermute | solution.py:331
  7.1 1.6 %fusion.9 = (f32[128,1024]{1,0:T(8,128)}, f32[1024,128]{0,1:T(8,128)S(1)}) fusion(s32[1024]{0:T(1024)} %param.19), kind=kLoop, calls=%fused_computation.19 | loop fusion | flops 393216 | bytes 1052672 | tf_op jit(solution)/shard_map/convert_element_type | solution.py:312
  9.8 3.1 %add_convert_fusion.1 = bf16[1024,1152]{1,0:T(8,128)(2,1)} fusion(s32[1024]{0:T(1024)S(1)} %bitcast.54, s32[1024]{0:T(1024)S(1)} %bitcast.52, pred[1024]{0:T(1024)(128)(4,1)S(1)} %get-tuple-element.163, pred[1024]{0:T(1024)(128)(4,1)S(1)} %get-tuple-element.162), kind=kLoop, calls=%fused_computation.3 | loop fusion | flops 9437184 | bytes 2369536 | tf_op jit(solution)/shard_map/convert_element_type | solution.py:353
  13.1 3.4 %conditional.4 = ((f32[96,1024]{1,0:T(8,128)}, f32[96,128]{1,0:T(8,128)S(1)})) conditional(s32[]{:T(128)} %convert_element_type.41, (f32[8,1024]{1,0:T(8,128)S(1)}, f32[96,1024]{1,0:T(8,128)S(1)}, bf16[1024,1152]{1,0:T(8,128)(2,1)}) %tuple.45, (f32[8,1024]{1,0:T(8,128)S(1)}, f32[96,1024]{1,0:T(8,128)S(1)}) %tuple.46), branch_computations={%region_0.1_spmd, %region_1.2_spmd} | conditional | flops 453967872 | bytes 3620888 | solution.py:379
  13.1 3.4 %branch_0_fun.4 = (f32[96,1024]{1,0:T(8,128)}, f32[96,1024]{1,0:T(8,128)}, f32[96,128]{1,0:T(8,128)S(1)}) custom-call(f32[8,1024]{1,0:T(8,128)S(1)} %get-tuple-element.71.refs_0_, f32[96,1024]{1,0:T(8,128)S(1)} %get-tuple-element.72.refs_1_, bf16[1024,1152]{1,0:T(8,128)(2,1)} %get-tuple-element.73.refs_2_), custom_call_target="tpu_custom_call" | custom-call | flops 453967872 | bytes 3620864 | tf_op jit(solution)/shard_map/cond/branch_0_fun/pallas_call | solution.py:181
  16.4 1.3 %collective-permute-start.4 = (f32[96,128]{1,0:T(8,128)S(1)}, f32[96,128]{1,0:T(8,128)S(1)}, u32[]{:S(2)}, u32[]{:S(2)}) collective-permute-start(f32[96,128]{1,0:T(8,128)S(1)} %get-tuple-element.129), channel_id=1, source_target_pairs={{67,1},{69,3},{71,5},{73,7},{75,9},{77,11},{79,13},{81,15},{83,17}... | collective-permute-start | bytes 147464 | tf_op jit(solution)/shard_map/ppermute | solution.py:297
  18.4 1.3 %collective-permute-start.2 = (f32[96,1024]{1,0:T(8,128)}, f32[96,1024]{1,0:T(8,128)S(1)}, u32[]{:S(2)}, u32[]{:S(2)}) collective-permute-start(f32[96,1024]{1,0:T(8,128)} %get-tuple-element.128), channel_id=1, source_target_pairs={{65,1},{67,3},{69,5},{71,7},{73,9},{75,11},{77,13},{79,15},{81,17}... | collective-permute-start | bytes 1179656 | tf_op jit(solution)/shard_map/ppermute | solution.py:297
  20.4 1.9 %add_convert_fusion = bf16[1152,1024]{1,0:T(8,128)(2,1)S(1)} fusion(s32[1024]{0:T(1024)S(1)} %bitcast.55, s32[1024]{0:T(1024)S(1)} %bitcast.53, pred[1024]{0:T(1024)(128)(4,1)S(1)} %get-tuple-element.163, pred[1024]{0:T(1024)(128)(4,1)S(1)} %get-tuple-element.162), kind=kLoop, calls=%fused_computation | loop fusion | flops 9437184 | bytes 2369536 | tf_op jit(solution)/shard_map/convert_element_type | solution.py:346
  22.3 4.8 %collective-permute-done.2 = f32[96,1024]{1,0:T(8,128)S(1)} collective-permute-done((f32[96,1024]{1,0:T(8,128)}, f32[96,1024]{1,0:T(8,128)S(1)}, u32[]{:S(2)}, u32[]{:S(2)}) %collective-permute-start.2) | collective-permute-done | bytes 393248 | tf_op jit(solution)/shard_map/ppermute | solution.py:297
  27.2 3.6 %conditional.5 = (f32[96,1024]{1,0:T(8,128)}, f32[96,128]{1,0:T(8,128)S(1)}) conditional(s32[]{:T(128)} %convert_element_type.41, (f32[8,1024]{1,0:T(8,128)S(1)}, f32[96,1024]{1,0:T(8,128)S(1)}, f32[96,1024]{1,0:T(8,128)S(1)}, f32[96,128]{1,0:T(8,128)S(1)}, bf16[1024,1152]{1,0:T(8,128)(2,1)}) %tuple.47, (f32[8,1024]{1,0:T(8,128)S(1)}, ...), branch_computations={%region_2.3_spmd, %region_3.4_spmd} | conditional | flops 453967872 | bytes 4063248 | solution.py:384
  27.2 3.6 %branch_0_fun.5 = (f32[96,1024]{1,0:T(8,128)}, f32[96,1024]{1,0:T(8,128)}, f32[96,128]{1,0:T(8,128)S(1)}) custom-call(f32[8,1024]{1,0:T(8,128)S(1)} %get-tuple-element.78.refs_0_, f32[96,1024]{1,0:T(8,128)S(1)} %get-tuple-element.79.refs_1_, f32[96,1024]{1,0:T(8,128)S(1)} %get-tuple-element.80.refs_2_, f32[96,128]{1,0:T(8,128)S(1)} %get-tuple-element.81.refs_3_, ...), custom_call_target="tpu_custom_call" | custom-call | flops 453967872 | bytes 4063232 | tf_op jit(solution)/shard_map/cond/branch_0_fun/pallas_call | solution.py:181
  30.8 1.3 %collective-permute-start.6 = (f32[96,1024]{1,0:T(8,128)}, f32[96,1024]{1,0:T(8,128)S(1)}, u32[]{:S(2)}, u32[]{:S(2)}) collective-permute-start(f32[96,1024]{1,0:T(8,128)} %get-tuple-element.130), channel_id=1, source_target_pairs={{65,1},{67,3},{69,5},{71,7},{73,9},{75,11},{77,13},{79,15},{81,17}... | collective-permute-start | bytes 1179656 | tf_op jit(solution)/shard_map/ppermute | solution.py:297
  32.8 1.3 %collective-permute-start.8 = (f32[96,128]{1,0:T(8,128)S(1)}, f32[96,128]{1,0:T(8,128)S(1)}, u32[]{:S(2)}, u32[]{:S(2)}) collective-permute-start(f32[96,128]{1,0:T(8,128)S(1)} %get-tuple-element.131), channel_id=1, source_target_pairs={{67,1},{69,3},{71,5},{73,7},{75,9},{77,11},{79,13},{81,15},{83,17}... | collective-permute-start | bytes 147464 | tf_op jit(solution)/shard_map/ppermute | solution.py:297
  34.7 5.3 %collective-permute-done.8 = f32[96,128]{1,0:T(8,128)S(1)} collective-permute-done((f32[96,128]{1,0:T(8,128)S(1)}, f32[96,128]{1,0:T(8,128)S(1)}, u32[]{:S(2)}, u32[]{:S(2)}) %collective-permute-start.8) | collective-permute-done | bytes 49184 | tf_op jit(solution)/shard_map/ppermute | solution.py:297
  40.1 3.6 %conditional.6 = (f32[96,1024]{1,0:T(8,128)}, f32[96,128]{1,0:T(8,128)S(1)}) conditional(s32[]{:T(128)} %convert_element_type.41, (f32[8,1024]{1,0:T(8,128)S(1)}, f32[96,1024]{1,0:T(8,128)S(1)}, f32[96,1024]{1,0:T(8,128)S(1)}, f32[96,128]{1,0:T(8,128)S(1)}, bf16[1024,1152]{1,0:T(8,128)(2,1)}) %tuple.49, (f32[8,1024]{1,0:T(8,128)S(1)}, ...), branch_computations={%region_4.5_spmd, %region_5.6_spmd} | conditional | flops 453967872 | bytes 4063248 | solution.py:384
  40.1 3.6 %branch_0_fun.6 = (f32[96,1024]{1,0:T(8,128)}, f32[96,1024]{1,0:T(8,128)}, f32[96,128]{1,0:T(8,128)S(1)}) custom-call(f32[8,1024]{1,0:T(8,128)S(1)} %get-tuple-element.92.refs_0_, f32[96,1024]{1,0:T(8,128)S(1)} %get-tuple-element.93.refs_1_, f32[96,1024]{1,0:T(8,128)S(1)} %get-tuple-element.94.refs_2_, f32[96,128]{1,0:T(8,128)S(1)} %get-tuple-element.95.refs_3_, ...), custom_call_target="tpu_custom_call" | custom-call | flops 453967872 | bytes 4063232 | tf_op jit(solution)/shard_map/cond/branch_0_fun/pallas_call | solution.py:181
  43.7 1.3 %collective-permute-start.10 = (f32[96,1024]{1,0:T(8,128)}, f32[96,1024]{1,0:T(8,128)S(1)}, u32[]{:S(2)}, u32[]{:S(2)}) collective-permute-start(f32[96,1024]{1,0:T(8,128)} %get-tuple-element.132), channel_id=1, source_target_pairs={{65,1},{67,3},{69,5},{71,7},{73,9},{75,11},{77,13},{79,15},{81,17}... | collective-permute-start | bytes 1179656 | tf_op jit(solution)/shard_map/ppermute | solution.py:297
  45.7 1.3 %collective-permute-start.12 = (f32[96,128]{1,0:T(8,128)S(1)}, f32[96,128]{1,0:T(8,128)S(1)}, u32[]{:S(2)}, u32[]{:S(2)}) collective-permute-start(f32[96,128]{1,0:T(8,128)S(1)} %get-tuple-element.133), channel_id=1, source_target_pairs={{67,1},{69,3},{71,5},{73,7},{75,9},{77,11},{79,13},{81,15},{83,17}... | collective-permute-start | bytes 147464 | tf_op jit(solution)/shard_map/ppermute | solution.py:297
  47.7 5.6 %collective-permute-done.12 = f32[96,128]{1,0:T(8,128)S(1)} collective-permute-done((f32[96,128]{1,0:T(8,128)S(1)}, f32[96,128]{1,0:T(8,128)S(1)}, u32[]{:S(2)}, u32[]{:S(2)}) %collective-permute-start.12) | collective-permute-done | bytes 49184 | tf_op jit(solution)/shard_map/ppermute | solution.py:297
  53.3 2.1 %conditional.7 = (f32[1,96,1024]{2,1,0:T(8,128)}, f32[1,96,1024]{2,1,0:T(8,128)}, f32[1,96,1024]{2,1,0:T(8,128)S(1)}) conditional(s32[]{:T(128)} %convert_element_type.41, (f32[8,1024]{1,0:T(8,128)S(1)}, f32[96,1024]{1,0:T(8,128)S(1)}, f32[96,1024]{1,0:T(8,128)S(1)}, f32[96,128]{1,0:T(8,128)S(1)}) %tuple.51, (f32[8,1024]{1,0:T(8,128)S(1)}, ...), branch_computations={%region_6.7_spmd, %region_7.8_spmd} | conditional | flops 453967872 | bytes 4063256 | solution.py:384
  53.3 1.3 %branch_0_fun.7 = f32[96,1024]{1,0:T(8,128)} custom-call(f32[8,1024]{1,0:T(8,128)S(1)} %get-tuple-element.106.refs_0_, f32[96,1024]{1,0:T(8,128)S(1)} %get-tuple-element.107.refs_1_, f32[96,1024]{1,0:T(8,128)S(1)} %get-tuple-element.108.refs_2_, f32[96,128]{1,0:T(8,128)S(1)} %get-tuple-element.109.refs_3_), custom_call_target="tpu_custom_call" | custom-call | flops 453967872 | bytes 1261568 | tf_op jit(solution)/shard_map/cond/branch_0_fun/pallas_call | solution.py:181
  58.7 2.5 %collective-permute-done.13 = f32[3,96,1024]{2,1,0:T(8,128)S(1)} collective-permute-done((f32[3,96,1024]{2,1,0:T(8,128)S(1)}, f32[3,96,1024]{2,1,0:T(8,128)S(1)}, u32[]{:S(2)}, u32[]{:S(2)}) %collective-permute-start.13) | collective-permute-done | bytes 1179680 | tf_op jit(solution)/shard_map/ppermute | solution.py:388
  65.0 15.5 %all-to-all-start = ((f32[128,1,128]{2,1,0:T(1,128)}), f32[128,1,128]{2,1,0:T(1,128)S(1)}, u32[]{:S(2)}, u32[]{:S(2)}) async-start(f32[128,1,128]{2,1,0:T(1,128)} %bitcast.23), calls=%async_computation | async-start | bytes 131072 | tf_op jit(solution)/shard_map/all_to_all | solution.py:417
  81.3 9.8 %all-to-all-done = f32[128,1,128]{2,1,0:T(1,128)S(1)} async-done(((f32[128,1,128]{2,1,0:T(1,128)}), f32[128,1,128]{2,1,0:T(1,128)S(1)}, u32[]{:S(2)}, u32[]{:S(2)}) %all-to-all-start) | async-done | bytes 65568 | tf_op jit(solution)/shard_map/all_to_all | solution.py:417
  (65 shorter events, 17.5 us)
Async XLA Ops:
  0.6 8.0 %copy-start = (f32[16,1024]{1,0:T(8,128)S(1)}, f32[16,1024]{1,0:T(8,128)}, u32[]{:S(2)}) copy-start(f32[16,1024]{1,0:T(8,128)} %param.18) | copy-start | bytes 196612
  0.6 8.0 %copy-start.4 = (f32[128,16,2]{0,2,1:T(2,128)S(1)}, f32[128,16,2]{0,2,1:T(2,128)}, u32[]{:S(2)}) copy-start(f32[128,16,2]{0,2,1:T(2,128)} %param.23) | copy-start | bytes 49156
  1.6 11.3 %collective-permute-start = (f32[48,1024]{1,0:T(8,128)S(1)}, f32[48,1024]{1,0:T(8,128)S(1)}, u32[]{:S(2)}, u32[]{:S(2)}) collective-permute-start(f32[48,1024]{1,0:T(8,128)S(1)} %broadcast_select_fusion.4), channel_id=1, source_target_pairs={{0,1},{1,0},{2,3},{3,2},{4,5},{5,4},{6,7},{7,6},{8,9},{9,8},{10,11... | collective-permute-start | bytes 589832 | tf_op jit(solution)/shard_map/ppermute | solution.py:331
  9.8 3.2 %copy-start.2 = (f32[48,1024]{1,0:T(8,128)S(1)}, f32[48,1024]{1,0:T(8,128)}, u32[]{:S(2)}) copy-start(f32[48,1024]{1,0:T(8,128)} %param.17) | copy-start | bytes 589828
  9.8 3.2 %copy-start.3 = (f32[48,1024]{1,0:T(8,128)S(1)}, f32[48,1024]{1,0:T(8,128)}, u32[]{:S(2)}) copy-start(f32[48,1024]{1,0:T(8,128)} %param.16) | copy-start | bytes 589828
  16.4 5.8 %collective-permute-start.4 = (f32[96,128]{1,0:T(8,128)S(1)}, f32[96,128]{1,0:T(8,128)S(1)}, u32[]{:S(2)}, u32[]{:S(2)}) collective-permute-start(f32[96,128]{1,0:T(8,128)S(1)} %get-tuple-element.129), channel_id=1, source_target_pairs={{67,1},{69,3},{71,5},{73,7},{75,9},{77,11},{79,13},{81,15},{83,17}... | collective-permute-start | bytes 147464 | tf_op jit(solution)/shard_map/ppermute | solution.py:297
  17.7 4.5 %collective-permute-start.3 = (f32[96,128]{1,0:T(8,128)S(1)}, f32[96,128]{1,0:T(8,128)S(1)}, u32[]{:S(2)}, u32[]{:S(2)}) collective-permute-start(f32[96,128]{1,0:T(8,128)S(1)} %get-tuple-element.129), channel_id=1, source_target_pairs={{0,66},{2,68},{4,70},{6,72},{8,74},{10,76},{12,78},{14,80},{16,82}... | collective-permute-start | bytes 147464 | tf_op jit(solution)/shard_map/ppermute | solution.py:296
  18.4 8.7 %collective-permute-start.2 = (f32[96,1024]{1,0:T(8,128)}, f32[96,1024]{1,0:T(8,128)S(1)}, u32[]{:S(2)}, u32[]{:S(2)}) collective-permute-start(f32[96,1024]{1,0:T(8,128)} %get-tuple-element.128), channel_id=1, source_target_pairs={{65,1},{67,3},{69,5},{71,7},{73,9},{75,11},{77,13},{79,15},{81,17}... | collective-permute-start | bytes 1179656 | tf_op jit(solution)/shard_map/ppermute | solution.py:297
  19.7 7.4 %collective-permute-start.1 = (f32[96,1024]{1,0:T(8,128)}, f32[96,1024]{1,0:T(8,128)S(1)}, u32[]{:S(2)}, u32[]{:S(2)}) collective-permute-start(f32[96,1024]{1,0:T(8,128)} %get-tuple-element.128), channel_id=1, source_target_pairs={{0,64},{2,66},{4,68},{6,70},{8,72},{10,74},{12,76},{14,78},{16,80}... | collective-permute-start | bytes 1179656 | tf_op jit(solution)/shard_map/ppermute | solution.py:296
  30.8 9.3 %collective-permute-start.6 = (f32[96,1024]{1,0:T(8,128)}, f32[96,1024]{1,0:T(8,128)S(1)}, u32[]{:S(2)}, u32[]{:S(2)}) collective-permute-start(f32[96,1024]{1,0:T(8,128)} %get-tuple-element.130), channel_id=1, source_target_pairs={{65,1},{67,3},{69,5},{71,7},{73,9},{75,11},{77,13},{79,15},{81,17}... | collective-permute-start | bytes 1179656 | tf_op jit(solution)/shard_map/ppermute | solution.py:297
  32.1 8.0 %collective-permute-start.5 = (f32[96,1024]{1,0:T(8,128)}, f32[96,1024]{1,0:T(8,128)S(1)}, u32[]{:S(2)}, u32[]{:S(2)}) collective-permute-start(f32[96,1024]{1,0:T(8,128)} %get-tuple-element.130), channel_id=1, source_target_pairs={{0,64},{2,66},{4,68},{6,70},{8,72},{10,74},{12,76},{14,78},{16,80}... | collective-permute-start | bytes 1179656 | tf_op jit(solution)/shard_map/ppermute | solution.py:296
  32.8 7.3 %collective-permute-start.8 = (f32[96,128]{1,0:T(8,128)S(1)}, f32[96,128]{1,0:T(8,128)S(1)}, u32[]{:S(2)}, u32[]{:S(2)}) collective-permute-start(f32[96,128]{1,0:T(8,128)S(1)} %get-tuple-element.131), channel_id=1, source_target_pairs={{67,1},{69,3},{71,5},{73,7},{75,9},{77,11},{79,13},{81,15},{83,17}... | collective-permute-start | bytes 147464 | tf_op jit(solution)/shard_map/ppermute | solution.py:297
  34.1 6.0 %collective-permute-start.7 = (f32[96,128]{1,0:T(8,128)S(1)}, f32[96,128]{1,0:T(8,128)S(1)}, u32[]{:S(2)}, u32[]{:S(2)}) collective-permute-start(f32[96,128]{1,0:T(8,128)S(1)} %get-tuple-element.131), channel_id=1, source_target_pairs={{0,66},{2,68},{4,70},{6,72},{8,74},{10,76},{12,78},{14,80},{16,82}... | collective-permute-start | bytes 147464 | tf_op jit(solution)/shard_map/ppermute | solution.py:296
  43.7 9.5 %collective-permute-start.10 = (f32[96,1024]{1,0:T(8,128)}, f32[96,1024]{1,0:T(8,128)S(1)}, u32[]{:S(2)}, u32[]{:S(2)}) collective-permute-start(f32[96,1024]{1,0:T(8,128)} %get-tuple-element.132), channel_id=1, source_target_pairs={{65,1},{67,3},{69,5},{71,7},{73,9},{75,11},{77,13},{79,15},{81,17}... | collective-permute-start | bytes 1179656 | tf_op jit(solution)/shard_map/ppermute | solution.py:297
  45.0 8.2 %collective-permute-start.9 = (f32[96,1024]{1,0:T(8,128)}, f32[96,1024]{1,0:T(8,128)S(1)}, u32[]{:S(2)}, u32[]{:S(2)}) collective-permute-start(f32[96,1024]{1,0:T(8,128)} %get-tuple-element.132), channel_id=1, source_target_pairs={{0,64},{2,66},{4,68},{6,70},{8,72},{10,74},{12,76},{14,78},{16,80}... | collective-permute-start | bytes 1179656 | tf_op jit(solution)/shard_map/ppermute | solution.py:296
  45.7 7.5 %collective-permute-start.12 = (f32[96,128]{1,0:T(8,128)S(1)}, f32[96,128]{1,0:T(8,128)S(1)}, u32[]{:S(2)}, u32[]{:S(2)}) collective-permute-start(f32[96,128]{1,0:T(8,128)S(1)} %get-tuple-element.133), channel_id=1, source_target_pairs={{67,1},{69,3},{71,5},{73,7},{75,9},{77,11},{79,13},{81,15},{83,17}... | collective-permute-start | bytes 147464 | tf_op jit(solution)/shard_map/ppermute | solution.py:297
  47.0 6.2 %collective-permute-start.11 = (f32[96,128]{1,0:T(8,128)S(1)}, f32[96,128]{1,0:T(8,128)S(1)}, u32[]{:S(2)}, u32[]{:S(2)}) collective-permute-start(f32[96,128]{1,0:T(8,128)S(1)} %get-tuple-element.133), channel_id=1, source_target_pairs={{0,66},{2,68},{4,70},{6,72},{8,74},{10,76},{12,78},{14,80},{16,82}... | collective-permute-start | bytes 147464 | tf_op jit(solution)/shard_map/ppermute | solution.py:296
  57.6 3.6 %collective-permute-start.13 = (f32[3,96,1024]{2,1,0:T(8,128)S(1)}, f32[3,96,1024]{2,1,0:T(8,128)S(1)}, u32[]{:S(2)}, u32[]{:S(2)}) collective-permute-start(f32[3,96,1024]{2,1,0:T(8,128)S(1)} %constant_dynamic-update-slice_fusion), channel_id=1, source_target_pairs={{0,1},{1,0},{2,3},{3,2},{4,5},{5,4},{6,7},{7,6},{8,9},{9,8},{10,11... | collective-permute-start | bytes 3538952 | tf_op jit(solution)/shard_map/ppermute | solution.py:388
  61.4 1.0 %copy-start.1 = (f32[128,1024]{1,0:T(8,128)S(1)}, f32[128,1024]{1,0:T(8,128)}, u32[]{:S(2)}) copy-start(f32[128,1024]{1,0:T(8,128)} %get-tuple-element.160) | copy-start | bytes 1572868
  65.0 26.1 %all-to-all-start = ((f32[128,1,128]{2,1,0:T(1,128)}), f32[128,1,128]{2,1,0:T(1,128)S(1)}, u32[]{:S(2)}, u32[]{:S(2)}) async-start(f32[128,1,128]{2,1,0:T(1,128)} %bitcast.23), calls=%async_computation | async-start | bytes 131072 | tf_op jit(solution)/shard_map/all_to_all | solution.py:417

commit v8 on v6

--- a/solution.py
+++ b/solution.py
@@ -103,37 +103,64 @@
     return jnp.concatenate([high, low], axis=0)
 
 
+def shifted_rows(value, shift, fill):
+    rows = lax.broadcasted_iota(jnp.int32, value.shape, 0)
+    return jnp.where(rows >= shift, pltpu.roll(value, shift, 0), fill)
+
+
 def forward_kernel(*refs, has_inflow):
     if has_inflow:
         coef_ref, upper_ref, side_ref, conf_ref, lateral_ref, out_ref, outlet_ref, inflow_ref = refs
     else:
         coef_ref, lateral_ref, out_ref, outlet_ref = refs
-    steps = lateral_ref.shape[0]
+    steps, width = lateral_ref.shape
     narrow = outlet_ref.shape[1]
+    tile = 8
     gain_now, gain_prev, gain_side = coef_ref[0:1, :], coef_ref[1:2, :], coef_ref[2:3, :]
     keep, live = coef_ref[3:4, :], coef_ref[4:5, :]
     if has_inflow:
         source = jnp.concatenate([upper_ref[...], side_ref[...]], axis=1)
         product = jnp.dot(split_pair(source), conf_ref[...], preferred_element_type=jnp.float32)
         inflow_ref[...] = product[:steps] + product[steps:]
-
-    def advance(hour, carry):
+    keep_tile = jnp.broadcast_to(keep, (tile, width))
+    powers = keep_tile
+    span = 1
+    while span < tile:
+        powers = powers * shifted_rows(powers, span, 1.0)
+        span *= 2
+    keep_steps = []
+    factor = keep
+    for unused in range(3):
+        keep_steps.append(factor)
+        factor = factor * factor
+
+    def advance(block, carry):
         state, before = carry
-        side_in = lateral_ref[pl.ds(hour, 1), :]
+        rows = pl.ds(pl.multiple_of(block * tile, tile), tile)
+        drive_side = gain_side * lateral_ref[rows, :]
         if has_inflow:
-            now = inflow_ref[pl.ds(hour, 1), :]
-            drive = (gain_now * now + gain_prev * before) + gain_side * side_in
+            now = inflow_ref[rows, :]
+            earlier = jnp.where(
+                lax.broadcasted_iota(jnp.int32, (tile, width), 0) >= 1,
+                pltpu.roll(now, 1, 0),
+                before,
+            )
+            drive = (gain_now * now + gain_prev * earlier) + drive_side
+            before = now[tile - 1 : tile, :]
         else:
-            now = before
-            drive = gain_side * side_in
-        state = keep * state + drive
-        flow = state * live
-        out_ref[pl.ds(hour, 1), :] = flow
-        outlet_ref[pl.ds(hour, 1), :] = flow[:, :narrow]
-        return state, now
+            drive = drive_side
+        span = 1
+        for factor in keep_steps:
+            drive = drive + factor * shifted_rows(drive, span, 0.0)
+            span *= 2
+        block_state = drive + powers * state
+        flow = block_state * live
+        out_ref[rows, :] = flow
+        outlet_ref[rows, :] = flow[:, :narrow]
+        return block_state[tile - 1 : tile, :], before
 
     zero = jnp.zeros_like(keep)
-    lax.fori_loop(0, steps, advance, (zero, zero), unroll=8)
+    lax.fori_loop(0, steps // tile, advance, (zero, zero), unroll=2)
 
 
 def backward_kernel(*refs, has_down, emit):

time: 90.6 us -> 90.6 us (level)
  no operation moved by 1% of the time
where the time goes in v8:
time: 90.6 us; the launch traced here: 90.1 us
  starting transfers between devices  34.3 us (38%)
  waiting for transfers between devices  30 us (33%)
  other arithmetic  9.83 us (11%)
  Pallas kernels  8.12 us (9%)
  local copies, waits for them, and re-layouts  4.26 us (5%)
  matrix products  2.01 us (2%)
  between operations  1.55 us (2%)
    ppermute x6, waiting for transfers between devices, both_ways(): return lax.ppermute(value, ('level', 'basin', 'group'), pairs)  17.7 us
    all_to_all x1, starting transfers between devices, body(): lax.all_to_all(replicated, ('level', 'basin'), 0, 0, tiled=True)  15.1 us
    all_to_all x1, waiting for transfers between devices, body(): lax.all_to_all(replicated, ('level', 'basin'), 0, 0, tiled=True)  9.85 us
    ppermute x1, starting transfers between devices, body(): other = lax.ppermute(kept, 'group', [(0, 1), (1, 0)])  8.17 us
    pallas_call x4, Pallas kernels, vmem_call(): pl.pallas_call(kernel, out_shape=[jax.ShapeDtypeStruct(shape, jnp.float32...  8.12 us
    ppermute x6, starting transfers between devices, both_ways(): return lax.ppermute(value, ('level', 'basin', 'group'), pairs)  7.72 us
    convert_element_type x1, other arithmetic, body(): confluence = confluence.astype(jnp.bfloat16)  3.3 us
    ppermute x1, starting transfers between devices, body(): lax.ppermute(jnp.where(mine == 0, cotangent, lateral), 'group', [(0, 1),...  3.29 us
  transfers between devices with their start and end apart: 9, of which 7 were waited for; matrix products, arithmetic and copies ran while one was open for 11% of the time, Pallas kernels for 0%

profile of v8, /device:TPU:1, one launch (start us, length us, event | category | flops | bytes accessed | tf_op | source)
XLA Modules:
  0.0 90.1 jit_solution(4010151695196194375)
XLA Ops:
  1.6 3.3 %collective-permute-start = (f32[48,1024]{1,0:T(8,128)S(1)}, f32[48,1024]{1,0:T(8,128)}, u32[]{:S(2)}, u32[]{:S(2)}) collective-permute-start(f32[48,1024]{1,0:T(8,128)S(1)} %broadcast_select_fusion.1), channel_id=1, source_target_pairs={{0,1},{1,0},{2,3},{3,2},{4,5},{5,4},{6,7},{7,6},{8,9},{9,8},{10,11... | collective-permute-start | bytes 589832 | tf_op jit(solution)/shard_map/ppermute | solution.py:356
  7.9 1.1 %fusion.5 = f32[1024,2]{0,1:T(2,128)S(1)} fusion(f32[1024,128]{0,1:T(8,128)S(1)} %get-tuple-element.161, f32[16,1024]{1,0:T(8,128)S(1)} %copy-done, f32[128,2,16]{0,1,2:T(2,128)S(1)} %bitcast.64), kind=kOutput, calls=%fused_computation.12 | convolution fusion | flops 50853888 | bytes 614400 | tf_op jit(solution)/shard_map/dot_general | solution.py:338
  9.0 2.0 %add_convert_fusion.1 = bf16[1024,1152]{1,0:T(8,128)(2,1)S(1)} fusion(s32[1024]{0:T(1024)S(1)} %bitcast.57, s32[1024]{0:T(1024)S(1)} %bitcast.55, pred[1024]{0:T(1024)(128)(4,1)S(1)} %get-tuple-element.163, pred[1024]{0:T(1024)(128)(4,1)S(1)} %get-tuple-element.162), kind=kLoop, calls=%fused_computation.3 | loop fusion | flops 9437184 | bytes 2369536 | tf_op jit(solution)/shard_map/convert_element_type | solution.py:378
  11.2 1.3 %maximum_select_fusion = f32[96,1024]{1,0:T(8,128)S(1)} fusion(f32[48,1024]{1,0:T(8,128)} %collective-permute-done, f32[48,1024]{1,0:T(8,128)} %param.16, f32[48,1024]{1,0:T(8,128)} %param.17, pred[]{:T(512)S(6)} %eq.58), kind=kLoop, calls=%fused_computation.32 | loop fusion | flops 294912 | bytes 983041 | tf_op jit(solution)/shard_map/jit(_where)/select_n | solution.py:357
  12.5 1.7 %conditional.4 = ((f32[96,1024]{1,0:T(8,128)}, f32[96,128]{1,0:T(8,128)S(1)})) conditional(s32[]{:T(128)} %convert_element_type.41, (f32[8,1024]{1,0:T(8,128)S(1)}, f32[96,1024]{1,0:T(8,128)S(1)}, bf16[1024,1152]{1,0:T(8,128)(2,1)S(1)}) %tuple.45, (f32[8,1024]{1,0:T(8,128)S(1)}, f32[96,1024]{1,0:T(8,128)S(1)}) %tuple.46), branch_computations={%region_0.1_spmd, %region_1.2_spmd} | conditional | flops 453967872 | bytes 3620888 | solution.py:404
  12.5 1.7 %branch_0_fun.4 = (f32[96,1024]{1,0:T(8,128)}, f32[96,1024]{1,0:T(8,128)}, f32[96,128]{1,0:T(8,128)S(1)}) custom-call(f32[8,1024]{1,0:T(8,128)S(1)} %get-tuple-element.71.refs_0_, f32[96,1024]{1,0:T(8,128)S(1)} %get-tuple-element.72.refs_1_, bf16[1024,1152]{1,0:T(8,128)(2,1)S(1)} %get-tuple-element.73.refs_2_), custom_call_target="tpu_custom_call" | custom-call | flops 453967872 | bytes 3620864 | tf_op jit(solution)/shard_map/cond/branch_0_fun/pallas_call | solution.py:208
  14.2 1.3 %collective-permute-start.2 = (f32[96,128]{1,0:T(8,128)S(1)}, f32[96,128]{1,0:T(8,128)S(1)}, u32[]{:S(2)}, u32[]{:S(2)}) collective-permute-start(f32[96,128]{1,0:T(8,128)S(1)} %get-tuple-element.129), channel_id=1, source_target_pairs={{0,66},{2,68},{4,70},{6,72},{8,74},{10,76},{12,78},{14,80},{16,82}... | collective-permute-start | bytes 147464 | tf_op jit(solution)/shard_map/ppermute | solution.py:323
  15.5 1.3 %collective-permute-start.1 = (f32[96,1024]{1,0:T(8,128)}, f32[96,1024]{1,0:T(8,128)}, u32[]{:S(2)}, u32[]{:S(2)}) collective-permute-start(f32[96,1024]{1,0:T(8,128)} %get-tuple-element.128), channel_id=1, source_target_pairs={{0,64},{2,66},{4,68},{6,70},{8,72},{10,74},{12,76},{14,78},{16,80}... | collective-permute-start | bytes 1179656 | tf_op jit(solution)/shard_map/ppermute | solution.py:323
  16.8 3.3 %add_convert_fusion = bf16[1152,1024]{1,0:T(8,128)(2,1)} fusion(s32[1024]{0:T(1024)S(1)} %bitcast.58, s32[1024]{0:T(1024)S(1)} %bitcast.56, pred[1024]{0:T(1024)(128)(4,1)S(1)} %get-tuple-element.163, pred[1024]{0:T(1024)(128)(4,1)S(1)} %get-tuple-element.162), kind=kLoop, calls=%fused_computation | loop fusion | flops 9437184 | bytes 2369536 | tf_op jit(solution)/shard_map/convert_element_type | solution.py:371
  20.1 4.2 %collective-permute-done.1 = f32[96,1024]{1,0:T(8,128)} collective-permute-done((f32[96,1024]{1,0:T(8,128)}, f32[96,1024]{1,0:T(8,128)}, u32[]{:S(2)}, u32[]{:S(2)}) %collective-permute-start.1) | collective-permute-done | bytes 393248 | tf_op jit(solution)/shard_map/ppermute | solution.py:323
  24.3 2.9 %conditional.5 = (f32[96,1024]{1,0:T(8,128)}, f32[96,128]{1,0:T(8,128)S(1)}) conditional(s32[]{:T(128)} %convert_element_type.41, (f32[8,1024]{1,0:T(8,128)S(1)}, f32[96,1024]{1,0:T(8,128)S(1)}, f32[96,1024]{1,0:T(8,128)}, f32[96,128]{1,0:T(8,128)S(1)}, bf16[1024,1152]{1,0:T(8,128)(2,1)S(1)}) %tuple.47, (f32[8,1024]{1,0:T(8,128)S(1)}, ...), branch_computations={%region_2.3_spmd, %region_3.4_spmd} | conditional | flops 453967872 | bytes 4063248 | solution.py:409
  24.3 2.9 %branch_0_fun.5 = (f32[96,1024]{1,0:T(8,128)}, f32[96,1024]{1,0:T(8,128)}, f32[96,128]{1,0:T(8,128)S(1)}) custom-call(f32[8,1024]{1,0:T(8,128)S(1)} %get-tuple-element.78.refs_0_, f32[96,1024]{1,0:T(8,128)S(1)} %get-tuple-element.79.refs_1_, f32[96,1024]{1,0:T(8,128)} %get-tuple-element.80.refs_2_, f32[96,128]{1,0:T(8,128)S(1)} %get-tuple-element.81.refs_3_, ...), custom_call_target="tpu_custom_call" | custom-call | flops 453967872 | bytes 4063232 | tf_op jit(solution)/shard_map/cond/branch_0_fun/pallas_call | solution.py:208
  27.3 1.3 %collective-permute-start.3 = (f32[96,1024]{1,0:T(8,128)}, f32[96,1024]{1,0:T(8,128)}, u32[]{:S(2)}, u32[]{:S(2)}) collective-permute-start(f32[96,1024]{1,0:T(8,128)} %get-tuple-element.130), channel_id=1, source_target_pairs={{0,64},{2,66},{4,68},{6,70},{8,72},{10,74},{12,76},{14,78},{16,80}... | collective-permute-start | bytes 1179656 | tf_op jit(solution)/shard_map/ppermute | solution.py:323
  28.5 1.3 %collective-permute-start.4 = (f32[96,128]{1,0:T(8,128)S(1)}, f32[96,128]{1,0:T(8,128)S(1)}, u32[]{:S(2)}, u32[]{:S(2)}) collective-permute-start(f32[96,128]{1,0:T(8,128)S(1)} %get-tuple-element.131), channel_id=1, source_target_pairs={{0,66},{2,68},{4,70},{6,72},{8,74},{10,76},{12,78},{14,80},{16,82}... | collective-permute-start | bytes 147464 | tf_op jit(solution)/shard_map/ppermute | solution.py:323
  29.8 6.1 %collective-permute-done.4 = f32[96,128]{1,0:T(8,128)S(1)} collective-permute-done((f32[96,128]{1,0:T(8,128)S(1)}, f32[96,128]{1,0:T(8,128)S(1)}, u32[]{:S(2)}, u32[]{:S(2)}) %collective-permute-start.4) | collective-permute-done | bytes 49184 | tf_op jit(solution)/shard_map/ppermute | solution.py:323
  36.6 2.9 %conditional.6 = (f32[96,1024]{1,0:T(8,128)}, f32[96,128]{1,0:T(8,128)S(1)}) conditional(s32[]{:T(128)} %convert_element_type.41, (f32[8,1024]{1,0:T(8,128)S(1)}, f32[96,1024]{1,0:T(8,128)S(1)}, f32[96,1024]{1,0:T(8,128)}, f32[96,128]{1,0:T(8,128)S(1)}, bf16[1024,1152]{1,0:T(8,128)(2,1)S(1)}) %tuple.49, (f32[8,1024]{1,0:T(8,128)S(1)}, ...), branch_computations={%region_4.5_spmd, %region_5.6_spmd} | conditional | flops 453967872 | bytes 4063248 | solution.py:409
  36.6 2.9 %branch_0_fun.6 = (f32[96,1024]{1,0:T(8,128)}, f32[96,1024]{1,0:T(8,128)}, f32[96,128]{1,0:T(8,128)S(1)}) custom-call(f32[8,1024]{1,0:T(8,128)S(1)} %get-tuple-element.92.refs_0_, f32[96,1024]{1,0:T(8,128)S(1)} %get-tuple-element.93.refs_1_, f32[96,1024]{1,0:T(8,128)} %get-tuple-element.94.refs_2_, f32[96,128]{1,0:T(8,128)S(1)} %get-tuple-element.95.refs_3_, ...), custom_call_target="tpu_custom_call" | custom-call | flops 453967872 | bytes 4063232 | tf_op jit(solution)/shard_map/cond/branch_0_fun/pallas_call | solution.py:208
  39.5 1.3 %collective-permute-start.5 = (f32[96,1024]{1,0:T(8,128)}, f32[96,1024]{1,0:T(8,128)S(1)}, u32[]{:S(2)}, u32[]{:S(2)}) collective-permute-start(f32[96,1024]{1,0:T(8,128)} %get-tuple-element.132), channel_id=1, source_target_pairs={{0,64},{2,66},{4,68},{6,70},{8,72},{10,74},{12,76},{14,78},{16,80}... | collective-permute-start | bytes 1179656 | tf_op jit(solution)/shard_map/ppermute | solution.py:323
  40.8 1.3 %collective-permute-start.6 = (f32[96,128]{1,0:T(8,128)S(1)}, f32[96,128]{1,0:T(8,128)S(1)}, u32[]{:S(2)}, u32[]{:S(2)}) collective-permute-start(f32[96,128]{1,0:T(8,128)S(1)} %get-tuple-element.133), channel_id=1, source_target_pairs={{0,66},{2,68},{4,70},{6,72},{8,74},{10,76},{12,78},{14,80},{16,82}... | collective-permute-start | bytes 147464 | tf_op jit(solution)/shard_map/ppermute | solution.py:323
  42.1 6.4 %collective-permute-done.6 = f32[96,128]{1,0:T(8,128)S(1)} collective-permute-done((f32[96,128]{1,0:T(8,128)S(1)}, f32[96,128]{1,0:T(8,128)S(1)}, u32[]{:S(2)}, u32[]{:S(2)}) %collective-permute-start.6) | collective-permute-done | bytes 49184 | tf_op jit(solution)/shard_map/ppermute | solution.py:323
  49.5 8.2 %collective-permute-start.7 = (f32[3,96,1024]{2,1,0:T(8,128)S(1)}, f32[3,96,1024]{2,1,0:T(8,128)S(1)}, u32[]{:S(2)}, u32[]{:S(2)}) collective-permute-start(f32[3,96,1024]{2,1,0:T(8,128)S(1)} %constant_dynamic-update-slice_fusion), channel_id=1, source_target_pairs={{0,1},{1,0},{2,3},{3,2},{4,5},{5,4},{6,7},{7,6},{8,9},{9,8},{10,11... | collective-permute-start | bytes 3538952 | tf_op jit(solution)/shard_map/ppermute | solution.py:413
  57.7 2.5 %collective-permute-done.7 = f32[3,96,1024]{2,1,0:T(8,128)S(1)} collective-permute-done((f32[3,96,1024]{2,1,0:T(8,128)S(1)}, f32[3,96,1024]{2,1,0:T(8,128)S(1)}, u32[]{:S(2)}, u32[]{:S(2)}) %collective-permute-start.7) | collective-permute-done | bytes 1179680 | tf_op jit(solution)/shard_map/ppermute | solution.py:413
  63.4 15.1 %all-to-all-start = ((f32[128,1,128]{2,1,0:T(1,128)}), f32[128,1,128]{2,1,0:T(1,128)S(1)}, u32[]{:S(2)}, u32[]{:S(2)}) async-start(f32[128,1,128]{2,1,0:T(1,128)} %bitcast.23), calls=%async_computation | async-start | bytes 131072 | tf_op jit(solution)/shard_map/all_to_all | solution.py:442
  79.3 9.8 %all-to-all-done = f32[128,1,128]{2,1,0:T(1,128)S(1)} async-done(((f32[128,1,128]{2,1,0:T(1,128)}), f32[128,1,128]{2,1,0:T(1,128)S(1)}, u32[]{:S(2)}, u32[]{:S(2)}) %all-to-all-start) | async-done | bytes 65568 | tf_op jit(solution)/shard_map/all_to_all | solution.py:442
  (41 shorter events, 10.5 us)
Async XLA Ops:
  0.6 7.2 %copy-start = (f32[16,1024]{1,0:T(8,128)S(1)}, f32[16,1024]{1,0:T(8,128)}, u32[]{:S(2)}) copy-start(f32[16,1024]{1,0:T(8,128)} %param.18) | copy-start | bytes 196612
  0.6 7.2 %copy-start.1 = (f32[128,16,2]{0,2,1:T(2,128)S(1)}, f32[128,16,2]{0,2,1:T(2,128)}, u32[]{:S(2)}) copy-start(f32[128,16,2]{0,2,1:T(2,128)} %param.23) | copy-start | bytes 49156
  1.6 9.5 %collective-permute-start = (f32[48,1024]{1,0:T(8,128)S(1)}, f32[48,1024]{1,0:T(8,128)}, u32[]{:S(2)}, u32[]{:S(2)}) collective-permute-start(f32[48,1024]{1,0:T(8,128)S(1)} %broadcast_select_fusion.1), channel_id=1, source_target_pairs={{0,1},{1,0},{2,3},{3,2},{4,5},{5,4},{6,7},{7,6},{8,9},{9,8},{10,11... | collective-permute-start | bytes 589832 | tf_op jit(solution)/shard_map/ppermute | solution.py:356
  14.2 5.9 %collective-permute-start.2 = (f32[96,128]{1,0:T(8,128)S(1)}, f32[96,128]{1,0:T(8,128)S(1)}, u32[]{:S(2)}, u32[]{:S(2)}) collective-permute-start(f32[96,128]{1,0:T(8,128)S(1)} %get-tuple-element.129), channel_id=1, source_target_pairs={{0,66},{2,68},{4,70},{6,72},{8,74},{10,76},{12,78},{14,80},{16,82}... | collective-permute-start | bytes 147464 | tf_op jit(solution)/shard_map/ppermute | solution.py:323
  15.5 8.8 %collective-permute-start.1 = (f32[96,1024]{1,0:T(8,128)}, f32[96,1024]{1,0:T(8,128)}, u32[]{:S(2)}, u32[]{:S(2)}) collective-permute-start(f32[96,1024]{1,0:T(8,128)} %get-tuple-element.128), channel_id=1, source_target_pairs={{0,64},{2,66},{4,68},{6,70},{8,72},{10,74},{12,76},{14,78},{16,80}... | collective-permute-start | bytes 1179656 | tf_op jit(solution)/shard_map/ppermute | solution.py:323
  27.3 9.4 %collective-permute-start.3 = (f32[96,1024]{1,0:T(8,128)}, f32[96,1024]{1,0:T(8,128)}, u32[]{:S(2)}, u32[]{:S(2)}) collective-permute-start(f32[96,1024]{1,0:T(8,128)} %get-tuple-element.130), channel_id=1, source_target_pairs={{0,64},{2,66},{4,68},{6,70},{8,72},{10,74},{12,76},{14,78},{16,80}... | collective-permute-start | bytes 1179656 | tf_op jit(solution)/shard_map/ppermute | solution.py:323
  28.5 7.4 %collective-permute-start.4 = (f32[96,128]{1,0:T(8,128)S(1)}, f32[96,128]{1,0:T(8,128)S(1)}, u32[]{:S(2)}, u32[]{:S(2)}) collective-permute-start(f32[96,128]{1,0:T(8,128)S(1)} %get-tuple-element.131), channel_id=1, source_target_pairs={{0,66},{2,68},{4,70},{6,72},{8,74},{10,76},{12,78},{14,80},{16,82}... | collective-permute-start | bytes 147464 | tf_op jit(solution)/shard_map/ppermute | solution.py:323
  39.5 9.2 %collective-permute-start.5 = (f32[96,1024]{1,0:T(8,128)}, f32[96,1024]{1,0:T(8,128)S(1)}, u32[]{:S(2)}, u32[]{:S(2)}) collective-permute-start(f32[96,1024]{1,0:T(8,128)} %get-tuple-element.132), channel_id=1, source_target_pairs={{0,64},{2,66},{4,68},{6,70},{8,72},{10,74},{12,76},{14,78},{16,80}... | collective-permute-start | bytes 1179656 | tf_op jit(solution)/shard_map/ppermute | solution.py:323
  40.8 7.7 %collective-permute-start.6 = (f32[96,128]{1,0:T(8,128)S(1)}, f32[96,128]{1,0:T(8,128)S(1)}, u32[]{:S(2)}, u32[]{:S(2)}) collective-permute-start(f32[96,128]{1,0:T(8,128)S(1)} %get-tuple-element.133), channel_id=1, source_target_pairs={{0,66},{2,68},{4,70},{6,72},{8,74},{10,76},{12,78},{14,80},{16,82}... | collective-permute-start | bytes 147464 | tf_op jit(solution)/shard_map/ppermute | solution.py:323
  49.5 10.6 %collective-permute-start.7 = (f32[3,96,1024]{2,1,0:T(8,128)S(1)}, f32[3,96,1024]{2,1,0:T(8,128)S(1)}, u32[]{:S(2)}, u32[]{:S(2)}) collective-permute-start(f32[3,96,1024]{2,1,0:T(8,128)S(1)} %constant_dynamic-update-slice_fusion), channel_id=1, source_target_pairs={{0,1},{1,0},{2,3},{3,2},{4,5},{5,4},{6,7},{7,6},{8,9},{9,8},{10,11... | collective-permute-start | bytes 3538952 | tf_op jit(solution)/shard_map/ppermute | solution.py:413
  63.4 25.7 %all-to-all-start = ((f32[128,1,128]{2,1,0:T(1,128)}), f32[128,1,128]{2,1,0:T(1,128)S(1)}, u32[]{:S(2)}, u32[]{:S(2)}) async-start(f32[128,1,128]{2,1,0:T(1,128)} %bitcast.23), calls=%async_computation | async-start | bytes 131072 | tf_op jit(solution)/shard_map/all_to_all | solution.py:442

commit v9 on v8

--- a/solution.py
+++ b/solution.py
@@ -403,8 +403,10 @@
 
     message, outlet_message, *kept = lax.cond(mine == 0, forward_first, backward_first, None)
     for level_step in range(1, levels):
-        upper = both_ways(message, 0)
+        upper_early = both_ways(message[:steps_dev], 0)
+        upper_late = both_ways(message[steps_dev:], 0)
         side = both_ways(outlet_message, 1)
+        upper = jnp.concatenate([upper_early, upper_late], axis=0)
         later = backward_step if level_step + 1 < levels else backward_last
         message, outlet_message, *kept = lax.cond(
             mine == 0, forward_step, later, (upper, side)

time: 90.6 us -> 97.3 us (1.074)
  local copies, waits for them, and re-layouts: 4.26 us -> 8.1 us
  Pallas kernels: 8.12 us -> 11.8 us
  waiting for transfers between devices: 30 us -> 28.9 us
    ppermute x1, starting transfers between devices: 8.17 us -> 0.43 us  [body(): other = lax.ppermute(kept, 'group', [(0, 1), (1, 0)])]
    all_to_all x1, starting transfers between devices: 15.1 us -> 19.6 us  [body(): lax.all_to_all(replicated, ('level', 'basin'), 0, 0, tiled=True)]
    ppermute x6 -> x9, starting transfers between devices: 7.72 us -> 11.6 us  [both_ways(): return lax.ppermute(value, ('level', 'basin', 'group'), pairs)]
    pallas_call x4, Pallas kernels: 8.12 us -> 11.8 us  [vmem_call(): pl.pallas_call(kernel, out_shape=[jax.ShapeDtypeStruct(shape, jnp.float32...]
    slice x0 -> x3, local copies, waits for them, and re-layouts: none -> 2.12 us  [body(): upper_late = both_ways(message[steps_dev:], 0)]
    unnamed x7 -> x16, local copies, waits for them, and re-layouts: 0.76 us -> 2.44 us
    convert_element_type x1, other arithmetic: 3.3 us -> 1.86 us  [body(): confluence = confluence.astype(jnp.bfloat16)]
    select_n x1, other arithmetic: 1.27 us -> 0.04 us  [body(): jnp.where(mine == 0, jnp.concatenate([lateral, arrived], axis=0), jnp.con...]
  transfers between devices with their start and end apart: 9 -> 12, of which waited for: 7 -> 9; matrix products, arithmetic and copies ran while one was open for 11% -> 10% of each run, Pallas kernels for 0% -> 0%
where the time goes in v9:
time: 97.3 us; the launch traced here: 96.6 us
  starting transfers between devices  35 us (36%)
  waiting for transfers between devices  28.9 us (30%)
  Pallas kernels  11.8 us (12%)
  other arithmetic  9.07 us (9%)
  local copies, waits for them, and re-layouts  8.1 us (8%)
  matrix products  2.01 us (2%)
  between operations  1.64 us (2%)
    all_to_all x1, starting transfers between devices, body(): lax.all_to_all(replicated, ('level', 'basin'), 0, 0, tiled=True)  19.6 us
    ppermute x9, waiting for transfers between devices, both_ways(): return lax.ppermute(value, ('level', 'basin', 'group'), pairs)  16.6 us
    pallas_call x4, Pallas kernels, vmem_call(): pl.pallas_call(kernel, out_shape=[jax.ShapeDtypeStruct(shape, jnp.float32...  11.8 us
    ppermute x9, starting transfers between devices, both_ways(): return lax.ppermute(value, ('level', 'basin', 'group'), pairs)  11.6 us
    all_to_all x1, waiting for transfers between devices, body(): lax.all_to_all(replicated, ('level', 'basin'), 0, 0, tiled=True)  9.85 us
    ppermute x1, starting transfers between devices, body(): lax.ppermute(jnp.where(mine == 0, cotangent, lateral), 'group', [(0, 1),...  3.29 us
    convert_element_type x1, other arithmetic, body(): confluence_t = confluence_t.astype(jnp.bfloat16)  3.09 us
    ppermute x1, waiting for transfers between devices, body(): other = lax.ppermute(kept, 'group', [(0, 1), (1, 0)])  2.51 us
  transfers between devices with their start and end apart: 12, of which 9 were waited for; matrix products, arithmetic and copies ran while one was open for 10% of the time, Pallas kernels for 0%

profile of v9, /device:TPU:1, one launch (start us, length us, event | category | flops | bytes accessed | tf_op | source)
XLA Modules:
  0.0 96.6 jit_solution(12842163342204323049)
XLA Ops:
  1.6 3.3 %collective-permute-start = (f32[48,1024]{1,0:T(8,128)S(1)}, f32[48,1024]{1,0:T(8,128)S(1)}, u32[]{:S(2)}, u32[]{:S(2)}) collective-permute-start(f32[48,1024]{1,0:T(8,128)S(1)} %broadcast_select_fusion.1), channel_id=1, source_target_pairs={{0,1},{1,0},{2,3},{3,2},{4,5},{5,4},{6,7},{7,6},{8,9},{9,8},{10,11... | collective-permute-start | bytes 589832 | tf_op jit(solution)/shard_map/ppermute | solution.py:356
  7.1 1.6 %fusion.9 = (f32[128,1024]{1,0:T(8,128)}, f32[1024,128]{0,1:T(8,128)S(1)}) fusion(s32[1024]{0:T(1024)} %param.19), kind=kLoop, calls=%fused_computation.19 | loop fusion | flops 393216 | bytes 1052672 | tf_op jit(solution)/shard_map/convert_element_type | solution.py:337
  9.9 3.1 %add_convert_fusion.1 = bf16[1024,1152]{1,0:T(8,128)(2,1)} fusion(s32[1024]{0:T(1024)S(1)} %bitcast.55, s32[1024]{0:T(1024)S(1)} %bitcast.53, pred[1024]{0:T(1024)(128)(4,1)S(1)} %get-tuple-element.169, pred[1024]{0:T(1024)(128)(4,1)S(1)} %get-tuple-element.168), kind=kLoop, calls=%fused_computation.3 | loop fusion | flops 9437184 | bytes 2369536 | tf_op jit(solution)/shard_map/convert_element_type | solution.py:378
  13.1 3.3 %conditional.4 = ((f32[96,1024]{1,0:T(8,128)S(1)}, f32[96,128]{1,0:T(8,128)S(1)})) conditional(s32[]{:T(128)} %convert_element_type.41, (f32[8,1024]{1,0:T(8,128)S(1)}, f32[96,1024]{1,0:T(8,128)S(1)}, bf16[1024,1152]{1,0:T(8,128)(2,1)}) %tuple.45, (f32[8,1024]{1,0:T(8,128)S(1)}, f32[96,1024]{1,0:T(8,128)S(1)}) %tuple.46), branch_computations={%region_0.1_spmd, %region_1.2_spmd} | conditional | flops 453967872 | bytes 3620888 | solution.py:404
  13.2 3.3 %branch_0_fun.4 = (f32[96,1024]{1,0:T(8,128)}, f32[96,1024]{1,0:T(8,128)S(1)}, f32[96,128]{1,0:T(8,128)S(1)}) custom-call(f32[8,1024]{1,0:T(8,128)S(1)} %get-tuple-element.71.refs_0_, f32[96,1024]{1,0:T(8,128)S(1)} %get-tuple-element.72.refs_1_, bf16[1024,1152]{1,0:T(8,128)(2,1)} %get-tuple-element.73.refs_2_), custom_call_target="tpu_custom_call" | custom-call | flops 453967872 | bytes 3620864 | tf_op jit(solution)/shard_map/cond/branch_0_fun/pallas_call | solution.py:208
  16.5 1.3 %collective-permute-start.2 = (f32[48,1024]{1,0:T(8,128)S(1)}, f32[48,1024]{1,0:T(8,128)S(1)}, u32[]{:S(2)}, u32[]{:S(2)}) collective-permute-start(f32[48,1024]{1,0:T(8,128)S(1)} %get-tuple-element.162), channel_id=1, source_target_pairs={{0,64},{2,66},{4,68},{6,70},{8,72},{10,74},{12,76},{14,78},{16,80}... | collective-permute-start | bytes 589832 | tf_op jit(solution)/shard_map/ppermute | solution.py:323
  17.8 1.3 %collective-permute-start.1 = (f32[48,1024]{1,0:T(8,128)S(1)}, f32[48,1024]{1,0:T(8,128)S(1)}, u32[]{:S(2)}, u32[]{:S(2)}) collective-permute-start(f32[48,1024]{1,0:T(8,128)S(1)} %get-tuple-element.163), channel_id=1, source_target_pairs={{0,64},{2,66},{4,68},{6,70},{8,72},{10,74},{12,76},{14,78},{16,80}... | collective-permute-start | bytes 589832 | tf_op jit(solution)/shard_map/ppermute | solution.py:323
  19.1 1.9 %add_convert_fusion = bf16[1152,1024]{1,0:T(8,128)(2,1)S(1)} fusion(s32[1024]{0:T(1024)S(1)} %bitcast.56, s32[1024]{0:T(1024)S(1)} %bitcast.54, pred[1024]{0:T(1024)(128)(4,1)S(1)} %get-tuple-element.169, pred[1024]{0:T(1024)(128)(4,1)S(1)} %get-tuple-element.168), kind=kLoop, calls=%fused_computation | loop fusion | flops 9437184 | bytes 2369536 | tf_op jit(solution)/shard_map/convert_element_type | solution.py:371
  21.0 1.3 %collective-permute-start.3 = (f32[96,128]{1,0:T(8,128)S(1)}, f32[96,128]{1,0:T(8,128)S(1)}, u32[]{:S(2)}, u32[]{:S(2)}) collective-permute-start(f32[96,128]{1,0:T(8,128)S(1)} %get-tuple-element.129), channel_id=1, source_target_pairs={{0,66},{2,68},{4,70},{6,72},{8,74},{10,76},{12,78},{14,80},{16,82}... | collective-permute-start | bytes 147464 | tf_op jit(solution)/shard_map/ppermute | solution.py:323
  22.3 2.8 %collective-permute-done.1 = f32[48,1024]{1,0:T(8,128)S(1)} collective-permute-done((f32[48,1024]{1,0:T(8,128)S(1)}, f32[48,1024]{1,0:T(8,128)S(1)}, u32[]{:S(2)}, u32[]{:S(2)}) %collective-permute-start.1) | collective-permute-done | bytes 196640 | tf_op jit(solution)/shard_map/ppermute | solution.py:323
  25.1 1.6 %collective-permute-done.3 = f32[96,128]{1,0:T(8,128)S(1)} collective-permute-done((f32[96,128]{1,0:T(8,128)S(1)}, f32[96,128]{1,0:T(8,128)S(1)}, u32[]{:S(2)}, u32[]{:S(2)}) %collective-permute-start.3) | collective-permute-done | bytes 49184 | tf_op jit(solution)/shard_map/ppermute | solution.py:323
  26.7 3.6 %conditional.5 = (f32[96,1024]{1,0:T(8,128)}, f32[96,128]{1,0:T(8,128)S(1)}) conditional(s32[]{:T(128)} %convert_element_type.41, (f32[8,1024]{1,0:T(8,128)S(1)}, f32[96,1024]{1,0:T(8,128)S(1)}, f32[96,1024]{1,0:T(8,128)S(1)}, f32[96,128]{1,0:T(8,128)S(1)}, bf16[1024,1152]{1,0:T(8,128)(2,1)}) %tuple.47, (f32[8,1024]{1,0:T(8,128)S(1)}, ...), branch_computations={%region_2.3_spmd, %region_3.4_spmd} | conditional | flops 453967872 | bytes 4063248 | solution.py:411
  26.7 3.6 %branch_0_fun.5 = (f32[96,1024]{1,0:T(8,128)}, f32[96,1024]{1,0:T(8,128)}, f32[96,128]{1,0:T(8,128)S(1)}) custom-call(f32[8,1024]{1,0:T(8,128)S(1)} %get-tuple-element.78.refs_0_, f32[96,1024]{1,0:T(8,128)S(1)} %get-tuple-element.79.refs_1_, f32[96,1024]{1,0:T(8,128)S(1)} %get-tuple-element.80.refs_2_, f32[96,128]{1,0:T(8,128)S(1)} %get-tuple-element.81.refs_3_, ...), custom_call_target="tpu_custom_call" | custom-call | flops 453967872 | bytes 4063232 | tf_op jit(solution)/shard_map/cond/branch_0_fun/pallas_call | solution.py:208
  31.4 1.3 %collective-permute-start.4 = (f32[48,1024]{1,0:T(8,128)S(1)}, f32[48,1024]{1,0:T(8,128)S(1)}, u32[]{:S(2)}, u32[]{:S(2)}) collective-permute-start(f32[48,1024]{1,0:T(8,128)S(1)} %get-tuple-element.161), channel_id=1, source_target_pairs={{0,64},{2,66},{4,68},{6,70},{8,72},{10,74},{12,76},{14,78},{16,80}... | collective-permute-start | bytes 589832 | tf_op jit(solution)/shard_map/ppermute | solution.py:323
  35.3 3.8 %collective-permute-done.4 = f32[48,1024]{1,0:T(8,128)S(1)} collective-permute-done((f32[48,1024]{1,0:T(8,128)S(1)}, f32[48,1024]{1,0:T(8,128)S(1)}, u32[]{:S(2)}, u32[]{:S(2)}) %collective-permute-start.4) | collective-permute-done | bytes 196640 | tf_op jit(solution)/shard_map/ppermute | solution.py:323
  39.0 2.6 %collective-permute-done.5 = f32[48,1024]{1,0:T(8,128)S(1)} collective-permute-done((f32[48,1024]{1,0:T(8,128)S(1)}, f32[48,1024]{1,0:T(8,128)S(1)}, u32[]{:S(2)}, u32[]{:S(2)}) %collective-permute-start.5) | collective-permute-done | bytes 196640 | tf_op jit(solution)/shard_map/ppermute | solution.py:323
  41.7 3.6 %conditional.6 = (f32[96,1024]{1,0:T(8,128)}, f32[96,128]{1,0:T(8,128)S(1)}) conditional(s32[]{:T(128)} %convert_element_type.41, (f32[8,1024]{1,0:T(8,128)S(1)}, f32[96,1024]{1,0:T(8,128)S(1)}, f32[96,1024]{1,0:T(8,128)S(1)}, f32[96,128]{1,0:T(8,128)S(1)}, bf16[1024,1152]{1,0:T(8,128)(2,1)}) %tuple.49, (f32[8,1024]{1,0:T(8,128)S(1)}, ...), branch_computations={%region_4.5_spmd, %region_5.6_spmd} | conditional | flops 453967872 | bytes 4063248 | solution.py:411
  41.7 3.6 %branch_0_fun.6 = (f32[96,1024]{1,0:T(8,128)}, f32[96,1024]{1,0:T(8,128)}, f32[96,128]{1,0:T(8,128)S(1)}) custom-call(f32[8,1024]{1,0:T(8,128)S(1)} %get-tuple-element.92.refs_0_, f32[96,1024]{1,0:T(8,128)S(1)} %get-tuple-element.93.refs_1_, f32[96,1024]{1,0:T(8,128)S(1)} %get-tuple-element.94.refs_2_, f32[96,128]{1,0:T(8,128)S(1)} %get-tuple-element.95.refs_3_, ...), custom_call_target="tpu_custom_call" | custom-call | flops 453967872 | bytes 4063232 | tf_op jit(solution)/shard_map/cond/branch_0_fun/pallas_call | solution.py:208
  50.2 3.0 %collective-permute-done.7 = f32[48,1024]{1,0:T(8,128)S(1)} collective-permute-done((f32[48,1024]{1,0:T(8,128)S(1)}, f32[48,1024]{1,0:T(8,128)S(1)}, u32[]{:S(2)}, u32[]{:S(2)}) %collective-permute-start.7) | collective-permute-done | bytes 196640 | tf_op jit(solution)/shard_map/ppermute | solution.py:323
  53.3 2.1 %collective-permute-done.8 = f32[48,1024]{1,0:T(8,128)S(1)} collective-permute-done((f32[48,1024]{1,0:T(8,128)S(1)}, f32[48,1024]{1,0:T(8,128)S(1)}, u32[]{:S(2)}, u32[]{:S(2)}) %collective-permute-start.8) | collective-permute-done | bytes 196640 | tf_op jit(solution)/shard_map/ppermute | solution.py:323
  56.1 1.4 %conditional.7 = (f32[1,96,1024]{2,1,0:T(8,128)}, f32[1,96,1024]{2,1,0:T(8,128)S(1)}, f32[1,96,1024]{2,1,0:T(8,128)S(1)}) conditional(s32[]{:T(128)} %convert_element_type.41, (f32[8,1024]{1,0:T(8,128)S(1)}, f32[96,1024]{1,0:T(8,128)S(1)}, f32[96,1024]{1,0:T(8,128)S(1)}, f32[96,128]{1,0:T(8,128)S(1)}) %tuple.51, (f32[8,1024]{1,0:T(8,128)S(1)}, ...), branch_computations={%region_6.7_spmd, %region_7.8_spmd} | conditional | flops 453967872 | bytes 5636148 | solution.py:411
  59.0 2.5 %collective-permute-done.10 = f32[3,96,1024]{2,1,0:T(8,128)S(1)} collective-permute-done((f32[3,96,1024]{2,1,0:T(8,128)S(1)}, f32[3,96,1024]{2,1,0:T(8,128)S(1)}, u32[]{:S(2)}, u32[]{:S(2)}) %collective-permute-start.10) | collective-permute-done | bytes 1179680 | tf_op jit(solution)/shard_map/ppermute | solution.py:415
  65.4 19.6 %all-to-all-start = ((f32[128,1,128]{2,1,0:T(1,128)}), f32[128,1,128]{2,1,0:T(1,128)S(1)}, u32[]{:S(2)}, u32[]{:S(2)}) async-start(f32[128,1,128]{2,1,0:T(1,128)} %bitcast.23), calls=%async_computation | async-start | bytes 131072 | tf_op jit(solution)/shard_map/all_to_all | solution.py:444
  85.7 9.8 %all-to-all-done = f32[128,1,128]{2,1,0:T(1,128)S(1)} async-done(((f32[128,1,128]{2,1,0:T(1,128)}), f32[128,1,128]{2,1,0:T(1,128)S(1)}, u32[]{:S(2)}, u32[]{:S(2)}) %all-to-all-start) | async-done | bytes 65568 | tf_op jit(solution)/shard_map/all_to_all | solution.py:444
  (62 shorter events, 21.5 us)
Async XLA Ops:
  0.6 8.1 %copy-start = (f32[16,1024]{1,0:T(8,128)S(1)}, f32[16,1024]{1,0:T(8,128)}, u32[]{:S(2)}) copy-start(f32[16,1024]{1,0:T(8,128)} %param.18) | copy-start | bytes 196612
  0.6 8.1 %copy-start.5 = (f32[128,16,2]{0,2,1:T(2,128)S(1)}, f32[128,16,2]{0,2,1:T(2,128)}, u32[]{:S(2)}) copy-start(f32[128,16,2]{0,2,1:T(2,128)} %param.23) | copy-start | bytes 49156
  1.6 11.4 %collective-permute-start = (f32[48,1024]{1,0:T(8,128)S(1)}, f32[48,1024]{1,0:T(8,128)S(1)}, u32[]{:S(2)}, u32[]{:S(2)}) collective-permute-start(f32[48,1024]{1,0:T(8,128)S(1)} %broadcast_select_fusion.1), channel_id=1, source_target_pairs={{0,1},{1,0},{2,3},{3,2},{4,5},{5,4},{6,7},{7,6},{8,9},{9,8},{10,11... | collective-permute-start | bytes 589832 | tf_op jit(solution)/shard_map/ppermute | solution.py:356
  9.9 3.2 %copy-start.3 = (f32[48,1024]{1,0:T(8,128)S(1)}, f32[48,1024]{1,0:T(8,128)}, u32[]{:S(2)}) copy-start(f32[48,1024]{1,0:T(8,128)} %param.17) | copy-start | bytes 589828
  9.9 3.2 %copy-start.4 = (f32[48,1024]{1,0:T(8,128)S(1)}, f32[48,1024]{1,0:T(8,128)}, u32[]{:S(2)}) copy-start(f32[48,1024]{1,0:T(8,128)} %param.16) | copy-start | bytes 589828
  16.5 8.5 %collective-permute-start.2 = (f32[48,1024]{1,0:T(8,128)S(1)}, f32[48,1024]{1,0:T(8,128)S(1)}, u32[]{:S(2)}, u32[]{:S(2)}) collective-permute-start(f32[48,1024]{1,0:T(8,128)S(1)} %get-tuple-element.162), channel_id=1, source_target_pairs={{0,64},{2,66},{4,68},{6,70},{8,72},{10,74},{12,76},{14,78},{16,80}... | collective-permute-start | bytes 589832 | tf_op jit(solution)/shard_map/ppermute | solution.py:323
  17.8 7.2 %collective-permute-start.1 = (f32[48,1024]{1,0:T(8,128)S(1)}, f32[48,1024]{1,0:T(8,128)S(1)}, u32[]{:S(2)}, u32[]{:S(2)}) collective-permute-start(f32[48,1024]{1,0:T(8,128)S(1)} %get-tuple-element.163), channel_id=1, source_target_pairs={{0,64},{2,66},{4,68},{6,70},{8,72},{10,74},{12,76},{14,78},{16,80}... | collective-permute-start | bytes 589832 | tf_op jit(solution)/shard_map/ppermute | solution.py:323
  21.0 5.7 %collective-permute-start.3 = (f32[96,128]{1,0:T(8,128)S(1)}, f32[96,128]{1,0:T(8,128)S(1)}, u32[]{:S(2)}, u32[]{:S(2)}) collective-permute-start(f32[96,128]{1,0:T(8,128)S(1)} %get-tuple-element.129), channel_id=1, source_target_pairs={{0,66},{2,68},{4,70},{6,72},{8,74},{10,76},{12,78},{14,80},{16,82}... | collective-permute-start | bytes 147464 | tf_op jit(solution)/shard_map/ppermute | solution.py:323
  31.4 7.7 %collective-permute-start.4 = (f32[48,1024]{1,0:T(8,128)S(1)}, f32[48,1024]{1,0:T(8,128)S(1)}, u32[]{:S(2)}, u32[]{:S(2)}) collective-permute-start(f32[48,1024]{1,0:T(8,128)S(1)} %get-tuple-element.161), channel_id=1, source_target_pairs={{0,64},{2,66},{4,68},{6,70},{8,72},{10,74},{12,76},{14,78},{16,80}... | collective-permute-start | bytes 589832 | tf_op jit(solution)/shard_map/ppermute | solution.py:323
  32.7 9.0 %collective-permute-start.5 = (f32[48,1024]{1,0:T(8,128)S(1)}, f32[48,1024]{1,0:T(8,128)S(1)}, u32[]{:S(2)}, u32[]{:S(2)}) collective-permute-start(f32[48,1024]{1,0:T(8,128)S(1)} %get-tuple-element.160), channel_id=1, source_target_pairs={{0,64},{2,66},{4,68},{6,70},{8,72},{10,74},{12,76},{14,78},{16,80}... | collective-permute-start | bytes 589832 | tf_op jit(solution)/shard_map/ppermute | solution.py:323
  34.0 7.7 %collective-permute-start.6 = (f32[96,128]{1,0:T(8,128)S(1)}, f32[96,128]{1,0:T(8,128)S(1)}, u32[]{:S(2)}, u32[]{:S(2)}) collective-permute-start(f32[96,128]{1,0:T(8,128)S(1)} %get-tuple-element.131), channel_id=1, source_target_pairs={{0,66},{2,68},{4,70},{6,72},{8,74},{10,76},{12,78},{14,80},{16,82}... | collective-permute-start | bytes 147464 | tf_op jit(solution)/shard_map/ppermute | solution.py:323
  46.3 6.9 %collective-permute-start.7 = (f32[48,1024]{1,0:T(8,128)S(1)}, f32[48,1024]{1,0:T(8,128)S(1)}, u32[]{:S(2)}, u32[]{:S(2)}) collective-permute-start(f32[48,1024]{1,0:T(8,128)S(1)} %get-tuple-element.159), channel_id=1, source_target_pairs={{0,64},{2,66},{4,68},{6,70},{8,72},{10,74},{12,76},{14,78},{16,80}... | collective-permute-start | bytes 589832 | tf_op jit(solution)/shard_map/ppermute | solution.py:323
  47.6 7.7 %collective-permute-start.8 = (f32[48,1024]{1,0:T(8,128)S(1)}, f32[48,1024]{1,0:T(8,128)S(1)}, u32[]{:S(2)}, u32[]{:S(2)}) collective-permute-start(f32[48,1024]{1,0:T(8,128)S(1)} %get-tuple-element.158), channel_id=1, source_target_pairs={{0,64},{2,66},{4,68},{6,70},{8,72},{10,74},{12,76},{14,78},{16,80}... | collective-permute-start | bytes 589832 | tf_op jit(solution)/shard_map/ppermute | solution.py:323
  48.9 7.2 %collective-permute-start.9 = (f32[96,128]{1,0:T(8,128)S(1)}, f32[96,128]{1,0:T(8,128)S(1)}, u32[]{:S(2)}, u32[]{:S(2)}) collective-permute-start(f32[96,128]{1,0:T(8,128)S(1)} %get-tuple-element.133), channel_id=1, source_target_pairs={{0,66},{2,68},{4,70},{6,72},{8,74},{10,76},{12,78},{14,80},{16,82}... | collective-permute-start | bytes 147464 | tf_op jit(solution)/shard_map/ppermute | solution.py:323
  58.6 2.9 %collective-permute-start.10 = (f32[3,96,1024]{2,1,0:T(8,128)S(1)}, f32[3,96,1024]{2,1,0:T(8,128)S(1)}, u32[]{:S(2)}, u32[]{:S(2)}) collective-permute-start(f32[3,96,1024]{2,1,0:T(8,128)S(1)} %constant_dynamic-update-slice_fusion.6), channel_id=1, source_target_pairs={{0,1},{1,0},{2,3},{3,2},{4,5},{5,4},{6,7},{7,6},{8,9},{9,8},{10,11... | collective-permute-start | bytes 3538952 | tf_op jit(solution)/shard_map/ppermute | solution.py:415
  61.7 1.0 %copy-start.1 = (f32[128,1024]{1,0:T(8,128)S(1)}, f32[128,1024]{1,0:T(8,128)}, u32[]{:S(2)}) copy-start(f32[128,1024]{1,0:T(8,128)} %get-tuple-element.166) | copy-start | bytes 1572868
  65.4 30.2 %all-to-all-start = ((f32[128,1,128]{2,1,0:T(1,128)}), f32[128,1,128]{2,1,0:T(1,128)S(1)}, u32[]{:S(2)}, u32[]{:S(2)}) async-start(f32[128,1,128]{2,1,0:T(1,128)} %bitcast.23), calls=%async_computation | async-start | bytes 131072 | tf_op jit(solution)/shard_map/all_to_all | solution.py:444

commit v10 on v8

--- a/solution.py
+++ b/solution.py
@@ -110,10 +110,11 @@
 
 def forward_kernel(*refs, has_inflow):
     if has_inflow:
-        coef_ref, upper_ref, side_ref, conf_ref, lateral_ref, out_ref, outlet_ref, inflow_ref = refs
+        coef_ref, upper_ref, side_ref, conf_ref, early_ref, late_ref, out_ref, outlet_ref, inflow_ref = refs
     else:
-        coef_ref, lateral_ref, out_ref, outlet_ref = refs
-    steps, width = lateral_ref.shape
+        coef_ref, early_ref, late_ref, out_ref, outlet_ref = refs
+    half, width = early_ref.shape
+    steps = 2 * half
     narrow = outlet_ref.shape[1]
     tile = 8
     gain_now, gain_prev, gain_side = coef_ref[0:1, :], coef_ref[1:2, :], coef_ref[2:3, :]
@@ -134,10 +135,11 @@
         keep_steps.append(factor)
         factor = factor * factor
 
-    def advance(block, carry):
+    def advance(block, carry, lateral_ref, first):
         state, before = carry
-        rows = pl.ds(pl.multiple_of(block * tile, tile), tile)
-        drive_side = gain_side * lateral_ref[rows, :]
+        rows = pl.ds(pl.multiple_of((block + first) * tile, tile), tile)
+        own_rows = pl.ds(pl.multiple_of(block * tile, tile), tile)
+        drive_side = gain_side * lateral_ref[own_rows, :]
         if has_inflow:
             now = inflow_ref[rows, :]
             earlier = jnp.where(
@@ -160,13 +162,19 @@
         return block_state[tile - 1 : tile, :], before
 
     zero = jnp.zeros_like(keep)
-    lax.fori_loop(0, steps // tile, advance, (zero, zero), unroll=2)
+    blocks = half // tile
+    carry = lax.fori_loop(
+        0, blocks, lambda block, carry: advance(block, carry, early_ref, 0), (zero, zero), unroll=2
+    )
+    lax.fori_loop(
+        0, blocks, lambda block, carry: advance(block, carry, late_ref, blocks), carry, unroll=2
+    )
 
 
 def backward_kernel(*refs, has_down, emit):
     refs = list(refs)
-    coef_ref, cot_ref = refs[0], refs[1]
-    rest = refs[2:]
+    coef_ref, early_ref, late_ref = refs[0], refs[1], refs[2]
+    rest = refs[3:]
     if has_down:
         down_ref, side_ref = rest[0], rest[1]
         rest = rest[2:]
@@ -174,14 +182,14 @@
         conf_ref, adj_ref, own_ref, spill_ref, work_ref = rest
     else:
         (adj_ref,) = rest
-    steps = cot_ref.shape[0]
+    half = early_ref.shape[0]
+    steps = 2 * half
     gain_now, gain_prev = coef_ref[0:1, :], coef_ref[1:2, :]
     keep, live = coef_ref[3:4, :], coef_ref[4:5, :]
 
-    def advance(position, carry):
-        hour = steps - 1 - position
+    def advance(hour, carry, cot_ref, cot_at):
         state, later = carry
-        load = cot_ref[pl.ds(hour, 1), :]
+        load = cot_ref[pl.ds(cot_at, 1), :]
         if has_down:
             down = down_ref[pl.ds(hour, 1), :]
             side = side_ref[pl.ds(hour, 1), :]
@@ -195,7 +203,20 @@
         return state, state
 
     zero = jnp.zeros_like(keep)
-    lax.fori_loop(0, steps, advance, (zero, zero), unroll=8)
+    carry = lax.fori_loop(
+        0,
+        half,
+        lambda position, carry: advance(steps - 1 - position, carry, late_ref, half - 1 - position),
+        (zero, zero),
+        unroll=8,
+    )
+    lax.fori_loop(
+        0,
+        half,
+        lambda position, carry: advance(half - 1 - position, carry, early_ref, half - 1 - position),
+        carry,
+        unroll=8,
+    )
     if emit:
         spread = jnp.dot(split_pair(work_ref[...]), conf_ref[...], preferred_element_type=jnp.float32)
         width = own_ref.shape[1]
@@ -219,26 +240,28 @@
     )(*args)
 
 
-def routed(coef, lateral_all, upper=None, side=None, confluence=None):
-    steps, width = lateral_all.shape
+def routed(coef, early, late, upper=None, side=None, confluence=None):
+    half, width = early.shape
+    steps = 2 * half
     narrow = width // 8
     if upper is None:
         kernel = functools.partial(forward_kernel, has_inflow=False)
-        flow, outlet = vmem_call(kernel, [(steps, width), (steps, narrow)], coef, lateral_all)
+        flow, outlet = vmem_call(kernel, [(steps, width), (steps, narrow)], coef, early, late)
         return flow, outlet, None
     kernel = functools.partial(forward_kernel, has_inflow=True)
     return vmem_call(
         kernel,
         [(steps, width), (steps, narrow), (steps, width)],
-        coef, upper, side, confluence, lateral_all,
-    )
-
-
-def adjoined(coef, cotangent_all, down=None, side=None, confluence_t=None):
-    steps, width = cotangent_all.shape
+        coef, upper, side, confluence, early, late,
+    )
+
+
+def adjoined(coef, early, late, down=None, side=None, confluence_t=None):
+    half, width = early.shape
+    steps = 2 * half
     emit = confluence_t is not None
     kernel = functools.partial(backward_kernel, has_down=down is not None, emit=emit)
-    args = (coef, cotangent_all) if down is None else (coef, cotangent_all, down, side)
+    args = (coef, early, late) if down is None else (coef, early, late, down, side)
     if not emit:
         return vmem_call(kernel, [(steps, width)], *args)[0], None, None
     adjoint, own, spill = vmem_call(
@@ -354,14 +377,9 @@
         [gain_now, gain_prev, gain_side, retain, live_mask, zero_row, zero_row, zero_row], axis=0
     )
     arrived = lax.ppermute(jnp.where(mine == 0, cotangent, lateral), "group", [(0, 1), (1, 0)])
-    window = jnp.where(
-        mine == 0,
-        jnp.concatenate([lateral, arrived], axis=0),
-        jnp.concatenate([arrived, cotangent], axis=0),
-    )
-    lateral_all = window
-    cotangent_all = window
-    steps_all = window.shape[0]
+    early = jnp.where(mine == 0, lateral, arrived)
+    late = jnp.where(mine == 0, arrived, cotangent)
+    steps_all = 2 * steps_dev
     source_ids = lax.broadcasted_iota(jnp.int32, (reach_dev + outlets, reach_dev), 0)
     confluence = jnp.zeros((reach_dev + outlets, reach_dev), jnp.float32)
     for upslot in range(up_count):
@@ -379,35 +397,42 @@
     zero_flow = jnp.zeros((steps_all, reach_dev), jnp.float32)
 
     def forward_first(operands):
-        flow, outlet, unused = routed(coef, lateral_all)
-        return flow, outlet, flow, zero_flow, lateral_all
+        flow, outlet, unused = routed(coef, early, late)
+        return flow, outlet, flow, zero_flow, zero_flow
 
     def backward_first(operands):
-        adjoint, own, side = adjoined(coef, cotangent_all, confluence_t=confluence_t)
+        adjoint, own, side = adjoined(coef, early, late, confluence_t=confluence_t)
         return own, side, adjoint, zero_flow, zero_flow
 
     def forward_step(operands):
         upper, side = operands
-        flow, outlet, inflow = routed(coef, lateral_all, upper, side, confluence)
-        return flow, outlet, flow, inflow, lateral_all
+        flow, outlet, inflow = routed(coef, early, late, upper, side, confluence)
+        return flow, outlet, flow, inflow, zero_flow
+
+    def forward_last(operands):
+        flow, outlet, first, inflow, unused = forward_step(operands)
+        return flow, outlet, first, inflow, jnp.concatenate([early, late], axis=0)
 
     def backward_step(operands):
         upper, side = operands
-        adjoint, own, side = adjoined(coef, cotangent_all, upper, side, confluence_t)
+        adjoint, own, side = adjoined(coef, early, late, upper, side, confluence_t)
         return own, side, adjoint, zero_flow, zero_flow
 
     def backward_last(operands):
         upper, side = operands
-        adjoint, unused, unused_side = adjoined(coef, cotangent_all, upper, side)
+        adjoint, unused, unused_side = adjoined(coef, early, late, upper, side)
         return zero_flow, side, adjoint, zero_flow, zero_flow
 
     message, outlet_message, *kept = lax.cond(mine == 0, forward_first, backward_first, None)
     for level_step in range(1, levels):
         upper = both_ways(message, 0)
         side = both_ways(outlet_message, 1)
-        later = backward_step if level_step + 1 < levels else backward_last
+        last = level_step + 1 == levels
         message, outlet_message, *kept = lax.cond(
-            mine == 0, forward_step, later, (upper, side)
+            mine == 0,
+            forward_last if last else forward_step,
+            backward_last if last else backward_step,
+            (upper, side),
         )
     kept = jnp.stack(kept, axis=0)
     other = lax.ppermute(kept, "group", [(0, 1), (1, 0)])

time: 90.6 us -> 91.2 us (level)
  no operation moved by 1% of the time
where the time goes in v10:
time: 91.2 us; the launch traced here: 90.7 us
  starting transfers between devices  34.3 us (38%)
  waiting for transfers between devices  30 us (33%)
  other arithmetic  10.3 us (11%)
  Pallas kernels  8.22 us (9%)
  local copies, waits for them, and re-layouts  4.26 us (5%)
  matrix products  2.01 us (2%)
  between operations  1.55 us (2%)
    ppermute x6, waiting for transfers between devices, both_ways(): return lax.ppermute(value, ('level', 'basin', 'group'), pairs)  17.6 us
    all_to_all x1, starting transfers between devices, body(): lax.all_to_all(replicated, ('level', 'basin'), 0, 0, tiled=True)  15.1 us
    all_to_all x1, waiting for transfers between devices, body(): lax.all_to_all(replicated, ('level', 'basin'), 0, 0, tiled=True)  9.85 us
    ppermute x1, starting transfers between devices, body(): other = lax.ppermute(kept, 'group', [(0, 1), (1, 0)])  8.27 us
    pallas_call x4, Pallas kernels, vmem_call(): pl.pallas_call(kernel, out_shape=[jax.ShapeDtypeStruct(shape, jnp.float32...  8.22 us
    ppermute x6, starting transfers between devices, both_ways(): return lax.ppermute(value, ('level', 'basin', 'group'), pairs)  7.72 us
    convert_element_type x1, other arithmetic, body(): confluence = confluence.astype(jnp.bfloat16)  3.31 us
    ppermute x1, starting transfers between devices, body(): lax.ppermute(jnp.where(mine == 0, cotangent, lateral), 'group', [(0, 1),...  3.2 us
  transfers between devices with their start and end apart: 9, of which 7 were waited for; matrix products, arithmetic and copies ran while one was open for 11% of the time, Pallas kernels for 0%

profile of v10, /device:TPU:1, one launch (start us, length us, event | category | flops | bytes accessed | tf_op | source)
XLA Modules:
  0.0 90.7 jit_solution(8433214229477722770)
XLA Ops:
  0.7 1.6 %broadcast_select_fusion.3 = f32[48,1024]{1,0:T(8,128)} fusion(f32[48,1024]{1,0:T(8,128)} %param.17, f32[48,1024]{1,0:T(8,128)} %param.16, pred[]{:T(512)S(6)} %eq.59), kind=kLoop, calls=%fused_computation.38 | loop fusion | flops 49152 | bytes 589825 | tf_op jit(solution)/shard_map/jit(_where)/select_n | solution.py:379
  2.3 3.2 %collective-permute-start = (f32[48,1024]{1,0:T(8,128)}, f32[48,1024]{1,0:T(8,128)}, u32[]{:S(2)}, u32[]{:S(2)}) collective-permute-start(f32[48,1024]{1,0:T(8,128)} %broadcast_select_fusion.3), channel_id=1, source_target_pairs={{0,1},{1,0},{2,3},{3,2},{4,5},{5,4},{6,7},{7,6},{8,9},{9,8},{10,11... | collective-permute-start | bytes 589832 | tf_op jit(solution)/shard_map/ppermute | solution.py:379
  8.4 1.1 %fusion.5 = f32[1024,2]{0,1:T(2,128)S(1)} fusion(f32[1024,128]{0,1:T(8,128)S(1)} %get-tuple-element.187, f32[16,1024]{1,0:T(8,128)S(1)} %copy-done, f32[128,2,16]{0,1,2:T(2,128)S(1)} %bitcast.64), kind=kOutput, calls=%fused_computation.13 | convolution fusion | flops 50853888 | bytes 614400 | tf_op jit(solution)/shard_map/dot_general | solution.py:361
  9.6 2.0 %add_convert_fusion.1 = bf16[1024,1152]{1,0:T(8,128)(2,1)S(1)} fusion(s32[1024]{0:T(1024)S(1)} %bitcast.57, s32[1024]{0:T(1024)S(1)} %bitcast.55, pred[1024]{0:T(1024)(128)(4,1)S(1)} %get-tuple-element.189, pred[1024]{0:T(1024)(128)(4,1)S(1)} %get-tuple-element.188), kind=kLoop, calls=%fused_computation.4 | loop fusion | flops 9437184 | bytes 2369536 | tf_op jit(solution)/shard_map/convert_element_type | solution.py:396
  12.8 1.8 %conditional.4 = ((f32[96,1024]{1,0:T(8,128)}, f32[96,128]{1,0:T(8,128)S(1)})) conditional(s32[]{:T(128)} %convert_element_type.41, (f32[8,1024]{1,0:T(8,128)S(1)}, f32[48,1024]{1,0:T(8,128)S(1)}, f32[48,1024]{1,0:T(8,128)S(1)}, bf16[1024,1152]{1,0:T(8,128)(2,1)S(1)}) %tuple.45, (f32[8,1024]{1,0:T(8,128)S(1)}, f32[48,1024]{1,0:T(8,128)S(1)}, ...), branch_computations={%region_0.1_spmd, %region_1.2_spmd} | conditional | flops 453967872 | bytes 3620888 | solution.py:426
  12.9 1.8 %branch_0_fun.4 = (f32[96,1024]{1,0:T(8,128)}, f32[96,1024]{1,0:T(8,128)}, f32[96,128]{1,0:T(8,128)S(1)}) custom-call(f32[8,1024]{1,0:T(8,128)S(1)} %get-tuple-element.87.refs_0_, f32[48,1024]{1,0:T(8,128)S(1)} %get-tuple-element.88.refs_1_, f32[48,1024]{1,0:T(8,128)S(1)} %get-tuple-element.89.refs_2_, bf16[1024,1152]{1,0:T(8,128)(2,1)S(1)} %get-tuple-element.90.refs_3_), custom_call_target="tpu_custom_call" | custom-call | flops 453967872 | bytes 3620864 | tf_op jit(solution)/shard_map/cond/branch_0_fun/pallas_call | solution.py:229
  14.6 1.3 %collective-permute-start.2 = (f32[96,128]{1,0:T(8,128)S(1)}, f32[96,128]{1,0:T(8,128)S(1)}, u32[]{:S(2)}, u32[]{:S(2)}) collective-permute-start(f32[96,128]{1,0:T(8,128)S(1)} %get-tuple-element.153), channel_id=1, source_target_pairs={{0,66},{2,68},{4,70},{6,72},{8,74},{10,76},{12,78},{14,80},{16,82}... | collective-permute-start | bytes 147464 | tf_op jit(solution)/shard_map/ppermute | solution.py:346
  15.9 1.3 %collective-permute-start.1 = (f32[96,1024]{1,0:T(8,128)}, f32[96,1024]{1,0:T(8,128)}, u32[]{:S(2)}, u32[]{:S(2)}) collective-permute-start(f32[96,1024]{1,0:T(8,128)} %get-tuple-element.152), channel_id=1, source_target_pairs={{0,64},{2,66},{4,68},{6,70},{8,72},{10,74},{12,76},{14,78},{16,80}... | collective-permute-start | bytes 1179656 | tf_op jit(solution)/shard_map/ppermute | solution.py:346
  17.2 3.3 %add_convert_fusion = bf16[1152,1024]{1,0:T(8,128)(2,1)} fusion(s32[1024]{0:T(1024)S(1)} %bitcast.58, s32[1024]{0:T(1024)S(1)} %bitcast.56, pred[1024]{0:T(1024)(128)(4,1)S(1)} %get-tuple-element.189, pred[1024]{0:T(1024)(128)(4,1)S(1)} %get-tuple-element.188), kind=kLoop, calls=%fused_computation.1 | loop fusion | flops 9437184 | bytes 2369536 | tf_op jit(solution)/shard_map/convert_element_type | solution.py:389
  20.5 4.2 %collective-permute-done.1 = f32[96,1024]{1,0:T(8,128)} collective-permute-done((f32[96,1024]{1,0:T(8,128)}, f32[96,1024]{1,0:T(8,128)}, u32[]{:S(2)}, u32[]{:S(2)}) %collective-permute-start.1) | collective-permute-done | bytes 393248 | tf_op jit(solution)/shard_map/ppermute | solution.py:346
  24.7 2.9 %conditional.5 = (f32[96,1024]{1,0:T(8,128)}, f32[96,128]{1,0:T(8,128)S(1)}) conditional(s32[]{:T(128)} %convert_element_type.41, (f32[8,1024]{1,0:T(8,128)S(1)}, f32[48,1024]{1,0:T(8,128)S(1)}, f32[48,1024]{1,0:T(8,128)S(1)}, f32[96,1024]{1,0:T(8,128)}, f32[96,128]{1,0:T(8,128)S(1)}, /*index=5*/bf16[1024,1152]{1,0:T(8,128)(2,1)S(1)}) %tuple.47, ...), branch_computations={%region_2.3_spmd, %region_3.4_spmd} | conditional | flops 453967872 | bytes 4063248 | solution.py:431
  24.7 2.9 %branch_0_fun.5 = (f32[96,1024]{1,0:T(8,128)}, f32[96,1024]{1,0:T(8,128)}, f32[96,128]{1,0:T(8,128)S(1)}) custom-call(f32[8,1024]{1,0:T(8,128)S(1)} %get-tuple-element.96.refs_0_, f32[48,1024]{1,0:T(8,128)S(1)} %get-tuple-element.97.refs_1_, f32[48,1024]{1,0:T(8,128)S(1)} %get-tuple-element.98.refs_2_, f32[96,1024]{1,0:T(8,128)} %get-tuple-element.99.refs_3_, ...), custom_call_target="tpu_custom_call" | custom-call | flops 453967872 | bytes 4063232 | tf_op jit(solution)/shard_map/cond/branch_0_fun/pallas_call | solution.py:229
  27.7 1.3 %collective-permute-start.3 = (f32[96,1024]{1,0:T(8,128)}, f32[96,1024]{1,0:T(8,128)}, u32[]{:S(2)}, u32[]{:S(2)}) collective-permute-start(f32[96,1024]{1,0:T(8,128)} %get-tuple-element.154), channel_id=1, source_target_pairs={{0,64},{2,66},{4,68},{6,70},{8,72},{10,74},{12,76},{14,78},{16,80}... | collective-permute-start | bytes 1179656 | tf_op jit(solution)/shard_map/ppermute | solution.py:346
  29.0 1.3 %collective-permute-start.4 = (f32[96,128]{1,0:T(8,128)S(1)}, f32[96,128]{1,0:T(8,128)S(1)}, u32[]{:S(2)}, u32[]{:S(2)}) collective-permute-start(f32[96,128]{1,0:T(8,128)S(1)} %get-tuple-element.155), channel_id=1, source_target_pairs={{0,66},{2,68},{4,70},{6,72},{8,74},{10,76},{12,78},{14,80},{16,82}... | collective-permute-start | bytes 147464 | tf_op jit(solution)/shard_map/ppermute | solution.py:346
  30.3 6.1 %collective-permute-done.4 = f32[96,128]{1,0:T(8,128)S(1)} collective-permute-done((f32[96,128]{1,0:T(8,128)S(1)}, f32[96,128]{1,0:T(8,128)S(1)}, u32[]{:S(2)}, u32[]{:S(2)}) %collective-permute-start.4) | collective-permute-done | bytes 49184 | tf_op jit(solution)/shard_map/ppermute | solution.py:346
  37.0 3.0 %conditional.6 = (f32[96,1024]{1,0:T(8,128)}, f32[96,128]{1,0:T(8,128)S(1)}) conditional(s32[]{:T(128)} %convert_element_type.41, (f32[8,1024]{1,0:T(8,128)S(1)}, f32[48,1024]{1,0:T(8,128)S(1)}, f32[48,1024]{1,0:T(8,128)S(1)}, f32[96,1024]{1,0:T(8,128)}, f32[96,128]{1,0:T(8,128)S(1)}, /*index=5*/bf16[1024,1152]{1,0:T(8,128)(2,1)S(1)}) %tuple.49, ...), branch_computations={%region_4.5_spmd, %region_5.6_spmd} | conditional | flops 453967872 | bytes 4063248 | solution.py:431
  37.0 2.9 %branch_0_fun.6 = (f32[96,1024]{1,0:T(8,128)}, f32[96,1024]{1,0:T(8,128)}, f32[96,128]{1,0:T(8,128)S(1)}) custom-call(f32[8,1024]{1,0:T(8,128)S(1)} %get-tuple-element.112.refs_0_, f32[48,1024]{1,0:T(8,128)S(1)} %get-tuple-element.113.refs_1_, f32[48,1024]{1,0:T(8,128)S(1)} %get-tuple-element.114.refs_2_, f32[96,1024]{1,0:T(8,128)} %get-tuple-element.115.refs_3_, ...), custom_call_target="tpu_custom_call" | custom-call | flops 453967872 | bytes 4063232 | tf_op jit(solution)/shard_map/cond/branch_0_fun/pallas_call | solution.py:229
  40.0 1.3 %collective-permute-start.5 = (f32[96,1024]{1,0:T(8,128)}, f32[96,1024]{1,0:T(8,128)S(1)}, u32[]{:S(2)}, u32[]{:S(2)}) collective-permute-start(f32[96,1024]{1,0:T(8,128)} %get-tuple-element.156), channel_id=1, source_target_pairs={{0,64},{2,66},{4,68},{6,70},{8,72},{10,74},{12,76},{14,78},{16,80}... | collective-permute-start | bytes 1179656 | tf_op jit(solution)/shard_map/ppermute | solution.py:346
  41.3 1.3 %collective-permute-start.6 = (f32[96,128]{1,0:T(8,128)S(1)}, f32[96,128]{1,0:T(8,128)S(1)}, u32[]{:S(2)}, u32[]{:S(2)}) collective-permute-start(f32[96,128]{1,0:T(8,128)S(1)} %get-tuple-element.157), channel_id=1, source_target_pairs={{0,66},{2,68},{4,70},{6,72},{8,74},{10,76},{12,78},{14,80},{16,82}... | collective-permute-start | bytes 147464 | tf_op jit(solution)/shard_map/ppermute | solution.py:346
  42.6 6.4 %collective-permute-done.6 = f32[96,128]{1,0:T(8,128)S(1)} collective-permute-done((f32[96,128]{1,0:T(8,128)S(1)}, f32[96,128]{1,0:T(8,128)S(1)}, u32[]{:S(2)}, u32[]{:S(2)}) %collective-permute-start.6) | collective-permute-done | bytes 49184 | tf_op jit(solution)/shard_map/ppermute | solution.py:346
  50.0 8.3 %collective-permute-start.7 = (f32[3,96,1024]{2,1,0:T(8,128)S(1)}, f32[3,96,1024]{2,1,0:T(8,128)S(1)}, u32[]{:S(2)}, u32[]{:S(2)}) collective-permute-start(f32[3,96,1024]{2,1,0:T(8,128)S(1)} %constant_dynamic-update-slice_fusion), channel_id=1, source_target_pairs={{0,1},{1,0},{2,3},{3,2},{4,5},{5,4},{6,7},{7,6},{8,9},{9,8},{10,11... | collective-permute-start | bytes 3538952 | tf_op jit(solution)/shard_map/ppermute | solution.py:438
  58.3 2.5 %collective-permute-done.7 = f32[3,96,1024]{2,1,0:T(8,128)S(1)} collective-permute-done((f32[3,96,1024]{2,1,0:T(8,128)S(1)}, f32[3,96,1024]{2,1,0:T(8,128)S(1)}, u32[]{:S(2)}, u32[]{:S(2)}) %collective-permute-start.7) | collective-permute-done | bytes 1179680 | tf_op jit(solution)/shard_map/ppermute | solution.py:438
  64.0 15.1 %all-to-all-start = ((f32[128,1,128]{2,1,0:T(1,128)}), f32[128,1,128]{2,1,0:T(1,128)S(1)}, u32[]{:S(2)}, u32[]{:S(2)}) async-start(f32[128,1,128]{2,1,0:T(1,128)} %bitcast.23), calls=%async_computation | async-start | bytes 131072 | tf_op jit(solution)/shard_map/all_to_all | solution.py:467
  79.8 9.9 %all-to-all-done = f32[128,1,128]{2,1,0:T(1,128)S(1)} async-done(((f32[128,1,128]{2,1,0:T(1,128)}), f32[128,1,128]{2,1,0:T(1,128)S(1)}, u32[]{:S(2)}, u32[]{:S(2)}) %all-to-all-start) | async-done | bytes 65568 | tf_op jit(solution)/shard_map/all_to_all | solution.py:467
  (41 shorter events, 10.7 us)
Async XLA Ops:
  0.6 7.8 %copy-start = (f32[16,1024]{1,0:T(8,128)S(1)}, f32[16,1024]{1,0:T(8,128)}, u32[]{:S(2)}) copy-start(f32[16,1024]{1,0:T(8,128)} %param.18) | copy-start | bytes 196612
  0.6 7.8 %copy-start.1 = (f32[128,16,2]{0,2,1:T(2,128)S(1)}, f32[128,16,2]{0,2,1:T(2,128)}, u32[]{:S(2)}) copy-start(f32[128,16,2]{0,2,1:T(2,128)} %param.23) | copy-start | bytes 49156
  2.3 9.5 %collective-permute-start = (f32[48,1024]{1,0:T(8,128)}, f32[48,1024]{1,0:T(8,128)}, u32[]{:S(2)}, u32[]{:S(2)}) collective-permute-start(f32[48,1024]{1,0:T(8,128)} %broadcast_select_fusion.3), channel_id=1, source_target_pairs={{0,1},{1,0},{2,3},{3,2},{4,5},{5,4},{6,7},{7,6},{8,9},{9,8},{10,11... | collective-permute-start | bytes 589832 | tf_op jit(solution)/shard_map/ppermute | solution.py:379
  14.6 5.9 %collective-permute-start.2 = (f32[96,128]{1,0:T(8,128)S(1)}, f32[96,128]{1,0:T(8,128)S(1)}, u32[]{:S(2)}, u32[]{:S(2)}) collective-permute-start(f32[96,128]{1,0:T(8,128)S(1)} %get-tuple-element.153), channel_id=1, source_target_pairs={{0,66},{2,68},{4,70},{6,72},{8,74},{10,76},{12,78},{14,80},{16,82}... | collective-permute-start | bytes 147464 | tf_op jit(solution)/shard_map/ppermute | solution.py:346
  15.9 8.8 %collective-permute-start.1 = (f32[96,1024]{1,0:T(8,128)}, f32[96,1024]{1,0:T(8,128)}, u32[]{:S(2)}, u32[]{:S(2)}) collective-permute-start(f32[96,1024]{1,0:T(8,128)} %get-tuple-element.152), channel_id=1, source_target_pairs={{0,64},{2,66},{4,68},{6,70},{8,72},{10,74},{12,76},{14,78},{16,80}... | collective-permute-start | bytes 1179656 | tf_op jit(solution)/shard_map/ppermute | solution.py:346
  27.7 9.4 %collective-permute-start.3 = (f32[96,1024]{1,0:T(8,128)}, f32[96,1024]{1,0:T(8,128)}, u32[]{:S(2)}, u32[]{:S(2)}) collective-permute-start(f32[96,1024]{1,0:T(8,128)} %get-tuple-element.154), channel_id=1, source_target_pairs={{0,64},{2,66},{4,68},{6,70},{8,72},{10,74},{12,76},{14,78},{16,80}... | collective-permute-start | bytes 1179656 | tf_op jit(solution)/shard_map/ppermute | solution.py:346
  29.0 7.4 %collective-permute-start.4 = (f32[96,128]{1,0:T(8,128)S(1)}, f32[96,128]{1,0:T(8,128)S(1)}, u32[]{:S(2)}, u32[]{:S(2)}) collective-permute-start(f32[96,128]{1,0:T(8,128)S(1)} %get-tuple-element.155), channel_id=1, source_target_pairs={{0,66},{2,68},{4,70},{6,72},{8,74},{10,76},{12,78},{14,80},{16,82}... | collective-permute-start | bytes 147464 | tf_op jit(solution)/shard_map/ppermute | solution.py:346
  40.0 9.2 %collective-permute-start.5 = (f32[96,1024]{1,0:T(8,128)}, f32[96,1024]{1,0:T(8,128)S(1)}, u32[]{:S(2)}, u32[]{:S(2)}) collective-permute-start(f32[96,1024]{1,0:T(8,128)} %get-tuple-element.156), channel_id=1, source_target_pairs={{0,64},{2,66},{4,68},{6,70},{8,72},{10,74},{12,76},{14,78},{16,80}... | collective-permute-start | bytes 1179656 | tf_op jit(solution)/shard_map/ppermute | solution.py:346
  41.3 7.7 %collective-permute-start.6 = (f32[96,128]{1,0:T(8,128)S(1)}, f32[96,128]{1,0:T(8,128)S(1)}, u32[]{:S(2)}, u32[]{:S(2)}) collective-permute-start(f32[96,128]{1,0:T(8,128)S(1)} %get-tuple-element.157), channel_id=1, source_target_pairs={{0,66},{2,68},{4,70},{6,72},{8,74},{10,76},{12,78},{14,80},{16,82}... | collective-permute-start | bytes 147464 | tf_op jit(solution)/shard_map/ppermute | solution.py:346
  50.0 10.7 %collective-permute-start.7 = (f32[3,96,1024]{2,1,0:T(8,128)S(1)}, f32[3,96,1024]{2,1,0:T(8,128)S(1)}, u32[]{:S(2)}, u32[]{:S(2)}) collective-permute-start(f32[3,96,1024]{2,1,0:T(8,128)S(1)} %constant_dynamic-update-slice_fusion), channel_id=1, source_target_pairs={{0,1},{1,0},{2,3},{3,2},{4,5},{5,4},{6,7},{7,6},{8,9},{9,8},{10,11... | collective-permute-start | bytes 3538952 | tf_op jit(solution)/shard_map/ppermute | solution.py:438
  64.0 25.7 %all-to-all-start = ((f32[128,1,128]{2,1,0:T(1,128)}), f32[128,1,128]{2,1,0:T(1,128)S(1)}, u32[]{:S(2)}, u32[]{:S(2)}) async-start(f32[128,1,128]{2,1,0:T(1,128)} %bitcast.23), calls=%async_computation | async-start | bytes 131072 | tf_op jit(solution)/shard_map/all_to_all | solution.py:467

commit v11 on v10

--- a/solution.py
+++ b/solution.py
@@ -377,8 +377,6 @@
         [gain_now, gain_prev, gain_side, retain, live_mask, zero_row, zero_row, zero_row], axis=0
     )
     arrived = lax.ppermute(jnp.where(mine == 0, cotangent, lateral), "group", [(0, 1), (1, 0)])
-    early = jnp.where(mine == 0, lateral, arrived)
-    late = jnp.where(mine == 0, arrived, cotangent)
     steps_all = 2 * steps_dev
     source_ids = lax.broadcasted_iota(jnp.int32, (reach_dev + outlets, reach_dev), 0)
     confluence = jnp.zeros((reach_dev + outlets, reach_dev), jnp.float32)
@@ -397,30 +395,30 @@
     zero_flow = jnp.zeros((steps_all, reach_dev), jnp.float32)
 
     def forward_first(operands):
-        flow, outlet, unused = routed(coef, early, late)
+        flow, outlet, unused = routed(coef, lateral, arrived)
         return flow, outlet, flow, zero_flow, zero_flow
 
     def backward_first(operands):
-        adjoint, own, side = adjoined(coef, early, late, confluence_t=confluence_t)
+        adjoint, own, side = adjoined(coef, arrived, cotangent, confluence_t=confluence_t)
         return own, side, adjoint, zero_flow, zero_flow
 
     def forward_step(operands):
         upper, side = operands
-        flow, outlet, inflow = routed(coef, early, late, upper, side, confluence)
+        flow, outlet, inflow = routed(coef, lateral, arrived, upper, side, confluence)
         return flow, outlet, flow, inflow, zero_flow
 
     def forward_last(operands):
         flow, outlet, first, inflow, unused = forward_step(operands)
-        return flow, outlet, first, inflow, jnp.concatenate([early, late], axis=0)
+        return flow, outlet, first, inflow, jnp.concatenate([lateral, arrived], axis=0)
 
     def backward_step(operands):
         upper, side = operands
-        adjoint, own, side = adjoined(coef, early, late, upper, side, confluence_t)
+        adjoint, own, side = adjoined(coef, arrived, cotangent, upper, side, confluence_t)
         return own, side, adjoint, zero_flow, zero_flow
 
     def backward_last(operands):
         upper, side = operands
-        adjoint, unused, unused_side = adjoined(coef, early, late, upper, side)
+        adjoint, unused, unused_side = adjoined(coef, arrived, cotangent, upper, side)
         return zero_flow, side, adjoint, zero_flow, zero_flow
 
     message, outlet_message, *kept = lax.cond(mine == 0, forward_first, backward_first, None)

time: 91.2 us -> 96.6 us (1.059)
  local copies, waits for them, and re-layouts: 4.26 us -> 7.13 us
  other arithmetic: 10.3 us -> 12.4 us
  Pallas kernels: 8.22 us -> 9.74 us
    another operation x2, local copies, waits for them, and re-layouts: 0.06 us -> 1.97 us  [body(): jnp.stack([gain_now, gain_prev, gain_side, retain, live_mask, zero_row, z...]
    pallas_call x4, Pallas kernels: 8.22 us -> 9.74 us  [vmem_call(): pl.pallas_call(kernel, out_shape=[jax.ShapeDtypeStruct(shape, jnp.float32...]
    select_n x1 -> x0, other arithmetic: 1.06 us -> none  [body(): late = jnp.where(mine == 0, arrived, cotangent)]
  transfers between devices with their start and end apart: 9 -> 9, of which waited for: 7 -> 7; matrix products, arithmetic and copies ran while one was open for 11% -> 16% of each run, Pallas kernels for 0% -> 0%
where the time goes in v11:
time: 96.6 us; the launch traced here: 95.9 us
  starting transfers between devices  33.7 us (35%)
  waiting for transfers between devices  29.4 us (30%)
  other arithmetic  12.4 us (13%)
  Pallas kernels  9.74 us (10%)
  local copies, waits for them, and re-layouts  7.13 us (7%)
  matrix products  1.99 us (2%)
  between operations  1.55 us (2%)
    ppermute x6, waiting for transfers between devices, both_ways(): return lax.ppermute(value, ('level', 'basin', 'group'), pairs)  17.1 us
    all_to_all x1, starting transfers between devices, body(): lax.all_to_all(replicated, ('level', 'basin'), 0, 0, tiled=True)  14.9 us
    all_to_all x1, waiting for transfers between devices, body(): lax.all_to_all(replicated, ('level', 'basin'), 0, 0, tiled=True)  9.85 us
    pallas_call x4, Pallas kernels, vmem_call(): pl.pallas_call(kernel, out_shape=[jax.ShapeDtypeStruct(shape, jnp.float32...  9.74 us
    ppermute x1, starting transfers between devices, body(): other = lax.ppermute(kept, 'group', [(0, 1), (1, 0)])  7.9 us
    ppermute x6, starting transfers between devices, both_ways(): return lax.ppermute(value, ('level', 'basin', 'group'), pairs)  7.72 us
    convert_element_type x1, other arithmetic, body(): confluence = confluence.astype(jnp.bfloat16)  4.02 us
    ppermute x1, starting transfers between devices, body(): lax.ppermute(jnp.where(mine == 0, cotangent, lateral), 'group', [(0, 1),...  3.2 us
  transfers between devices with their start and end apart: 9, of which 7 were waited for; matrix products, arithmetic and copies ran while one was open for 16% of the time, Pallas kernels for 0%

profile of v11, /device:TPU:1, one launch (start us, length us, event | category | flops | bytes accessed | tf_op | source)
XLA Modules:
  0.0 95.9 jit_solution(5936893128606178890)
XLA Ops:
  0.7 1.6 %broadcast_select_fusion.1 = f32[48,1024]{1,0:T(8,128)} fusion(f32[48,1024]{1,0:T(8,128)} %param.17, f32[48,1024]{1,0:T(8,128)} %param.16, pred[]{:T(512)S(6)} %eq.57), kind=kLoop, calls=%fused_computation.36 | loop fusion | flops 49152 | bytes 589825 | tf_op jit(solution)/shard_map/jit(_where)/select_n | solution.py:379
  2.3 3.2 %collective-permute-start = (f32[48,1024]{1,0:T(8,128)}, f32[48,1024]{1,0:T(8,128)S(1)}, u32[]{:S(2)}, u32[]{:S(2)}) collective-permute-start(f32[48,1024]{1,0:T(8,128)} %broadcast_select_fusion.1), channel_id=1, source_target_pairs={{0,1},{1,0},{2,3},{3,2},{4,5},{5,4},{6,7},{7,6},{8,9},{9,8},{10,11... | collective-permute-start | bytes 589832 | tf_op jit(solution)/shard_map/ppermute | solution.py:379
  11.4 2.0 %add_convert_fusion.1 = bf16[1024,1152]{1,0:T(8,128)(2,1)S(1)} fusion(s32[1024]{0:T(1024)S(1)} %bitcast.57, s32[1024]{0:T(1024)S(1)} %bitcast.55, pred[1024]{0:T(1024)(128)(4,1)S(1)} %get-tuple-element.187, pred[1024]{0:T(1024)(128)(4,1)S(1)} %get-tuple-element.186), kind=kLoop, calls=%fused_computation.4 | loop fusion | flops 9437184 | bytes 2369536 | tf_op jit(solution)/shard_map/convert_element_type | solution.py:394
  15.3 1.4 %stack.34 = f32[8,1024]{1,0:T(8,128)} concatenate(f32[1,1024]{1,0:T(1,128)} %subtract_divide_fusion, f32[1,1024]{1,0:T(1,128)} %get-tuple-element.178, f32[1,1024]{1,0:T(1,128)} %get-tuple-element.188, f32[1,1024]{1,0:T(1,128)} %get-tuple-element.174, f32[1,1024]{1,0:T(1,128)} %compare_convert_fusion, f32[1,1024]{1,0:T(1,128)} %broadcast.137, f32[2,1024]{1,0:T(2,128)} %stack.33), dimensions={0} | concatenate | bytes 65536 | tf_op jit(solution)/shard_map/stack | solution.py:376
  16.7 2.5 %conditional.4 = ((f32[96,1024]{1,0:T(8,128)}, f32[96,128]{1,0:T(8,128)})) conditional(s32[]{:T(128)} %convert_element_type.41, (f32[8,1024]{1,0:T(8,128)}, f32[48,1024]{1,0:T(8,128)S(1)}, f32[48,1024]{1,0:T(8,128)S(1)}, bf16[1024,1152]{1,0:T(8,128)(2,1)S(1)}) %tuple.85, (f32[8,1024]{1,0:T(8,128)}, f32[48,1024]{1,0:T(8,128)S(1)}, ...), branch_computations={%region_0.1_spmd, %region_1.2_spmd} | conditional | flops 453967872 | bytes 3620888 | solution.py:424
  16.7 2.5 %branch_0_fun.4 = (f32[96,1024]{1,0:T(8,128)}, f32[96,1024]{1,0:T(8,128)}, f32[96,128]{1,0:T(8,128)}) custom-call(f32[8,1024]{1,0:T(8,128)} %get-tuple-element.87.refs_0_, f32[48,1024]{1,0:T(8,128)S(1)} %get-tuple-element.88.refs_1_, f32[48,1024]{1,0:T(8,128)S(1)} %get-tuple-element.89.refs_2_, bf16[1024,1152]{1,0:T(8,128)(2,1)S(1)} %get-tuple-element.90.refs_3_), custom_call_target="tpu_custom_call" | custom-call | flops 453967872 | bytes 3620864 | tf_op jit(solution)/shard_map/cond/branch_0_fun/pallas_call | solution.py:229
  19.2 1.3 %collective-permute-start.2 = (f32[96,128]{1,0:T(8,128)}, f32[96,128]{1,0:T(8,128)}, u32[]{:S(2)}, u32[]{:S(2)}) collective-permute-start(f32[96,128]{1,0:T(8,128)} %get-tuple-element.153), channel_id=1, source_target_pairs={{0,66},{2,68},{4,70},{6,72},{8,74},{10,76},{12,78},{14,80},{16,82}... | collective-permute-start | bytes 147464 | tf_op jit(solution)/shard_map/ppermute | solution.py:346
  20.5 1.3 %collective-permute-start.1 = (f32[96,1024]{1,0:T(8,128)}, f32[96,1024]{1,0:T(8,128)}, u32[]{:S(2)}, u32[]{:S(2)}) collective-permute-start(f32[96,1024]{1,0:T(8,128)} %get-tuple-element.152), channel_id=1, source_target_pairs={{0,64},{2,66},{4,68},{6,70},{8,72},{10,74},{12,76},{14,78},{16,80}... | collective-permute-start | bytes 1179656 | tf_op jit(solution)/shard_map/ppermute | solution.py:346
  21.8 4.0 %add_convert_fusion = bf16[1152,1024]{1,0:T(8,128)(2,1)} fusion(s32[1024]{0:T(1024)} %bitcast.58, s32[1024]{0:T(1024)S(1)} %bitcast.56, pred[1024]{0:T(1024)(128)(4,1)} %copy-done.8, pred[1024]{0:T(1024)(128)(4,1)} %copy-done.7), kind=kLoop, calls=%fused_computation.1 | loop fusion | flops 9437184 | bytes 2369536 | tf_op jit(solution)/shard_map/convert_element_type | solution.py:387
  25.8 3.6 %collective-permute-done.1 = f32[96,1024]{1,0:T(8,128)} collective-permute-done((f32[96,1024]{1,0:T(8,128)}, f32[96,1024]{1,0:T(8,128)}, u32[]{:S(2)}, u32[]{:S(2)}) %collective-permute-start.1) | collective-permute-done | bytes 393248 | tf_op jit(solution)/shard_map/ppermute | solution.py:346
  29.4 3.0 %conditional.5 = (f32[96,1024]{1,0:T(8,128)}, f32[96,128]{1,0:T(8,128)}) conditional(s32[]{:T(128)} %convert_element_type.41, (f32[8,1024]{1,0:T(8,128)}, f32[48,1024]{1,0:T(8,128)S(1)}, f32[48,1024]{1,0:T(8,128)S(1)}, f32[96,1024]{1,0:T(8,128)}, f32[96,128]{1,0:T(8,128)}, /*index=5*/bf16[1024,1152]{1,0:T(8,128)(2,1)S(1)}) %tuple.86, ...), branch_computations={%region_2.3_spmd, %region_3.4_spmd} | conditional | flops 453967872 | bytes 4063248 | solution.py:429
  29.4 3.0 %branch_0_fun.5 = (f32[96,1024]{1,0:T(8,128)}, f32[96,1024]{1,0:T(8,128)}, f32[96,128]{1,0:T(8,128)}) custom-call(f32[8,1024]{1,0:T(8,128)} %get-tuple-element.96.refs_0_, f32[48,1024]{1,0:T(8,128)S(1)} %get-tuple-element.97.refs_1_, f32[48,1024]{1,0:T(8,128)S(1)} %get-tuple-element.98.refs_2_, f32[96,1024]{1,0:T(8,128)} %get-tuple-element.99.refs_3_, ...), custom_call_target="tpu_custom_call" | custom-call | flops 453967872 | bytes 4063232 | tf_op jit(solution)/shard_map/cond/branch_0_fun/pallas_call | solution.py:229
  33.7 1.3 %collective-permute-start.4 = (f32[96,128]{1,0:T(8,128)}, f32[96,128]{1,0:T(8,128)}, u32[]{:S(2)}, u32[]{:S(2)}) collective-permute-start(f32[96,128]{1,0:T(8,128)} %get-tuple-element.155), channel_id=1, source_target_pairs={{0,66},{2,68},{4,70},{6,72},{8,74},{10,76},{12,78},{14,80},{16,82}... | collective-permute-start | bytes 147464 | tf_op jit(solution)/shard_map/ppermute | solution.py:346
  35.0 6.3 %collective-permute-done.4 = f32[96,128]{1,0:T(8,128)} collective-permute-done((f32[96,128]{1,0:T(8,128)}, f32[96,128]{1,0:T(8,128)}, u32[]{:S(2)}, u32[]{:S(2)}) %collective-permute-start.4) | collective-permute-done | bytes 49184 | tf_op jit(solution)/shard_map/ppermute | solution.py:346
  41.8 3.0 %conditional.6 = (f32[96,1024]{1,0:T(8,128)}, f32[96,128]{1,0:T(8,128)}) conditional(s32[]{:T(128)} %convert_element_type.41, (f32[8,1024]{1,0:T(8,128)}, f32[48,1024]{1,0:T(8,128)S(1)}, f32[48,1024]{1,0:T(8,128)S(1)}, f32[96,1024]{1,0:T(8,128)}, f32[96,128]{1,0:T(8,128)}, /*index=5*/bf16[1024,1152]{1,0:T(8,128)(2,1)S(1)}) %tuple.87, ...), branch_computations={%region_4.5_spmd, %region_5.6_spmd} | conditional | flops 453967872 | bytes 4063248 | solution.py:429
  41.8 3.0 %branch_0_fun.6 = (f32[96,1024]{1,0:T(8,128)}, f32[96,1024]{1,0:T(8,128)}, f32[96,128]{1,0:T(8,128)}) custom-call(f32[8,1024]{1,0:T(8,128)} %get-tuple-element.112.refs_0_, f32[48,1024]{1,0:T(8,128)S(1)} %get-tuple-element.113.refs_1_, f32[48,1024]{1,0:T(8,128)S(1)} %get-tuple-element.114.refs_2_, f32[96,1024]{1,0:T(8,128)} %get-tuple-element.115.refs_3_, ...), custom_call_target="tpu_custom_call" | custom-call | flops 453967872 | bytes 4063232 | tf_op jit(solution)/shard_map/cond/branch_0_fun/pallas_call | solution.py:229
  46.0 1.3 %collective-permute-start.6 = (f32[96,128]{1,0:T(8,128)}, f32[96,128]{1,0:T(8,128)S(1)}, u32[]{:S(2)}, u32[]{:S(2)}) collective-permute-start(f32[96,128]{1,0:T(8,128)} %get-tuple-element.157), channel_id=1, source_target_pairs={{0,66},{2,68},{4,70},{6,72},{8,74},{10,76},{12,78},{14,80},{16,82}... | collective-permute-start | bytes 147464 | tf_op jit(solution)/shard_map/ppermute | solution.py:346
  47.3 6.5 %collective-permute-done.6 = f32[96,128]{1,0:T(8,128)S(1)} collective-permute-done((f32[96,128]{1,0:T(8,128)}, f32[96,128]{1,0:T(8,128)S(1)}, u32[]{:S(2)}, u32[]{:S(2)}) %collective-permute-start.6) | collective-permute-done | bytes 49184 | tf_op jit(solution)/shard_map/ppermute | solution.py:346
  54.0 1.4 %conditional.7 = (f32[1,96,1024]{2,1,0:T(8,128)S(1)}, f32[1,96,1024]{2,1,0:T(8,128)S(1)}, f32[1,96,1024]{2,1,0:T(8,128)S(1)}) conditional(s32[]{:T(128)} %convert_element_type.41, (f32[8,1024]{1,0:T(8,128)}, f32[48,1024]{1,0:T(8,128)S(1)}, f32[48,1024]{1,0:T(8,128)S(1)}, f32[96,1024]{1,0:T(8,128)S(1)}, f32[96,128]{1,0:T(8,128)S(1)}) %tuple.88, ...), branch_computations={%region_6.7_spmd, %region_7.8_spmd} | conditional | flops 454066176 | bytes 4849688 | solution.py:429
  54.0 1.3 %branch_0_fun.7 = f32[96,1024]{1,0:T(8,128)S(1)} custom-call(f32[8,1024]{1,0:T(8,128)} %get-tuple-element.128.refs_0_, f32[48,1024]{1,0:T(8,128)S(1)} %get-tuple-element.129.refs_1_, f32[48,1024]{1,0:T(8,128)S(1)} %get-tuple-element.130.refs_2_, f32[96,1024]{1,0:T(8,128)S(1)} %get-tuple-element.131.refs_3_, f32[96,128]{1,0:T(8,128)S(1)} %get-tuple-element.132.refs_4_), custom_call_target="tpu_custom_call" | custom-call | flops 453967872 | bytes 1261568 | tf_op jit(solution)/shard_map/cond/branch_0_fun/pallas_call | solution.py:229
  55.5 7.9 %collective-permute-start.7 = (f32[3,96,1024]{2,1,0:T(8,128)S(1)}, f32[3,96,1024]{2,1,0:T(8,128)S(1)}, u32[]{:S(2)}, u32[]{:S(2)}) collective-permute-start(f32[3,96,1024]{2,1,0:T(8,128)S(1)} %constant_dynamic-update-slice_fusion), channel_id=1, source_target_pairs={{0,1},{1,0},{2,3},{3,2},{4,5},{5,4},{6,7},{7,6},{8,9},{9,8},{10,11... | collective-permute-start | bytes 3538952 | tf_op jit(solution)/shard_map/ppermute | solution.py:436
  63.4 2.5 %collective-permute-done.7 = f32[3,96,1024]{2,1,0:T(8,128)S(1)} collective-permute-done((f32[3,96,1024]{2,1,0:T(8,128)S(1)}, f32[3,96,1024]{2,1,0:T(8,128)S(1)}, u32[]{:S(2)}, u32[]{:S(2)}) %collective-permute-start.7) | collective-permute-done | bytes 1179680 | tf_op jit(solution)/shard_map/ppermute | solution.py:436
  69.4 14.9 %all-to-all-start = ((f32[128,1,128]{2,1,0:T(1,128)}), f32[128,1,128]{2,1,0:T(1,128)S(1)}, u32[]{:S(2)}, u32[]{:S(2)}) async-start(f32[128,1,128]{2,1,0:T(1,128)} %bitcast.23), calls=%async_computation | async-start | bytes 131072 | tf_op jit(solution)/shard_map/all_to_all | solution.py:465
  85.1 9.8 %all-to-all-done = f32[128,1,128]{2,1,0:T(1,128)S(1)} async-done(((f32[128,1,128]{2,1,0:T(1,128)}), f32[128,1,128]{2,1,0:T(1,128)S(1)}, u32[]{:S(2)}, u32[]{:S(2)}) %all-to-all-start) | async-done | bytes 65568 | tf_op jit(solution)/shard_map/all_to_all | solution.py:465
  (54 shorter events, 15.6 us)
Async XLA Ops:
  0.6 8.4 %copy-start = (f32[16,1024]{1,0:T(8,128)S(1)}, f32[16,1024]{1,0:T(8,128)}, u32[]{:S(2)}) copy-start(f32[16,1024]{1,0:T(8,128)} %param.18) | copy-start | bytes 196612
  0.6 8.4 %copy-start.6 = (f32[128,16,2]{0,2,1:T(2,128)S(1)}, f32[128,16,2]{0,2,1:T(2,128)}, u32[]{:S(2)}) copy-start(f32[128,16,2]{0,2,1:T(2,128)} %param.23) | copy-start | bytes 49156
  2.3 14.4 %collective-permute-start = (f32[48,1024]{1,0:T(8,128)}, f32[48,1024]{1,0:T(8,128)S(1)}, u32[]{:S(2)}, u32[]{:S(2)}) collective-permute-start(f32[48,1024]{1,0:T(8,128)} %broadcast_select_fusion.1), channel_id=1, source_target_pairs={{0,1},{1,0},{2,3},{3,2},{4,5},{5,4},{6,7},{7,6},{8,9},{9,8},{10,11... | collective-permute-start | bytes 589832 | tf_op jit(solution)/shard_map/ppermute | solution.py:379
  6.9 6.6 %copy-start.7 = (pred[1024]{0:T(1024)(128)(4,1)}, pred[1024]{0:T(1024)(128)(4,1)S(1)}, u32[]{:S(2)}) copy-start(pred[1024]{0:T(1024)(128)(4,1)S(1)} %get-tuple-element.186) | copy-start | bytes 3076
  6.9 6.6 %copy-start.8 = (pred[1024]{0:T(1024)(128)(4,1)}, pred[1024]{0:T(1024)(128)(4,1)S(1)}, u32[]{:S(2)}) copy-start(pred[1024]{0:T(1024)(128)(4,1)S(1)} %get-tuple-element.187) | copy-start | bytes 3076
  8.2 5.2 %copy-start.3 = (s32[1,1024]{1,0:T(1,128)}, s32[1,1024]{1,0:T(1,128)S(1)}, u32[]{:S(2)}) copy-start(s32[1,1024]{1,0:T(1,128)S(1)} %get-tuple-element.183) | copy-start | bytes 12292
  11.4 2.1 %copy-start.4 = (f32[1,1024]{1,0:T(1,128)}, f32[1,1024]{1,0:T(1,128)S(1)}, u32[]{:S(2)}) copy-start(f32[1,1024]{1,0:T(1,128)S(1)} %get-tuple-element.179) | copy-start | bytes 12292
  11.4 5.3 %copy-start.1 = (f32[48,1024]{1,0:T(8,128)S(1)}, f32[48,1024]{1,0:T(8,128)}, u32[]{:S(2)}) copy-start(f32[48,1024]{1,0:T(8,128)} %param.16) | copy-start | bytes 589828
  11.4 5.3 %copy-start.2 = (f32[48,1024]{1,0:T(8,128)S(1)}, f32[48,1024]{1,0:T(8,128)}, u32[]{:S(2)}) copy-start(f32[48,1024]{1,0:T(8,128)} %param.17) | copy-start | bytes 589828
  19.2 6.6 %collective-permute-start.2 = (f32[96,128]{1,0:T(8,128)}, f32[96,128]{1,0:T(8,128)}, u32[]{:S(2)}, u32[]{:S(2)}) collective-permute-start(f32[96,128]{1,0:T(8,128)} %get-tuple-element.153), channel_id=1, source_target_pairs={{0,66},{2,68},{4,70},{6,72},{8,74},{10,76},{12,78},{14,80},{16,82}... | collective-permute-start | bytes 147464 | tf_op jit(solution)/shard_map/ppermute | solution.py:346
  20.5 9.0 %collective-permute-start.1 = (f32[96,1024]{1,0:T(8,128)}, f32[96,1024]{1,0:T(8,128)}, u32[]{:S(2)}, u32[]{:S(2)}) collective-permute-start(f32[96,1024]{1,0:T(8,128)} %get-tuple-element.152), channel_id=1, source_target_pairs={{0,64},{2,66},{4,68},{6,70},{8,72},{10,74},{12,76},{14,78},{16,80}... | collective-permute-start | bytes 1179656 | tf_op jit(solution)/shard_map/ppermute | solution.py:346
  32.4 9.4 %collective-permute-start.3 = (f32[96,1024]{1,0:T(8,128)}, f32[96,1024]{1,0:T(8,128)}, u32[]{:S(2)}, u32[]{:S(2)}) collective-permute-start(f32[96,1024]{1,0:T(8,128)} %get-tuple-element.154), channel_id=1, source_target_pairs={{0,64},{2,66},{4,68},{6,70},{8,72},{10,74},{12,76},{14,78},{16,80}... | collective-permute-start | bytes 1179656 | tf_op jit(solution)/shard_map/ppermute | solution.py:346
  33.7 7.6 %collective-permute-start.4 = (f32[96,128]{1,0:T(8,128)}, f32[96,128]{1,0:T(8,128)}, u32[]{:S(2)}, u32[]{:S(2)}) collective-permute-start(f32[96,128]{1,0:T(8,128)} %get-tuple-element.155), channel_id=1, source_target_pairs={{0,66},{2,68},{4,70},{6,72},{8,74},{10,76},{12,78},{14,80},{16,82}... | collective-permute-start | bytes 147464 | tf_op jit(solution)/shard_map/ppermute | solution.py:346
  44.7 9.2 %collective-permute-start.5 = (f32[96,1024]{1,0:T(8,128)}, f32[96,1024]{1,0:T(8,128)S(1)}, u32[]{:S(2)}, u32[]{:S(2)}) collective-permute-start(f32[96,1024]{1,0:T(8,128)} %get-tuple-element.156), channel_id=1, source_target_pairs={{0,64},{2,66},{4,68},{6,70},{8,72},{10,74},{12,76},{14,78},{16,80}... | collective-permute-start | bytes 1179656 | tf_op jit(solution)/shard_map/ppermute | solution.py:346
  46.0 7.8 %collective-permute-start.6 = (f32[96,128]{1,0:T(8,128)}, f32[96,128]{1,0:T(8,128)S(1)}, u32[]{:S(2)}, u32[]{:S(2)}) collective-permute-start(f32[96,128]{1,0:T(8,128)} %get-tuple-element.157), channel_id=1, source_target_pairs={{0,66},{2,68},{4,70},{6,72},{8,74},{10,76},{12,78},{14,80},{16,82}... | collective-permute-start | bytes 147464 | tf_op jit(solution)/shard_map/ppermute | solution.py:346
  55.5 10.4 %collective-permute-start.7 = (f32[3,96,1024]{2,1,0:T(8,128)S(1)}, f32[3,96,1024]{2,1,0:T(8,128)S(1)}, u32[]{:S(2)}, u32[]{:S(2)}) collective-permute-start(f32[3,96,1024]{2,1,0:T(8,128)S(1)} %constant_dynamic-update-slice_fusion), channel_id=1, source_target_pairs={{0,1},{1,0},{2,3},{3,2},{4,5},{5,4},{6,7},{7,6},{8,9},{9,8},{10,11... | collective-permute-start | bytes 3538952 | tf_op jit(solution)/shard_map/ppermute | solution.py:436
  66.1 0.7 copy-start.5
  69.4 25.5 %all-to-all-start = ((f32[128,1,128]{2,1,0:T(1,128)}), f32[128,1,128]{2,1,0:T(1,128)S(1)}, u32[]{:S(2)}, u32[]{:S(2)}) async-start(f32[128,1,128]{2,1,0:T(1,128)} %bitcast.23), calls=%async_computation | async-start | bytes 131072 | tf_op jit(solution)/shard_map/all_to_all | solution.py:465
